TPU v7x, 256 devices: a whole 4x4x8 slice. The times are simulated.
256 devices in a mesh: row: 32 (over y, x, core), col: 8 (over z).
Axes of the slice: x: 4, y: 4, z: 8, core: 2. Of those that a mesh axis runs over, the one named last changes fastest.
Arguments:
- start_block: float32 [8192, 256], P(('col', 'row')), may hold values from -6 to 6
- tile_values: float32 [32, 8, 2, 256, 256], P('row', 'col'), may hold values from -0.0625 to 0.0625
- tile_rows: int32 [32, 8, 2], P('row', 'col'), may hold values from 0 to 0, as said below
- tile_cols: int32 [32, 8, 2], P('row', 'col'), may hold values from 0 to 3
- tile_count: int32 [32, 8], P('row', 'col'), may hold values from 1 to 2, as said below
Outputs:
- image_block: float32 [8192, 256], P('row')
- new_basis: float32 [8192, 256], P(('col', 'row'))
- factor: float32 [256, 256], replicated
Inputs may be any that keep to these rules, and one draw needn't show every extreme that they name: On each device the slots name distinct positions (tile_rows, tile_cols) of its 1 x 4 grid of blocks, slots at or beyond tile_count included. `tile_count`: some devices hold exactly 2 live tiles.
All inputs are finite; a program needn't handle non-finite values.
Results may differ from a plain program's by a relative error of at most 0.0001.
Values sent between devices are 32-bit elements; how exact they have to be, the bound alone decides.
No kernel may reach another device: no remote copies, remote signals or barrier semaphores. Data moves between devices by JAX's collectives and lax.ppermute only.
A program may use at most 64 MiB of HBM per device.

v0:
```python
import jax
import jax.numpy as jnp
from jax import lax
from jax.sharding import PartitionSpec as P

BR = 1


def cholesky_lower(gram):
    size = gram.shape[0]
    index = jnp.arange(size, dtype=jnp.int32)

    def column_step(j, lower):
        known = lower * (index[None, :] < j).astype(gram.dtype)
        row_j = lax.dynamic_slice_in_dim(known, j, 1, 0)[0]
        column = lax.dynamic_slice_in_dim(gram, j, 1, 1)[:, 0] - jnp.dot(
            known, row_j, precision=lax.Precision.HIGHEST
        )
        pivot = jnp.sqrt(lax.dynamic_slice_in_dim(column, j, 1, 0)[0])
        column = jnp.where(index >= j, column / pivot, jnp.zeros_like(column))
        return lax.dynamic_update_slice_in_dim(lower, column[:, None], j, 1)

    return lax.fori_loop(0, size, column_step, jnp.zeros_like(gram))


def lower_inverse(lower):
    size = lower.shape[0]
    index = jnp.arange(size, dtype=jnp.int32)

    def row_step(i, inverse):
        row_l = lax.dynamic_slice_in_dim(lower, i, 1, 0)[0]
        known = row_l * (index < i).astype(lower.dtype)
        unit = (index == i).astype(lower.dtype)
        pivot = lax.dynamic_slice_in_dim(row_l, i, 1, 0)[0]
        new_row = (unit - jnp.dot(known, inverse, precision=lax.Precision.HIGHEST)) / pivot
        return lax.dynamic_update_slice_in_dim(inverse, new_row[None, :], i, 0)

    return lax.fori_loop(0, size, row_step, jnp.zeros_like(lower))


def body(start_block, tile_values, tile_rows, tile_cols, tile_count):
    tile_size = tile_values.shape[-1]
    basis_width = start_block.shape[1]
    slot_total = tile_values.shape[2]
    slab = lax.all_gather(start_block, "row", axis=0, tiled=True)
    start_blocks = slab.reshape(-1, tile_size, basis_width)
    block_cols = start_blocks.shape[0]
    values = tile_values.reshape(slot_total, tile_size, tile_size)
    row_ids = tile_rows.reshape(slot_total)
    col_ids = tile_cols.reshape(slot_total)
    live_count = tile_count.reshape(())
    block_rows = BR
    live_mask = (jnp.arange(slot_total, dtype=jnp.int32) < live_count).astype(jnp.float32)
    row_onehot = (row_ids[:, None] == jnp.arange(block_rows, dtype=jnp.int32)[None, :]).astype(
        jnp.float32
    ) * live_mask[:, None]
    products = jnp.einsum(
        "tij,tjk->tik",
        values,
        start_blocks[col_ids],
        precision=lax.Precision.HIGHEST,
        preferred_element_type=jnp.float32,
    )
    partial_image = jnp.einsum(
        "tb,tik->bik",
        row_onehot,
        products,
        precision=lax.Precision.HIGHEST,
        preferred_element_type=jnp.float32,
    )
    partial_rows = partial_image.reshape(-1, basis_width)
    image_block = lax.psum(partial_rows, "col")
    image_blocks = image_block.reshape(block_rows, tile_size, basis_width)
    col_onehot = (col_ids[:, None] == jnp.arange(block_cols, dtype=jnp.int32)[None, :]).astype(
        jnp.float32
    ) * live_mask[:, None]
    back_products = jnp.einsum(
        "tji,tjk->tik",
        values,
        image_blocks[row_ids],
        precision=lax.Precision.HIGHEST,
        preferred_element_type=jnp.float32,
    )
    partial_projected = jnp.einsum(
        "tc,tik->cik",
        col_onehot,
        back_products,
        precision=lax.Precision.HIGHEST,
        preferred_element_type=jnp.float32,
    )
    partial_flat = partial_projected.reshape(-1, basis_width)
    projected = lax.psum_scatter(partial_flat, "row", scatter_dimension=0, tiled=True)
    share_rows = projected.shape[0]
    matrix_order = share_rows * lax.axis_size("row") * lax.axis_size("col")
    local_gram = jnp.dot(
        projected.T, projected, precision=lax.Precision.HIGHEST, preferred_element_type=jnp.float32
    )
    gram_matrix = lax.psum(local_gram, ("row", "col")) / matrix_order
    lower = cholesky_lower(gram_matrix)
    inverse = lower_inverse(lower)
    factor = lower.T
    new_basis = jnp.dot(
        projected, inverse.T, precision=lax.Precision.HIGHEST, preferred_element_type=jnp.float32
    )
    return (image_block, new_basis, factor)


def solution(mesh):
    placed = (
        P(("col", "row"), None),
        P("row", "col", None, None, None),
        P("row", "col", None),
        P("row", "col", None),
        P("row", "col"),
    )
    return jax.shard_map(
        body,
        mesh=mesh,
        in_specs=placed,
        out_specs=(P("row", None), P(("col", "row"), None), P()),
        check_vma=False,
    )
```

profile of v0, /device:TPU:1, one launch (start us, length us, event | category | flops | bytes accessed | tf_op | source)
XLA Modules:
  0.0 1525.3 jit_solution(4812023314239359038)
XLA Ops:
  7.2 0.7 all-gather.2.cloned.1.call-update
  8.7 54.0 %all-gather.2.cloned.1.call-done = f32[1024,256]{1,0:T(8,128)} async-done(((f32[32,256]{1,0:T(8,128)}), f32[1024,256]{1,0:T(8,128)}) %all-gather.2.cloned.1.call-update) | async-done | bytes 1048592 | tf_op jit(solution)/shard_map/all_gather | solution.py:45
  62.6 1.8 gather_fusion
  64.4 1.0 convolution_bitcast_fusion.1
  66.4 1.8 fusion.22
  68.2 0.7 copy.30
  69.0 67.0 %all-reduce.3.cloned.1.call-done = f32[256,256]{1,0:T(8,128)} async-done(((f32[256,256]{1,0:T(8,128)}), f32[256,256]{1,0:T(8,128)}) %all-reduce.3.cloned.1.call-update) | async-done | bytes 262160 | tf_op jit(solution)/shard_map/psum | solution.py:72
  136.0 1.1 copy.21
  138.0 2.3 fusion.14
  140.3 1.2 copy.23
  141.5 86.6 %reduce-scatter.2.cloned.1.call-done = f32[32,256]{1,0:T(8,128)} async-done(((f32[1024,256]{1,0:T(8,128)}), f32[32,256]{1,0:T(8,128)}) %reduce-scatter.2.cloned.1.call-update) | async-done | bytes 32784 | tf_op jit(solution)/shard_map/reduce_scatter | solution.py:92
  228.1 1.9 fusion.30
  230.1 253.9 %all-reduce.5.cloned.1.call-done = f32[256,256]{1,0:T(8,128)} async-done(((f32[256,256]{1,0:T(8,128)}), f32[256,256]{1,0:T(8,128)}) %all-reduce.5.cloned.1.call-update) | async-done | bytes 262160 | tf_op jit(solution)/shard_map/psum | solution.py:98
  483.9 1.0 broadcast_multiply_fusion.1
  485.1 631.3 %while.33 = (s32[]{:T(128)}, f32[256,256]{1,0:T(8,128)S(1)}, f32[256,256]{0,1:T(8,128)S(1)}, s32[]{:T(128)}, s32[]{:T(128)}) while((s32[]{:T(128)}, f32[256,256]{1,0:T(8,128)S(1)}, f32[256,256]{0,1:T(8,128)S(1)}, s32[]{:T(128)}, s32[]{:T(128)}) %tuple.82), condition=%wide.region_4.5_spmd.clone.clone, body=%wide.region_3.4_spmd.clone.clone.sunk | while | flops 853506 | bytes 801897 | solution.py:23
  1116.3 0.8 copy.25
  1117.2 399.9 %while.34 = (s32[]{:T(128)}, f32[256,256]{1,0:T(8,128)S(1)}, f32[256,256]{1,0:T(8,128)S(1)}, s32[]{:T(128)}, s32[]{:T(128)}, /*index=5*/s32[]{:T(128)}) while((s32[]{:T(128)}, f32[256,256]{1,0:T(8,128)S(1)}, f32[256,256]{1,0:T(8,128)S(1)}, s32[]{:T(128)}, s32[]{:T(128)}, /*index=5*/s32[]{:T(128)}) %tuple.85), condition=%wide.region_6.7_spmd.clone.clone, body=%wide.region_5.6_spmd.clone.clone.sunk | while | flops 787971 | bytes 272501 | solution.py:38
  1119.6 0.6 fusion.55
  1121.2 0.6 fusion.55
  1125.9 0.6 fusion.55
  1127.4 0.6 fusion.55
  1132.1 0.6 fusion.55
  1138.4 0.6 fusion.55
  1144.6 0.6 fusion.55
  1149.3 0.6 fusion.55
  1150.9 0.6 fusion.55
  1155.6 0.6 fusion.55
  1157.1 0.6 fusion.55
  1161.8 0.6 fusion.55
  1168.1 0.6 fusion.55
  1517.1 1.0 fusion.31
  1518.1 0.7 copy.50
  (3853 shorter events, 818.4 us)
Async XLA Ops:
  7.2 57.3 %copy-start = (f32[1,1,2,256,256]{4,3,2,1,0:T(8,128)S(1)}, f32[1,1,2,256,256]{4,3,2,1,0:T(8,128)}, u32[]{:S(2)}) copy-start(f32[1,1,2,256,256]{4,3,2,1,0:T(8,128)} %param.10) | copy-start | bytes 1572868
  7.2 55.4 %all-gather.2.cloned.1.call-start = ((), (), s32[]{:S(2)}) async-start(), calls=%async_computation.1 | async-start | bytes 1081344 | tf_op jit(solution)/shard_map/all_gather | solution.py:45
  7.9 0.7 copy-start.3
  7.9 128.1 %all-reduce.3.cloned.1.call-start = ((), (), s32[]{:S(2)}) async-start(), calls=%async_computation.2 | async-start | bytes 524288 | tf_op jit(solution)/shard_map/psum | solution.py:72
  65.7 0.7 copy-start.4
  69.0 159.1 %reduce-scatter.2.cloned.1.call-start = ((), (), s32[]{:S(2)}) async-start(), calls=%async_computation.3 | async-start | bytes 1081344 | tf_op jit(solution)/shard_map/reduce_scatter | solution.py:92
  141.5 342.5 %all-reduce.5.cloned.1.call-start = ((), (), s32[]{:S(2)}) async-start(), calls=%async_computation.4 | async-start | bytes 524288 | tf_op jit(solution)/shard_map/psum | solution.py:98
  1117.2 399.9 %copy-start.2 = (f32[32,256]{1,0:T(8,128)S(1)}, f32[32,256]{1,0:T(8,128)}, u32[]{:S(2)}) copy-start(f32[32,256]{1,0:T(8,128)} %reduce-scatter.2.cloned.1.call-done) | copy-start | bytes 98308
  1517.1 1.0 copy-start.1
Sparse Core Ops, SparseCore 0:
  10.6 52.0 all-gather.1
  69.1 66.8 all-reduce.2
  141.6 86.4 reduce-scatter.1
  234.0 249.9 all-reduce.4
where the time goes:
time: 1530 us
  local copies, waits for them, and re-layouts  539 us (35%)
  waiting for transfers between devices  462 us (30%)
  loops' own time  206 us (13%)
  other arithmetic  177 us (12%)
  matrix products  126 us (8%)
    psum x1, waiting for transfers between devices, body(): gram_matrix = lax.psum(local_gram, ('row', 'col')) / matrix_order  254 us
    another operation x1, loops' own time, cholesky_lower(): return lax.fori_loop(0, size, column_step, jnp.zeros_like(gram))  195 us
    div x256, other arithmetic, row_step(): (unit - jnp.dot(known, inverse, precision=lax.Precision.HIGHEST)) / pivot  166 us
    dynamic_slice x256, local copies, waits for them, and re-layouts, row_step(): pivot = lax.dynamic_slice_in_dim(row_l, i, 1, 0)[0]  161 us
    dynamic_update_slice x256, local copies, waits for them, and re-layouts, column_step(): return lax.dynamic_update_slice_in_dim(lower, column[:, None], j, 1)  157 us
    dynamic_slice x256, local copies, waits for them, and re-layouts, column_step(): pivot = jnp.sqrt(lax.dynamic_slice_in_dim(column, j, 1, 0)[0])  151 us
    reduce_scatter x1, waiting for transfers between devices, body(): lax.psum_scatter(partial_flat, 'row', scatter_dimension=0, tiled=True)  86.6 us
    dot_general x256, matrix products, column_step(): jnp.dot(known, row_j, precision=lax.Precision.HIGHEST)  69.8 us
  transfers between devices with their start and end apart: 4, of which 4 were waited for; matrix products, arithmetic and copies ran while one was open for 0% of the time, Pallas kernels for 0%

commit v1 on v0

--- a/solution.py
+++ b/solution.py
@@ -1,41 +1,62 @@
 import jax
 import jax.numpy as jnp
 from jax import lax
+from jax.experimental import pallas as pl
+from jax.experimental.pallas import tpu as pltpu
 from jax.sharding import PartitionSpec as P
 
 BR = 1
 
 
-def cholesky_lower(gram):
-    size = gram.shape[0]
-    index = jnp.arange(size, dtype=jnp.int32)
+def chol_inv_kernel(g_ref, u_ref, w_ref, a_ref):
+    n = g_ref.shape[0]
+    a_ref[...] = g_ref[...]
+    rr = lax.broadcasted_iota(jnp.int32, (n, n), 0)
+    cc = lax.broadcasted_iota(jnp.int32, (n, n), 1)
+    w_ref[...] = jnp.where(rr == cc, 1.0, 0.0).astype(jnp.float32)
+    lane = lax.broadcasted_iota(jnp.int32, (1, n), 1)
+    sub = lax.broadcasted_iota(jnp.int32, (n, 1), 0)
+    lane128 = lax.broadcasted_iota(jnp.int32, (n, 128), 1)
 
-    def column_step(j, lower):
-        known = lower * (index[None, :] < j).astype(gram.dtype)
-        row_j = lax.dynamic_slice_in_dim(known, j, 1, 0)[0]
-        column = lax.dynamic_slice_in_dim(gram, j, 1, 1)[:, 0] - jnp.dot(
-            known, row_j, precision=lax.Precision.HIGHEST
-        )
-        pivot = jnp.sqrt(lax.dynamic_slice_in_dim(column, j, 1, 0)[0])
-        column = jnp.where(index >= j, column / pivot, jnp.zeros_like(column))
-        return lax.dynamic_update_slice_in_dim(lower, column[:, None], j, 1)
+    def step(j, carry):
+        row = a_ref[pl.ds(j, 1), :]
+        ajj = jnp.sum(jnp.where(lane == j, row, 0.0), axis=1, keepdims=True)
+        piv = jnp.sqrt(ajj)
+        lrow = jnp.where(lane >= j, row / piv, 0.0)
+        base = pl.multiple_of((j // 128) * 128, 128)
+        blk = a_ref[:, pl.ds(base, 128)]
+        cola = jnp.sum(jnp.where(lane128 == j - base, blk, 0.0), axis=1, keepdims=True)
+        lcol = jnp.where(sub >= j, cola / piv, 0.0)
+        a_ref[...] = a_ref[...] - lcol * lrow
+        u_ref[pl.ds(j, 1), :] = lrow
+        wrow = w_ref[pl.ds(j, 1), :] / piv
+        w_ref[...] = w_ref[...] - jnp.where(sub > j, lcol, 0.0) * wrow
+        w_ref[pl.ds(j, 1), :] = wrow
+        return carry
 
-    return lax.fori_loop(0, size, column_step, jnp.zeros_like(gram))
+    lax.fori_loop(0, n, step, 0)
+
+def chol_inv(g):
+    n = g.shape[0]
+    r = lax.broadcasted_iota(jnp.int32, (n, n), 0)
+    c = lax.broadcasted_iota(jnp.int32, (n, n), 1)
+    g = jnp.where(r >= c, g, g.T)
+    return pl.pallas_call(
+        chol_inv_kernel,
+        out_shape=(jax.ShapeDtypeStruct((n, n), jnp.float32), jax.ShapeDtypeStruct((n, n), jnp.float32)),
+        in_specs=[pl.BlockSpec(memory_space=pltpu.VMEM)],
+        out_specs=(pl.BlockSpec(memory_space=pltpu.VMEM), pl.BlockSpec(memory_space=pltpu.VMEM)),
+        scratch_shapes=[pltpu.VMEM((n, n), jnp.float32)],
+    )(g)
 
 
-def lower_inverse(lower):
-    size = lower.shape[0]
-    index = jnp.arange(size, dtype=jnp.int32)
-
-    def row_step(i, inverse):
-        row_l = lax.dynamic_slice_in_dim(lower, i, 1, 0)[0]
-        known = row_l * (index < i).astype(lower.dtype)
-        unit = (index == i).astype(lower.dtype)
-        pivot = lax.dynamic_slice_in_dim(row_l, i, 1, 0)[0]
-        new_row = (unit - jnp.dot(known, inverse, precision=lax.Precision.HIGHEST)) / pivot
-        return lax.dynamic_update_slice_in_dim(inverse, new_row[None, :], i, 0)
-
-    return lax.fori_loop(0, size, row_step, jnp.zeros_like(lower))
+def butterfly_sum(x, axis):
+    size = lax.axis_size(axis)
+    step = 1
+    while step < size:
+        x = x + lax.ppermute(x, axis, [(i, i ^ step) for i in range(size)])
+        step *= 2
+    return x
 
 
 def body(start_block, tile_values, tile_rows, tile_cols, tile_count):
@@ -69,7 +90,7 @@
         preferred_element_type=jnp.float32,
     )
     partial_rows = partial_image.reshape(-1, basis_width)
-    image_block = lax.psum(partial_rows, "col")
+    image_block = butterfly_sum(partial_rows, "col")
     image_blocks = image_block.reshape(block_rows, tile_size, basis_width)
     col_onehot = (col_ids[:, None] == jnp.arange(block_cols, dtype=jnp.int32)[None, :]).astype(
         jnp.float32
@@ -95,12 +116,14 @@
     local_gram = jnp.dot(
         projected.T, projected, precision=lax.Precision.HIGHEST, preferred_element_type=jnp.float32
     )
-    gram_matrix = lax.psum(local_gram, ("row", "col")) / matrix_order
-    lower = cholesky_lower(gram_matrix)
-    inverse = lower_inverse(lower)
-    factor = lower.T
-    new_basis = jnp.dot(
-        projected, inverse.T, precision=lax.Precision.HIGHEST, preferred_element_type=jnp.float32
+    gram_matrix = butterfly_sum(butterfly_sum(local_gram, "row"), "col") / matrix_order
+    factor, inverse = chol_inv(gram_matrix)
+    new_basis = lax.dot_general(
+        projected,
+        inverse,
+        (((1,), (1,)), ((), ())),
+        precision=lax.Precision.HIGHEST,
+        preferred_element_type=jnp.float32,
     )
     return (image_block, new_basis, factor)
 

time: 1530 us -> 319 us (0.21)
  the two profiles are of different devices: /device:TPU:1 before, /device:TPU:6 now
where the time goes in v1:
time: 319 us
  waiting for transfers between devices  223 us (70%)
  Pallas kernels  41.9 us (13%)
  starting transfers between devices  23.9 us (7%)
  between operations  14.9 us (5%)
  matrix products  9.37 us (3%)
  local copies, waits for them, and re-layouts  4.27 us (1%)
    ppermute x11, waiting for transfers between devices, butterfly_sum(): x = x + lax.ppermute(x, axis, [(i, i ^ step) for i in range(size)])  88.3 us
    reduce_scatter x1, waiting for transfers between devices, body(): lax.psum_scatter(partial_flat, 'row', scatter_dimension=0, tiled=True)  81.8 us
    all_gather x1, waiting for transfers between devices, body(): slab = lax.all_gather(start_block, 'row', axis=0, tiled=True)  52.3 us
    pallas_call x1, Pallas kernels, chol_inv(): pl.pallas_call(chol_inv_kernel, out_shape=(jax.ShapeDtypeStruct((n, n), j...  41.9 us
    ppermute x11, starting transfers between devices, butterfly_sum(): x = x + lax.ppermute(x, axis, [(i, i ^ step) for i in range(size)])  23.8 us
  transfers between devices with their start and end apart: 13, of which 13 were waited for; matrix products, arithmetic and copies ran while one was open for 0% of the time, Pallas kernels for 0%

profile of v1, /device:TPU:6, one launch (start us, length us, event | category | flops | bytes accessed | tf_op | source)
XLA Modules:
  0.0 318.6 jit_solution(14636938917668390016)
XLA Ops:
  8.7 52.3 %all-gather.2.cloned.1.call-done = f32[1024,256]{1,0:T(8,128)} async-done(((f32[32,256]{1,0:T(8,128)}), f32[1024,256]{1,0:T(8,128)}) %all-gather.2.cloned.1.call-update) | async-done | bytes 1048592 | tf_op jit(solution)/shard_map/all_gather | solution.py:66
  61.0 1.8 gather_fusion
  62.8 1.0 convolution_bitcast_fusion
  64.7 1.8 fusion.14
  66.6 1.6 collective-permute-start
  68.2 6.9 %collective-permute-done = f32[256,256]{1,0:T(8,128)S(1)} collective-permute-done((f32[256,256]{1,0:T(8,128)S(1)}, f32[256,256]{1,0:T(8,128)S(1)}, u32[]{:S(2)}, u32[]{:S(2)}) %collective-permute-start) | collective-permute-done | bytes 262176 | tf_op jit(solution)/shard_map/ppermute | solution.py:57
  75.2 2.6 collective-permute-start.1
  77.8 11.6 %collective-permute-done.1 = f32[256,256]{1,0:T(8,128)S(1)} collective-permute-done((f32[256,256]{1,0:T(8,128)S(1)}, f32[256,256]{1,0:T(8,128)S(1)}, u32[]{:S(2)}, u32[]{:S(2)}) %collective-permute-start.1) | collective-permute-done | bytes 262176 | tf_op jit(solution)/shard_map/ppermute | solution.py:57
  89.5 5.8 %collective-permute-start.2 = (f32[256,256]{1,0:T(8,128)S(1)}, f32[256,256]{1,0:T(8,128)S(1)}, u32[]{:S(2)}, u32[]{:S(2)}) collective-permute-start(f32[256,256]{1,0:T(8,128)S(1)} %add.57), channel_id=1, source_target_pairs={{0,4},{1,5},{2,6},{3,7},{4,0},{5,1},{6,2},{7,3},{8,12},{9,13},{10,... | collective-permute-start | bytes 786440 | tf_op jit(solution)/shard_map/ppermute | solution.py:57
  95.3 12.1 %collective-permute-done.2 = f32[256,256]{1,0:T(8,128)S(1)} collective-permute-done((f32[256,256]{1,0:T(8,128)S(1)}, f32[256,256]{1,0:T(8,128)S(1)}, u32[]{:S(2)}, u32[]{:S(2)}) %collective-permute-start.2) | collective-permute-done | bytes 262176 | tf_op jit(solution)/shard_map/ppermute | solution.py:57
  107.4 1.0 fusion.2
  108.7 2.3 fusion
  111.1 1.2 copy.11
  112.3 81.8 %reduce-scatter.2.cloned.1.call-done = f32[32,256]{1,0:T(8,128)} async-done(((f32[1024,256]{1,0:T(8,128)}), f32[32,256]{1,0:T(8,128)}) %reduce-scatter.2.cloned.1.call-update) | async-done | bytes 32784 | tf_op jit(solution)/shard_map/reduce_scatter | solution.py:113
  194.1 1.2 fusion.22
  195.5 1.5 collective-permute-done.3
  197.0 0.9 collective-permute-start.4
  197.9 7.5 %collective-permute-done.4 = f32[256,256]{0,1:T(8,128)S(1)} collective-permute-done((f32[256,256]{0,1:T(8,128)S(1)}, f32[256,256]{0,1:T(8,128)S(1)}, u32[]{:S(2)}, u32[]{:S(2)}) %collective-permute-start.4) | collective-permute-done | bytes 262176 | tf_op jit(solution)/shard_map/ppermute | solution.py:57
  205.5 1.5 collective-permute-start.5
  207.0 7.6 %collective-permute-done.5 = f32[256,256]{0,1:T(8,128)S(1)} collective-permute-done((f32[256,256]{0,1:T(8,128)S(1)}, f32[256,256]{0,1:T(8,128)S(1)}, u32[]{:S(2)}, u32[]{:S(2)}) %collective-permute-start.5) | collective-permute-done | bytes 262176 | tf_op jit(solution)/shard_map/ppermute | solution.py:57
  215.0 6.4 %collective-permute-done.6 = f32[256,256]{0,1:T(8,128)S(1)} collective-permute-done((f32[256,256]{0,1:T(8,128)S(1)}, f32[256,256]{0,1:T(8,128)S(1)}, u32[]{:S(2)}, u32[]{:S(2)}) %collective-permute-start.6) | collective-permute-done | bytes 262176 | tf_op jit(solution)/shard_map/ppermute | solution.py:57
  221.4 1.4 collective-permute-start.7
  222.9 6.5 %collective-permute-done.7 = f32[256,256]{0,1:T(8,128)S(1)} collective-permute-done((f32[256,256]{0,1:T(8,128)S(1)}, f32[256,256]{0,1:T(8,128)S(1)}, u32[]{:S(2)}, u32[]{:S(2)}) %collective-permute-start.7) | collective-permute-done | bytes 262176 | tf_op jit(solution)/shard_map/ppermute | solution.py:57
  229.4 1.6 collective-permute-start.8
  231.0 7.0 %collective-permute-done.8 = f32[256,256]{0,1:T(8,128)S(1)} collective-permute-done((f32[256,256]{0,1:T(8,128)S(1)}, f32[256,256]{0,1:T(8,128)S(1)}, u32[]{:S(2)}, u32[]{:S(2)}) %collective-permute-start.8) | collective-permute-done | bytes 262176 | tf_op jit(solution)/shard_map/ppermute | solution.py:57
  238.1 2.7 collective-permute-start.9
  240.8 13.0 %collective-permute-done.9 = f32[256,256]{0,1:T(8,128)S(1)} collective-permute-done((f32[256,256]{0,1:T(8,128)S(1)}, f32[256,256]{0,1:T(8,128)S(1)}, u32[]{:S(2)}, u32[]{:S(2)}) %collective-permute-start.9) | collective-permute-done | bytes 262176 | tf_op jit(solution)/shard_map/ppermute | solution.py:57
  253.8 5.1 %collective-permute-start.10 = (f32[256,256]{0,1:T(8,128)S(1)}, f32[256,256]{0,1:T(8,128)S(1)}, u32[]{:S(2)}, u32[]{:S(2)}) collective-permute-start(f32[256,256]{0,1:T(8,128)S(1)} %add.66), channel_id=1, source_target_pairs={{0,4},{1,5},{2,6},{3,7},{4,0},{5,1},{6,2},{7,3},{8,12},{9,13},{10,... | collective-permute-start | bytes 786440 | tf_op jit(solution)/shard_map/ppermute | solution.py:57
  258.9 8.1 %collective-permute-done.10 = f32[256,256]{0,1:T(8,128)S(1)} collective-permute-done((f32[256,256]{0,1:T(8,128)S(1)}, f32[256,256]{0,1:T(8,128)S(1)}, u32[]{:S(2)}, u32[]{:S(2)}) %collective-permute-start.10) | collective-permute-done | bytes 262176 | tf_op jit(solution)/shard_map/ppermute | solution.py:57
  267.2 0.7 bitcast_select_fusion.g_ref
  267.9 41.9 %shard_map.76 = (f32[256,256]{1,0:T(8,128)}, f32[256,256]{1,0:T(8,128)}) custom-call(f32[256,256]{1,0:T(8,128)} %bitcast_select_fusion.g_ref), custom_call_target="tpu_custom_call" | custom-call | tf_op jit(solution)/shard_map/pallas_call | solution.py:44
  309.8 1.9 fusion.23
  (34 shorter events, 2.9 us)
Async XLA Ops:
  7.2 55.6 %copy-start = (f32[1,1,2,256,256]{4,3,2,1,0:T(8,128)S(1)}, f32[1,1,2,256,256]{4,3,2,1,0:T(8,128)}, u32[]{:S(2)}) copy-start(f32[1,1,2,256,256]{4,3,2,1,0:T(8,128)} %param.6) | copy-start | bytes 1572868
  7.2 53.8 %all-gather.2.cloned.1.call-start = ((), (), s32[]{:S(2)}) async-start(), calls=%async_computation.1 | async-start | bytes 1081344 | tf_op jit(solution)/shard_map/all_gather | solution.py:66
  7.9 0.7 copy-start.3
  7.9 186.2 %reduce-scatter.2.cloned.1.call-start = ((), (), s32[]{:S(2)}) async-start(), calls=%async_computation.2 | async-start | bytes 1081344 | tf_op jit(solution)/shard_map/reduce_scatter | solution.py:113
  64.1 0.7 copy-start.4
  66.6 8.6 %collective-permute-start = (f32[256,256]{1,0:T(8,128)S(1)}, f32[256,256]{1,0:T(8,128)S(1)}, u32[]{:S(2)}, u32[]{:S(2)}) collective-permute-start(f32[256,256]{1,0:T(8,128)S(1)} %bitcast.45), channel_id=1, source_target_pairs={{0,1},{1,0},{2,3},{3,2},{4,5},{5,4},{6,7},{7,6},{8,9},{9,8},{10,11... | collective-permute-start | bytes 786440 | tf_op jit(solution)/shard_map/ppermute | solution.py:57
  75.2 14.3 %collective-permute-start.1 = (f32[256,256]{1,0:T(8,128)S(1)}, f32[256,256]{1,0:T(8,128)S(1)}, u32[]{:S(2)}, u32[]{:S(2)}) collective-permute-start(f32[256,256]{1,0:T(8,128)S(1)} %fusion.21), channel_id=1, source_target_pairs={{0,2},{1,3},{2,0},{3,1},{4,6},{5,7},{6,4},{7,5},{8,10},{9,11},{10,... | collective-permute-start | bytes 786440 | tf_op jit(solution)/shard_map/ppermute | solution.py:57
  89.5 17.9 %collective-permute-start.2 = (f32[256,256]{1,0:T(8,128)S(1)}, f32[256,256]{1,0:T(8,128)S(1)}, u32[]{:S(2)}, u32[]{:S(2)}) collective-permute-start(f32[256,256]{1,0:T(8,128)S(1)} %add.57), channel_id=1, source_target_pairs={{0,4},{1,5},{2,6},{3,7},{4,0},{5,1},{6,2},{7,3},{8,12},{9,13},{10,... | collective-permute-start | bytes 786440 | tf_op jit(solution)/shard_map/ppermute | solution.py:57
  107.4 1.1 copy-start.1
  195.4 1.6 collective-permute-start.3
  197.0 8.4 %collective-permute-start.4 = (f32[256,256]{0,1:T(8,128)S(1)}, f32[256,256]{0,1:T(8,128)S(1)}, u32[]{:S(2)}, u32[]{:S(2)}) collective-permute-start(f32[256,256]{0,1:T(8,128)S(1)} %add.60), channel_id=1, source_target_pairs={{0,16},{8,24},{16,0},{24,8},{32,48},{40,56},{48,32},{56,40},{64,80... | collective-permute-start | bytes 786440 | tf_op jit(solution)/shard_map/ppermute | solution.py:57
  205.5 9.1 %collective-permute-start.5 = (f32[256,256]{0,1:T(8,128)S(1)}, f32[256,256]{0,1:T(8,128)S(1)}, u32[]{:S(2)}, u32[]{:S(2)}) collective-permute-start(f32[256,256]{0,1:T(8,128)S(1)} %add.61), channel_id=1, source_target_pairs={{0,32},{8,40},{16,48},{24,56},{32,0},{40,8},{48,16},{56,24},{64,96... | collective-permute-start | bytes 786440 | tf_op jit(solution)/shard_map/ppermute | solution.py:57
  214.6 6.8 %collective-permute-start.6 = (f32[256,256]{0,1:T(8,128)S(1)}, f32[256,256]{0,1:T(8,128)S(1)}, u32[]{:S(2)}, u32[]{:S(2)}) collective-permute-start(f32[256,256]{0,1:T(8,128)S(1)} %add.62), channel_id=1, source_target_pairs={{0,64},{8,72},{16,80},{24,88},{32,96},{40,104},{48,112},{56,120},{... | collective-permute-start | bytes 786440 | tf_op jit(solution)/shard_map/ppermute | solution.py:57
  221.4 8.0 %collective-permute-start.7 = (f32[256,256]{0,1:T(8,128)S(1)}, f32[256,256]{0,1:T(8,128)S(1)}, u32[]{:S(2)}, u32[]{:S(2)}) collective-permute-start(f32[256,256]{0,1:T(8,128)S(1)} %add.63), channel_id=1, source_target_pairs={{0,128},{8,136},{16,144},{24,152},{32,160},{40,168},{48,176},{56,1... | collective-permute-start | bytes 786440 | tf_op jit(solution)/shard_map/ppermute | solution.py:57
  229.4 8.6 %collective-permute-start.8 = (f32[256,256]{0,1:T(8,128)S(1)}, f32[256,256]{0,1:T(8,128)S(1)}, u32[]{:S(2)}, u32[]{:S(2)}) collective-permute-start(f32[256,256]{0,1:T(8,128)S(1)} %add.64), channel_id=1, source_target_pairs={{0,1},{1,0},{2,3},{3,2},{4,5},{5,4},{6,7},{7,6},{8,9},{9,8},{10,11... | collective-permute-start | bytes 786440 | tf_op jit(solution)/shard_map/ppermute | solution.py:57
  238.1 15.7 %collective-permute-start.9 = (f32[256,256]{0,1:T(8,128)S(1)}, f32[256,256]{0,1:T(8,128)S(1)}, u32[]{:S(2)}, u32[]{:S(2)}) collective-permute-start(f32[256,256]{0,1:T(8,128)S(1)} %add.65), channel_id=1, source_target_pairs={{0,2},{1,3},{2,0},{3,1},{4,6},{5,7},{6,4},{7,5},{8,10},{9,11},{10,... | collective-permute-start | bytes 786440 | tf_op jit(solution)/shard_map/ppermute | solution.py:57
  253.8 13.2 %collective-permute-start.10 = (f32[256,256]{0,1:T(8,128)S(1)}, f32[256,256]{0,1:T(8,128)S(1)}, u32[]{:S(2)}, u32[]{:S(2)}) collective-permute-start(f32[256,256]{0,1:T(8,128)S(1)} %add.66), channel_id=1, source_target_pairs={{0,4},{1,5},{2,6},{3,7},{4,0},{5,1},{6,2},{7,3},{8,12},{9,13},{10,... | collective-permute-start | bytes 786440 | tf_op jit(solution)/shard_map/ppermute | solution.py:57
  267.9 41.9 %copy-start.2 = (f32[32,256]{1,0:T(8,128)S(1)}, f32[32,256]{1,0:T(8,128)}, u32[]{:S(2)}) copy-start(f32[32,256]{1,0:T(8,128)} %reduce-scatter.2.cloned.1.call-done) | copy-start | bytes 98308
Sparse Core Ops, SparseCore 0:
  10.6 50.3 all-gather.1
  112.4 81.6 reduce-scatter.1

commit v2 on v1

--- a/solution.py
+++ b/solution.py
@@ -59,11 +59,42 @@
     return x
 
 
+def butterfly_gather(x, axis):
+    size = lax.axis_size(axis)
+    me = lax.axis_index(axis)
+    rows, width = x.shape
+    buf = x[None]
+    step = size // 2
+    while step >= 1:
+        other = lax.ppermute(buf, axis, [(i, i ^ step) for i in range(size)])
+        upper = (me // step) % 2 == 1
+        low = jnp.where(upper, other, buf)
+        high = jnp.where(upper, buf, other)
+        buf = jnp.stack([low, high], axis=1).reshape(-1, rows, width)
+        step //= 2
+    return buf.reshape(-1, width)
+
+def butterfly_scatter(x, axis):
+    size = lax.axis_size(axis)
+    me = lax.axis_index(axis)
+    rows = x.shape[0] // size
+    width = x.shape[1]
+    buf = x.reshape(size, rows, width)
+    step = 1
+    while step < size:
+        pairs = buf.reshape(-1, 2, rows, width)
+        upper = (me // step) % 2 == 1
+        keep = jnp.where(upper, pairs[:, 1], pairs[:, 0])
+        send = jnp.where(upper, pairs[:, 0], pairs[:, 1])
+        buf = keep + lax.ppermute(send, axis, [(i, i ^ step) for i in range(size)])
+        step *= 2
+    return buf.reshape(rows, width)
+
 def body(start_block, tile_values, tile_rows, tile_cols, tile_count):
     tile_size = tile_values.shape[-1]
     basis_width = start_block.shape[1]
     slot_total = tile_values.shape[2]
-    slab = lax.all_gather(start_block, "row", axis=0, tiled=True)
+    slab = butterfly_gather(start_block, "row")
     start_blocks = slab.reshape(-1, tile_size, basis_width)
     block_cols = start_blocks.shape[0]
     values = tile_values.reshape(slot_total, tile_size, tile_size)
@@ -110,7 +141,7 @@
         preferred_element_type=jnp.float32,
     )
     partial_flat = partial_projected.reshape(-1, basis_width)
-    projected = lax.psum_scatter(partial_flat, "row", scatter_dimension=0, tiled=True)
+    projected = butterfly_scatter(partial_flat, "row")
     share_rows = projected.shape[0]
     matrix_order = share_rows * lax.axis_size("row") * lax.axis_size("col")
     local_gram = jnp.dot(

time: 319 us -> 221 us (0.69)
  the two profiles are of different devices: /device:TPU:6 before, /device:TPU:30 now
where the time goes in v2:
time: 221 us
  waiting for transfers between devices  137 us (62%)
  Pallas kernels  41.9 us (19%)
  starting transfers between devices  28 us (13%)
  matrix products  8.1 us (4%)
  local copies, waits for them, and re-layouts  2.89 us (1%)
    ppermute x11, waiting for transfers between devices, butterfly_sum(): x = x + lax.ppermute(x, axis, [(i, i ^ step) for i in range(size)])  92.6 us
    pallas_call x1, Pallas kernels, chol_inv(): pl.pallas_call(chol_inv_kernel, out_shape=(jax.ShapeDtypeStruct((n, n), j...  41.9 us
    ppermute x5, waiting for transfers between devices, butterfly_scatter(): buf = keep + lax.ppermute(send, axis, [(i, i ^ step) for i in range(size)])  23.3 us
    ppermute x5, waiting for transfers between devices, butterfly_gather(): other = lax.ppermute(buf, axis, [(i, i ^ step) for i in range(size)])  20.8 us
    ppermute x11, starting transfers between devices, butterfly_sum(): x = x + lax.ppermute(x, axis, [(i, i ^ step) for i in range(size)])  19.7 us
    ppermute x5, starting transfers between devices, butterfly_gather(): other = lax.ppermute(buf, axis, [(i, i ^ step) for i in range(size)])  4.59 us
  transfers between devices with their start and end apart: 21, of which 21 were waited for; matrix products, arithmetic and copies ran while one was open for 0% of the time, Pallas kernels for 0%

profile of v2, /device:TPU:30, one launch (start us, length us, event | category | flops | bytes accessed | tf_op | source)
XLA Modules:
  0.0 221.2 jit_solution(17699626418066892701)
XLA Ops:
  0.7 1.3 collective-permute-start
  2.0 4.4 %collective-permute-done = f32[1,32,256]{2,1,0:T(8,128)S(1)} collective-permute-done((f32[1,32,256]{2,1,0:T(8,128)}, f32[1,32,256]{2,1,0:T(8,128)S(1)}, u32[]{:S(2)}, u32[]{:S(2)}) %collective-permute-start) | collective-permute-done | bytes 32800 | tf_op jit(solution)/shard_map/ppermute | solution.py:69
  7.2 3.5 %collective-permute-done.1 = f32[2,32,256]{2,1,0:T(8,128)S(1)} collective-permute-done((f32[2,32,256]{2,1,0:T(8,128)S(1)}, f32[2,32,256]{2,1,0:T(8,128)S(1)}, u32[]{:S(2)}, u32[]{:S(2)}) %collective-permute-start.1) | collective-permute-done | bytes 65568 | tf_op jit(solution)/shard_map/ppermute | solution.py:69
  10.8 1.5 collective-permute-start.2
  12.3 6.1 %collective-permute-done.2 = f32[4,32,256]{2,1,0:T(8,128)S(1)} collective-permute-done((f32[4,32,256]{2,1,0:T(8,128)S(1)}, f32[4,32,256]{2,1,0:T(8,128)S(1)}, u32[]{:S(2)}, u32[]{:S(2)}) %collective-permute-start.2) | collective-permute-done | bytes 131104 | tf_op jit(solution)/shard_map/ppermute | solution.py:69
  19.3 5.6 %collective-permute-done.3 = f32[8,32,256]{2,1,0:T(8,128)S(1)} collective-permute-done((f32[8,32,256]{2,1,0:T(8,128)S(1)}, f32[8,32,256]{2,1,0:T(8,128)S(1)}, u32[]{:S(2)}, u32[]{:S(2)}) %collective-permute-start.3) | collective-permute-done | bytes 262176 | tf_op jit(solution)/shard_map/ppermute | solution.py:69
  29.9 1.8 fusion.25
  31.8 2.0 collective-permute-start.5
  33.8 6.6 %collective-permute-done.5 = f32[256,256]{1,0:T(8,128)S(1)} collective-permute-done((f32[256,256]{1,0:T(8,128)S(1)}, f32[256,256]{1,0:T(8,128)S(1)}, u32[]{:S(2)}, u32[]{:S(2)}) %collective-permute-start.5) | collective-permute-done | bytes 262176 | tf_op jit(solution)/shard_map/ppermute | solution.py:57
  40.4 3.4 %collective-permute-start.6 = (f32[256,256]{1,0:T(8,128)S(1)}, f32[256,256]{1,0:T(8,128)S(1)}, u32[]{:S(2)}, u32[]{:S(2)}) collective-permute-start(f32[256,256]{1,0:T(8,128)S(1)} %fusion.32), channel_id=1, source_target_pairs={{0,2},{1,3},{2,0},{3,1},{4,6},{5,7},{6,4},{7,5},{8,10},{9,11},{10,... | collective-permute-start | bytes 786440 | tf_op jit(solution)/shard_map/ppermute | solution.py:57
  43.8 11.6 %collective-permute-done.6 = f32[256,256]{1,0:T(8,128)S(1)} collective-permute-done((f32[256,256]{1,0:T(8,128)S(1)}, f32[256,256]{1,0:T(8,128)S(1)}, u32[]{:S(2)}, u32[]{:S(2)}) %collective-permute-start.6) | collective-permute-done | bytes 262176 | tf_op jit(solution)/shard_map/ppermute | solution.py:57
  55.4 6.3 %collective-permute-start.7 = (f32[256,256]{1,0:T(8,128)S(1)}, f32[256,256]{1,0:T(8,128)S(1)}, u32[]{:S(2)}, u32[]{:S(2)}) collective-permute-start(f32[256,256]{1,0:T(8,128)S(1)} %add.101), channel_id=1, source_target_pairs={{0,4},{1,5},{2,6},{3,7},{4,0},{5,1},{6,2},{7,3},{8,12},{9,13},{10,... | collective-permute-start | bytes 786440 | tf_op jit(solution)/shard_map/ppermute | solution.py:57
  61.7 11.7 %collective-permute-done.7 = f32[256,256]{1,0:T(8,128)S(1)} collective-permute-done((f32[256,256]{1,0:T(8,128)S(1)}, f32[256,256]{1,0:T(8,128)S(1)}, u32[]{:S(2)}, u32[]{:S(2)}) %collective-permute-start.7) | collective-permute-done | bytes 262176 | tf_op jit(solution)/shard_map/ppermute | solution.py:57
  75.0 2.3 %fusion.17 = f32[4,256,256]{2,0,1:T(4,128)S(1)} fusion(f32[2,256,256]{2,0,1:T(2,128)S(1)} %copy.77, f32[2]{0:T(128)S(1)} %compare_convert_fusion, s32[2]{0:T(128)S(1)} %bitcast.185), kind=kOutput, calls=%fused_computation.54 | convolution fusion | flops 6291472 | bytes 1572880 | tf_op jit(solution)/shard_map/tc,tik->cik/dot_general | solution.py:136
  77.9 1.9 collective-permute-done.8
  80.8 7.6 %collective-permute-done.9 = f32[8,32,256]{2,1,0:T(8,128)S(1)} collective-permute-done((f32[8,32,256]{2,1,0:T(8,128)S(1)}, f32[8,32,256]{2,1,0:T(8,128)S(1)}, u32[]{:S(2)}, u32[]{:S(2)}) %collective-permute-start.9) | collective-permute-done | bytes 262176 | tf_op jit(solution)/shard_map/ppermute | solution.py:89
  88.9 6.1 %collective-permute-done.10 = f32[4,32,256]{2,1,0:T(8,128)S(1)} collective-permute-done((f32[4,32,256]{2,1,0:T(8,128)S(1)}, f32[4,32,256]{2,1,0:T(8,128)S(1)}, u32[]{:S(2)}, u32[]{:S(2)}) %collective-permute-start.10) | collective-permute-done | bytes 131104 | tf_op jit(solution)/shard_map/ppermute | solution.py:89
  95.9 3.5 %collective-permute-done.11 = f32[2,32,256]{2,1,0:T(8,128)S(1)} collective-permute-done((f32[2,32,256]{2,1,0:T(8,128)S(1)}, f32[2,32,256]{2,1,0:T(8,128)S(1)}, u32[]{:S(2)}, u32[]{:S(2)}) %collective-permute-start.11) | collective-permute-done | bytes 65568 | tf_op jit(solution)/shard_map/ppermute | solution.py:89
  99.4 1.3 collective-permute-start.12
  100.7 4.2 %collective-permute-done.12 = f32[1,32,256]{2,1,0:T(8,128)S(1)} collective-permute-done((f32[1,32,256]{2,1,0:T(8,128)S(1)}, f32[1,32,256]{2,1,0:T(8,128)S(1)}, u32[]{:S(2)}, u32[]{:S(2)}) %collective-permute-start.12) | collective-permute-done | bytes 32800 | tf_op jit(solution)/shard_map/ppermute | solution.py:89
  105.5 1.5 collective-permute-done.13
  107.9 7.6 %collective-permute-done.14 = f32[256,256]{0,1:T(8,128)S(1)} collective-permute-done((f32[256,256]{0,1:T(8,128)S(1)}, f32[256,256]{0,1:T(8,128)S(1)}, u32[]{:S(2)}, u32[]{:S(2)}) %collective-permute-start.14) | collective-permute-done | bytes 262176 | tf_op jit(solution)/shard_map/ppermute | solution.py:57
  116.0 8.6 %collective-permute-done.15 = f32[256,256]{0,1:T(8,128)S(1)} collective-permute-done((f32[256,256]{0,1:T(8,128)S(1)}, f32[256,256]{0,1:T(8,128)S(1)}, u32[]{:S(2)}, u32[]{:S(2)}) %collective-permute-start.15) | collective-permute-done | bytes 262176 | tf_op jit(solution)/shard_map/ppermute | solution.py:57
  125.5 6.6 %collective-permute-done.16 = f32[256,256]{0,1:T(8,128)S(1)} collective-permute-done((f32[256,256]{0,1:T(8,128)S(1)}, f32[256,256]{0,1:T(8,128)S(1)}, u32[]{:S(2)}, u32[]{:S(2)}) %collective-permute-start.16) | collective-permute-done | bytes 262176 | tf_op jit(solution)/shard_map/ppermute | solution.py:57
  132.7 7.4 %collective-permute-done.17 = f32[256,256]{0,1:T(8,128)S(1)} collective-permute-done((f32[256,256]{0,1:T(8,128)S(1)}, f32[256,256]{0,1:T(8,128)S(1)}, u32[]{:S(2)}, u32[]{:S(2)}) %collective-permute-start.17) | collective-permute-done | bytes 262176 | tf_op jit(solution)/shard_map/ppermute | solution.py:57
  140.2 9.1 %collective-permute-done.18 = f32[256,256]{0,1:T(8,128)S(1)} collective-permute-done((f32[256,256]{0,1:T(8,128)S(1)}, f32[256,256]{0,1:T(8,128)S(1)}, u32[]{:S(2)}, u32[]{:S(2)}) %collective-permute-start.18) | collective-permute-done | bytes 262176 | tf_op jit(solution)/shard_map/ppermute | solution.py:57
  149.3 1.9 collective-permute-start.19
  151.2 12.3 %collective-permute-done.19 = f32[256,256]{0,1:T(8,128)S(1)} collective-permute-done((f32[256,256]{0,1:T(8,128)S(1)}, f32[256,256]{0,1:T(8,128)S(1)}, u32[]{:S(2)}, u32[]{:S(2)}) %collective-permute-start.19) | collective-permute-done | bytes 262176 | tf_op jit(solution)/shard_map/ppermute | solution.py:57
  163.5 3.2 %collective-permute-start.20 = (f32[256,256]{0,1:T(8,128)S(1)}, f32[256,256]{0,1:T(8,128)S(1)}, u32[]{:S(2)}, u32[]{:S(2)}) collective-permute-start(f32[256,256]{0,1:T(8,128)S(1)} %add.115), channel_id=1, source_target_pairs={{0,4},{1,5},{2,6},{3,7},{4,0},{5,1},{6,2},{7,3},{8,12},{9,13},{10,... | collective-permute-start | bytes 786440 | tf_op jit(solution)/shard_map/ppermute | solution.py:57
  166.7 9.7 %collective-permute-done.20 = f32[256,256]{0,1:T(8,128)S(1)} collective-permute-done((f32[256,256]{0,1:T(8,128)S(1)}, f32[256,256]{0,1:T(8,128)S(1)}, u32[]{:S(2)}, u32[]{:S(2)}) %collective-permute-start.20) | collective-permute-done | bytes 262176 | tf_op jit(solution)/shard_map/ppermute | solution.py:57
  177.4 41.9 %shard_map.76 = (f32[256,256]{1,0:T(8,128)}, f32[256,256]{1,0:T(8,128)}) custom-call(f32[256,256]{1,0:T(8,128)} %bitcast_select_fusion.2.g_ref), custom_call_target="tpu_custom_call" | custom-call | tf_op jit(solution)/shard_map/pallas_call | solution.py:44
  219.3 1.9 fusion.12
  (72 shorter events, 15.2 us)
Async XLA Ops:
  0.6 27.3 %copy-start = (f32[1,1,2,256,256]{4,3,2,1,0:T(8,128)S(1)}, f32[1,1,2,256,256]{4,3,2,1,0:T(8,128)}, u32[]{:S(2)}) copy-start(f32[1,1,2,256,256]{4,3,2,1,0:T(8,128)} %param.6) | copy-start | bytes 1572868
  0.6 5.7 %copy-start.2 = (f32[32,256]{1,0:T(8,128)S(1)}, f32[32,256]{1,0:T(8,128)}, u32[]{:S(2)}) copy-start(f32[32,256]{1,0:T(8,128)} %param.5) | copy-start | bytes 98308
  0.7 5.7 %collective-permute-start = (f32[1,32,256]{2,1,0:T(8,128)}, f32[1,32,256]{2,1,0:T(8,128)S(1)}, u32[]{:S(2)}, u32[]{:S(2)}) collective-permute-start(f32[1,32,256]{2,1,0:T(8,128)} %bitcast.184), channel_id=1, source_target_pairs={{0,128},{8,136},{16,144},{24,152},{32,160},{40,168},{48,176},{56,1... | collective-permute-start | bytes 98312 | tf_op jit(solution)/shard_map/ppermute | solution.py:69
  6.4 4.4 %collective-permute-start.1 = (f32[2,32,256]{2,1,0:T(8,128)S(1)}, f32[2,32,256]{2,1,0:T(8,128)S(1)}, u32[]{:S(2)}, u32[]{:S(2)}) collective-permute-start(f32[2,32,256]{2,1,0:T(8,128)S(1)} %maximum_bitcast_fusion), channel_id=1, source_target_pairs={{0,64},{8,72},{16,80},{24,88},{32,96},{40,104},{48,112},{56,120},{... | collective-permute-start | bytes 196616 | tf_op jit(solution)/shard_map/ppermute | solution.py:69
  10.8 7.6 %collective-permute-start.2 = (f32[4,32,256]{2,1,0:T(8,128)S(1)}, f32[4,32,256]{2,1,0:T(8,128)S(1)}, u32[]{:S(2)}, u32[]{:S(2)}) collective-permute-start(f32[4,32,256]{2,1,0:T(8,128)S(1)} %bitcast.182), channel_id=1, source_target_pairs={{0,32},{8,40},{16,48},{24,56},{32,0},{40,8},{48,16},{56,24},{64,96... | collective-permute-start | bytes 393224 | tf_op jit(solution)/shard_map/ppermute | solution.py:69
  18.4 6.5 %collective-permute-start.3 = (f32[8,32,256]{2,1,0:T(8,128)S(1)}, f32[8,32,256]{2,1,0:T(8,128)S(1)}, u32[]{:S(2)}, u32[]{:S(2)}) collective-permute-start(f32[8,32,256]{2,1,0:T(8,128)S(1)} %bitcast.181), channel_id=1, source_target_pairs={{0,16},{8,24},{16,0},{24,8},{32,48},{40,56},{48,32},{56,40},{64,80... | collective-permute-start | bytes 786440 | tf_op jit(solution)/shard_map/ppermute | solution.py:69
  25.0 2.0 collective-permute-start.4
  25.2 0.7 copy-start.3
  29.3 0.7 copy-start.4
  31.8 8.6 %collective-permute-start.5 = (f32[256,256]{1,0:T(8,128)S(1)}, f32[256,256]{1,0:T(8,128)S(1)}, u32[]{:S(2)}, u32[]{:S(2)}) collective-permute-start(f32[256,256]{1,0:T(8,128)S(1)} %bitcast.183), channel_id=1, source_target_pairs={{0,1},{1,0},{2,3},{3,2},{4,5},{5,4},{6,7},{7,6},{8,9},{9,8},{10,11... | collective-permute-start | bytes 786440 | tf_op jit(solution)/shard_map/ppermute | solution.py:57
  40.4 15.0 %collective-permute-start.6 = (f32[256,256]{1,0:T(8,128)S(1)}, f32[256,256]{1,0:T(8,128)S(1)}, u32[]{:S(2)}, u32[]{:S(2)}) collective-permute-start(f32[256,256]{1,0:T(8,128)S(1)} %fusion.32), channel_id=1, source_target_pairs={{0,2},{1,3},{2,0},{3,1},{4,6},{5,7},{6,4},{7,5},{8,10},{9,11},{10,... | collective-permute-start | bytes 786440 | tf_op jit(solution)/shard_map/ppermute | solution.py:57
  55.4 17.9 %collective-permute-start.7 = (f32[256,256]{1,0:T(8,128)S(1)}, f32[256,256]{1,0:T(8,128)S(1)}, u32[]{:S(2)}, u32[]{:S(2)}) collective-permute-start(f32[256,256]{1,0:T(8,128)S(1)} %add.101), channel_id=1, source_target_pairs={{0,4},{1,5},{2,6},{3,7},{4,0},{5,1},{6,2},{7,3},{8,12},{9,13},{10,... | collective-permute-start | bytes 786440 | tf_op jit(solution)/shard_map/ppermute | solution.py:57
  73.4 0.7 copy-start.1
  77.6 2.2 collective-permute-start.8
  79.9 8.4 %collective-permute-start.9 = (f32[8,32,256]{2,1,0:T(8,128)S(1)}, f32[8,32,256]{2,1,0:T(8,128)S(1)}, u32[]{:S(2)}, u32[]{:S(2)}) collective-permute-start(f32[8,32,256]{2,1,0:T(8,128)S(1)} %select_bitcast_fusion.3), channel_id=1, source_target_pairs={{0,16},{8,24},{16,0},{24,8},{32,48},{40,56},{48,32},{56,40},{64,80... | collective-permute-start | bytes 786440 | tf_op jit(solution)/shard_map/ppermute | solution.py:89
  88.4 6.6 %collective-permute-start.10 = (f32[4,32,256]{2,1,0:T(8,128)S(1)}, f32[4,32,256]{2,1,0:T(8,128)S(1)}, u32[]{:S(2)}, u32[]{:S(2)}) collective-permute-start(f32[4,32,256]{2,1,0:T(8,128)S(1)} %select_bitcast_fusion.6), channel_id=1, source_target_pairs={{0,32},{8,40},{16,48},{24,56},{32,0},{40,8},{48,16},{56,24},{64,96... | collective-permute-start | bytes 393224 | tf_op jit(solution)/shard_map/ppermute | solution.py:89
  95.0 4.4 %collective-permute-start.11 = (f32[2,32,256]{2,1,0:T(8,128)S(1)}, f32[2,32,256]{2,1,0:T(8,128)S(1)}, u32[]{:S(2)}, u32[]{:S(2)}) collective-permute-start(f32[2,32,256]{2,1,0:T(8,128)S(1)} %select_bitcast_fusion.9), channel_id=1, source_target_pairs={{0,64},{8,72},{16,80},{24,88},{32,96},{40,104},{48,112},{56,120},{... | collective-permute-start | bytes 196616 | tf_op jit(solution)/shard_map/ppermute | solution.py:89
  99.4 5.5 %collective-permute-start.12 = (f32[1,32,256]{2,1,0:T(8,128)S(1)}, f32[1,32,256]{2,1,0:T(8,128)S(1)}, u32[]{:S(2)}, u32[]{:S(2)}) collective-permute-start(f32[1,32,256]{2,1,0:T(8,128)S(1)} %select_bitcast_fusion.12), channel_id=1, source_target_pairs={{0,128},{8,136},{16,144},{24,152},{32,160},{40,168},{48,176},{56,1... | collective-permute-start | bytes 98312 | tf_op jit(solution)/shard_map/ppermute | solution.py:89
  105.4 1.6 collective-permute-start.13
  107.0 8.4 %collective-permute-start.14 = (f32[256,256]{0,1:T(8,128)S(1)}, f32[256,256]{0,1:T(8,128)S(1)}, u32[]{:S(2)}, u32[]{:S(2)}) collective-permute-start(f32[256,256]{0,1:T(8,128)S(1)} %add.109), channel_id=1, source_target_pairs={{0,16},{8,24},{16,0},{24,8},{32,48},{40,56},{48,32},{56,40},{64,80... | collective-permute-start | bytes 786440 | tf_op jit(solution)/shard_map/ppermute | solution.py:57
  115.5 9.1 %collective-permute-start.15 = (f32[256,256]{0,1:T(8,128)S(1)}, f32[256,256]{0,1:T(8,128)S(1)}, u32[]{:S(2)}, u32[]{:S(2)}) collective-permute-start(f32[256,256]{0,1:T(8,128)S(1)} %add.110), channel_id=1, source_target_pairs={{0,32},{8,40},{16,48},{24,56},{32,0},{40,8},{48,16},{56,24},{64,96... | collective-permute-start | bytes 786440 | tf_op jit(solution)/shard_map/ppermute | solution.py:57
  124.7 7.4 %collective-permute-start.16 = (f32[256,256]{0,1:T(8,128)S(1)}, f32[256,256]{0,1:T(8,128)S(1)}, u32[]{:S(2)}, u32[]{:S(2)}) collective-permute-start(f32[256,256]{0,1:T(8,128)S(1)} %add.111), channel_id=1, source_target_pairs={{0,64},{8,72},{16,80},{24,88},{32,96},{40,104},{48,112},{56,120},{... | collective-permute-start | bytes 786440 | tf_op jit(solution)/shard_map/ppermute | solution.py:57
  132.1 8.0 %collective-permute-start.17 = (f32[256,256]{0,1:T(8,128)S(1)}, f32[256,256]{0,1:T(8,128)S(1)}, u32[]{:S(2)}, u32[]{:S(2)}) collective-permute-start(f32[256,256]{0,1:T(8,128)S(1)} %add.112), channel_id=1, source_target_pairs={{0,128},{8,136},{16,144},{24,152},{32,160},{40,168},{48,176},{56,1... | collective-permute-start | bytes 786440 | tf_op jit(solution)/shard_map/ppermute | solution.py:57
  140.1 9.2 %collective-permute-start.18 = (f32[256,256]{0,1:T(8,128)S(1)}, f32[256,256]{0,1:T(8,128)S(1)}, u32[]{:S(2)}, u32[]{:S(2)}) collective-permute-start(f32[256,256]{0,1:T(8,128)S(1)} %add.113), channel_id=1, source_target_pairs={{0,1},{1,0},{2,3},{3,2},{4,5},{5,4},{6,7},{7,6},{8,9},{9,8},{10,11... | collective-permute-start | bytes 786440 | tf_op jit(solution)/shard_map/ppermute | solution.py:57
  149.3 14.2 %collective-permute-start.19 = (f32[256,256]{0,1:T(8,128)S(1)}, f32[256,256]{0,1:T(8,128)S(1)}, u32[]{:S(2)}, u32[]{:S(2)}) collective-permute-start(f32[256,256]{0,1:T(8,128)S(1)} %add.114), channel_id=1, source_target_pairs={{0,2},{1,3},{2,0},{3,1},{4,6},{5,7},{6,4},{7,5},{8,10},{9,11},{10,... | collective-permute-start | bytes 786440 | tf_op jit(solution)/shard_map/ppermute | solution.py:57
  163.5 12.9 %collective-permute-start.20 = (f32[256,256]{0,1:T(8,128)S(1)}, f32[256,256]{0,1:T(8,128)S(1)}, u32[]{:S(2)}, u32[]{:S(2)}) collective-permute-start(f32[256,256]{0,1:T(8,128)S(1)} %add.115), channel_id=1, source_target_pairs={{0,4},{1,5},{2,6},{3,7},{4,0},{5,1},{6,2},{7,3},{8,12},{9,13},{10,... | collective-permute-start | bytes 786440 | tf_op jit(solution)/shard_map/ppermute | solution.py:57

commit v3 on v0

v3 whole, which is shorter than its diff:
```python
import jax
import jax.numpy as jnp
from jax import lax
from jax.experimental import pallas as pl
from jax.experimental.pallas import tpu as pltpu
from jax.sharding import PartitionSpec as P

BR = 1


PHASE = 64

def chol_solve_kernel(g_ref, p_ref, u_ref, x_ref, a_ref):
    n = g_ref.shape[0]
    m = p_ref.shape[0]
    a_ref[...] = g_ref[...]
    u_ref[...] = jnp.zeros_like(u_ref)
    x_ref[...] = p_ref[...]
    for lo in range(0, n, PHASE):
        c0 = (lo // 128) * 128
        nr = n - lo
        nc = n - c0
        sub = lax.broadcasted_iota(jnp.int32, (nr, 1), 0) + lo
        lane = lax.broadcasted_iota(jnp.int32, (1, nc), 1) + c0
        win = lax.broadcasted_iota(jnp.int32, (nr, 128), 1)
        xwin = lax.broadcasted_iota(jnp.int32, (m, 128), 1)
        full = lax.broadcasted_iota(jnp.int32, (1, n), 1)

        def step(j, carry, lo=lo, c0=c0, sub=sub, lane=lane, win=win, xwin=xwin, full=full):
            row = a_ref[pl.ds(j, 1), :]
            ajj = jnp.sum(jnp.where(full == j, row, 0.0), axis=1, keepdims=True)
            piv = jnp.sqrt(ajj)
            lfull = jnp.where(full >= j, row / piv, 0.0)
            lrow = lfull[:, c0:]
            base = pl.multiple_of((j // 128) * 128, 128)
            blk = a_ref[lo:, pl.ds(base, 128)]
            cola = jnp.sum(jnp.where(win == j - base, blk, 0.0), axis=1, keepdims=True)
            lcol = jnp.where(sub >= j, cola / piv, 0.0)
            a_ref[lo:, c0:] = a_ref[lo:, c0:] - lcol * lrow
            u_ref[pl.ds(j, 1), :] = lfull
            xblk = x_ref[:, pl.ds(base, 128)]
            xcol = jnp.sum(jnp.where(xwin == j - base, xblk, 0.0), axis=1, keepdims=True) / piv
            rest = x_ref[:, c0:]
            x_ref[:, c0:] = jnp.where(lane == j, xcol, rest - xcol * jnp.where(lane > j, lrow, 0.0))
            return carry

        lax.fori_loop(lo, lo + PHASE, step, 0)

def chol_solve(g, p):
    n = g.shape[0]
    r = lax.broadcasted_iota(jnp.int32, (n, n), 0)
    c = lax.broadcasted_iota(jnp.int32, (n, n), 1)
    g = jnp.where(r >= c, g, g.T)
    return pl.pallas_call(
        chol_solve_kernel,
        out_shape=(jax.ShapeDtypeStruct((n, n), jnp.float32), jax.ShapeDtypeStruct(p.shape, jnp.float32)),
        in_specs=[pl.BlockSpec(memory_space=pltpu.VMEM)] * 2,
        out_specs=(pl.BlockSpec(memory_space=pltpu.VMEM), pl.BlockSpec(memory_space=pltpu.VMEM)),
        scratch_shapes=[pltpu.VMEM((n, n), jnp.float32)],
    )(g, p)


def group_size(axes):
    size = 1
    for axis in axes:
        size *= lax.axis_size(axis)
    return size


def exchange_sum(x, axes):
    size = group_size(axes)
    chunks = lax.all_to_all(x.reshape(size, -1, x.shape[-1]), axes, 0, 0, tiled=False)
    return jnp.sum(chunks, axis=0)


def exchange_gather(x, axes):
    size = group_size(axes)
    copies = jnp.broadcast_to(x[None], (size,) + x.shape)
    return lax.all_to_all(copies, axes, 0, 0, tiled=False).reshape(-1, x.shape[-1])


def body(start_block, tile_values, tile_rows, tile_cols, tile_count):
    tile_size = tile_values.shape[-1]
    basis_width = start_block.shape[1]
    slot_total = tile_values.shape[2]
    slab = exchange_gather(start_block, ("row",))
    start_blocks = slab.reshape(-1, tile_size, basis_width)
    block_cols = start_blocks.shape[0]
    values = tile_values.reshape(slot_total, tile_size, tile_size)
    row_ids = tile_rows.reshape(slot_total)
    col_ids = tile_cols.reshape(slot_total)
    live_count = tile_count.reshape(())
    block_rows = BR
    live_mask = (jnp.arange(slot_total, dtype=jnp.int32) < live_count).astype(jnp.float32)
    row_onehot = (row_ids[:, None] == jnp.arange(block_rows, dtype=jnp.int32)[None, :]).astype(
        jnp.float32
    ) * live_mask[:, None]
    products = jnp.einsum(
        "tij,tjk->tik",
        values,
        start_blocks[col_ids],
        precision=lax.Precision.HIGHEST,
        preferred_element_type=jnp.float32,
    )
    partial_image = jnp.einsum(
        "tb,tik->bik",
        row_onehot,
        products,
        precision=lax.Precision.HIGHEST,
        preferred_element_type=jnp.float32,
    )
    partial_rows = partial_image.reshape(-1, basis_width)
    image_block = exchange_gather(exchange_sum(partial_rows, ("col",)), ("col",))
    image_blocks = image_block.reshape(block_rows, tile_size, basis_width)
    col_onehot = (col_ids[:, None] == jnp.arange(block_cols, dtype=jnp.int32)[None, :]).astype(
        jnp.float32
    ) * live_mask[:, None]
    back_products = jnp.einsum(
        "tji,tjk->tik",
        values,
        image_blocks[row_ids],
        precision=lax.Precision.HIGHEST,
        preferred_element_type=jnp.float32,
    )
    partial_projected = jnp.einsum(
        "tc,tik->cik",
        col_onehot,
        back_products,
        precision=lax.Precision.HIGHEST,
        preferred_element_type=jnp.float32,
    )
    partial_flat = partial_projected.reshape(-1, basis_width)
    projected = exchange_sum(partial_flat, ("row",))
    share_rows = projected.shape[0]
    matrix_order = share_rows * lax.axis_size("row") * lax.axis_size("col")
    local_gram = jnp.dot(
        projected.T, projected, precision=lax.Precision.HIGHEST, preferred_element_type=jnp.float32
    )
    both = ("row", "col")
    gram_matrix = exchange_gather(exchange_sum(local_gram, both), both) / matrix_order
    factor, new_basis = chol_solve(gram_matrix, projected)
    return (image_block, new_basis, factor)


def solution(mesh):
    placed = (
        P(("col", "row"), None),
        P("row", "col", None, None, None),
        P("row", "col", None),
        P("row", "col", None),
        P("row", "col"),
    )
    return jax.shard_map(
        body,
        mesh=mesh,
        in_specs=placed,
        out_specs=(P("row", None), P(("col", "row"), None), P()),
        check_vma=False,
    )
```

time: 1530 us -> 171 us (0.11)
  local copies, waits for them, and re-layouts: 539 us -> 6.04 us
  waiting for transfers between devices: 462 us -> 25.6 us
  loops' own time: 206 us -> 0 us
  other arithmetic: 177 us -> 1.14 us
  matrix products: 126 us -> 6.01 us
  blocking collectives: 0 us -> 86.8 us
  Pallas kernels: 0 us -> 31.9 us
    dynamic_slice x1024 -> x0, local copies, waits for them, and re-layouts: 329 us -> none  [the longest x256 161 us: row_step(): pivot = lax.dynamic_slice_in_dim(row_l, i, 1, 0)[0]]
    psum x2 -> x0, waiting for transfers between devices: 321 us -> none  [the longest x1 254 us: body(): gram_matrix = lax.psum(local_gram, ('row', 'col')) / matrix_order]
    another operation x2 -> x0, loops' own time: 206 us -> none  [the longest x1 195 us: cholesky_lower(): return lax.fori_loop(0, size, column_step, jnp.zeros_like(gram))]
    dynamic_update_slice x512 -> x0, local copies, waits for them, and re-layouts: 168 us -> none  [the longest x256 157 us: column_step(): return lax.dynamic_update_slice_in_dim(lower, column[:, None], j, 1)]
    div x257 -> x1, other arithmetic: 167 us -> 0.02 us  [body(): exchange_gather(exchange_sum(local_gram, both), both) / matrix_order]
    dot_general x513 -> x0, matrix products: 118 us -> none  [the longest x256 69.8 us: column_step(): jnp.dot(known, row_j, precision=lax.Precision.HIGHEST)]
    all_to_all x0 -> x4, blocking collectives: none -> 86.8 us  [the longest x3 65.7 us: exchange_sum(): lax.all_to_all(x.reshape(size, -1, x.shape[-1]), axes, 0, 0, tiled=False)]
    reduce_scatter x1 -> x0, waiting for transfers between devices: 86.6 us -> none  [body(): lax.psum_scatter(partial_flat, 'row', scatter_dimension=0, tiled=True)]
  transfers between devices with their start and end apart: 4 -> 2, of which waited for: 4 -> 2; matrix products, arithmetic and copies ran while one was open for 0% -> 0% of each run, Pallas kernels for 0% -> 0%
where the time goes in v3:
time: 171 us
  blocking collectives  86.8 us (51%)
  Pallas kernels  31.9 us (19%)
  waiting for transfers between devices  25.6 us (15%)
  starting transfers between devices  12 us (7%)
  local copies, waits for them, and re-layouts  6.04 us (4%)
  matrix products  6.01 us (4%)
    all_to_all x3, blocking collectives, exchange_sum(): lax.all_to_all(x.reshape(size, -1, x.shape[-1]), axes, 0, 0, tiled=False)  65.7 us
    pallas_call x1, Pallas kernels, chol_solve(): pl.pallas_call(chol_solve_kernel, out_shape=(jax.ShapeDtypeStruct((n, n),...  31.9 us
    all_to_all x2, waiting for transfers between devices, exchange_gather(): lax.all_to_all(copies, axes, 0, 0, tiled=False).reshape(-1, x.shape[-1])  25.6 us
    all_to_all x1, blocking collectives, exchange_gather(): lax.all_to_all(copies, axes, 0, 0, tiled=False).reshape(-1, x.shape[-1])  21.1 us
    all_to_all x2, starting transfers between devices, exchange_gather(): lax.all_to_all(copies, axes, 0, 0, tiled=False).reshape(-1, x.shape[-1])  12 us
  transfers between devices with their start and end apart: 2, of which 2 were waited for; matrix products, arithmetic and copies ran while one was open for 0% of the time, Pallas kernels for 0%

profile of v3, /device:TPU:1, one launch (start us, length us, event | category | flops | bytes accessed | tf_op | source)
XLA Modules:
  0.0 171.0 jit_solution(1397118412876939927)
XLA Ops:
  0.6 0.0 copy-start
  0.6 1.9 %broadcast_in_dim.6 = f32[32,32,256]{2,1,0:T(8,128)} broadcast(f32[32,256]{1,0:T(8,128)} %param.5), dimensions={1,2} | broadcast | bytes 1081344 | tf_op jit(solution)/shard_map/broadcast_in_dim | solution.py:78
  2.6 8.6 %all-to-all-start = ((f32[32,32,256]{2,1,0:T(8,128)}), f32[32,32,256]{2,1,0:T(8,128)S(1)}, u32[]{:S(2)}, u32[]{:S(2)}) async-start(f32[32,32,256]{2,1,0:T(8,128)} %broadcast_in_dim.6), calls=%async_computation | async-start | bytes 2097152 | tf_op jit(solution)/shard_map/all_to_all | solution.py:79
  11.9 16.5 %all-to-all-done = f32[32,32,256]{2,1,0:T(8,128)S(1)} async-done(((f32[32,32,256]{2,1,0:T(8,128)}), f32[32,32,256]{2,1,0:T(8,128)S(1)}, u32[]{:S(2)}, u32[]{:S(2)}) %all-to-all-start) | async-done | bytes 1048608 | tf_op jit(solution)/shard_map/all_to_all | solution.py:79
  28.3 0.6 gather_fusion
  28.9 0.7 fusion.1
  29.6 0.0 copy-start.3
  29.6 0.6 copy-done.3
  30.3 2.0 %fusion.3 = f32[1,8,32,256]{3,0,2,1:T(1,128)S(1)} fusion(f32[8,32,256,2]{2,1,0,3:T(8,128)S(1)} %bitcast.50, s32[1,1,2]{2,1,0:T(1,128)S(1)} %copy-done.3, s32[]{:T(128)} %bitcast.43), kind=kOutput, calls=%fused_computation.6 | convolution fusion | flops 1572872 | bytes 786444 | tf_op jit(solution)/shard_map/tb,tik->bik/dot_general | solution.py:105
  32.3 18.9 %all_to_all.30 = f32[8,32,256]{2,1,0:T(8,128)S(1)} all-to-all(f32[8,32,256]{2,1,0:T(8,128)S(1)} %bitcast.49), channel_id=1, replica_groups=mesh['row'=32,'col'=8] {'col'}, dimensions={0} | all-to-all | bytes 524288 | tf_op jit(solution)/shard_map/all_to_all | solution.py:72
  51.3 0.7 broadcast_in_dim.7
  52.0 3.4 %all-to-all-start.2 = ((f32[8,32,256]{2,1,0:T(8,128)}), f32[8,32,256]{2,1,0:T(8,128)S(1)}, u32[]{:S(2)}, u32[]{:S(2)}) async-start(f32[8,32,256]{2,1,0:T(8,128)} %broadcast_in_dim.7), calls=%async_computation.2 | async-start | bytes 524288 | tf_op jit(solution)/shard_map/all_to_all | solution.py:79
  55.4 9.1 %all-to-all-done.2 = f32[8,32,256]{2,1,0:T(8,128)S(1)} async-done(((f32[8,32,256]{2,1,0:T(8,128)}), f32[8,32,256]{2,1,0:T(8,128)S(1)}, u32[]{:S(2)}, u32[]{:S(2)}) %all-to-all-start.2) | async-done | bytes 262176 | tf_op jit(solution)/shard_map/all_to_all | solution.py:79
  64.6 0.1 copy.17
  64.7 0.6 convolution_bitcast_fusion
  65.3 0.2 copy.18
  65.6 2.3 %fusion.7 = f32[4,256,256]{2,0,1:T(4,128)S(1)} fusion(f32[2,256,256]{2,0,1:T(2,128)S(1)} %copy.18, f32[2]{0:T(128)S(1)} %compare_convert_fusion, s32[2]{0:T(128)S(1)} %bitcast.51), kind=kOutput, calls=%fused_computation.20 | convolution fusion | flops 6291472 | bytes 1572880 | tf_op jit(solution)/shard_map/tc,tik->cik/dot_general | solution.py:125
  67.9 0.2 copy.19
  68.1 25.6 %all_to_all.31 = f32[32,32,256]{2,1,0:T(8,128)S(1)} all-to-all(f32[32,32,256]{2,1,0:T(8,128)S(1)} %bitcast.45), channel_id=1, replica_groups=mesh['row'=32,'col'=8] {'row'}, dimensions={0} | all-to-all | bytes 2097152 | tf_op jit(solution)/shard_map/all_to_all | solution.py:72
  93.7 0.1 reduce_sum.28.p_ref
  93.8 0.4 convolution_bitcast_fusion.1
  94.2 0.2 copy-done.1
  94.4 0.3 copy.20
  94.7 21.1 %all_to_all.32 = f32[256,1,256]{2,1,0:T(1,128)S(1)} all-to-all(f32[256,1,256]{2,1,0:T(1,128)S(1)} %copy.20), channel_id=1, replica_groups=mesh['row'=32,'col'=8] {'row','col'}, dimensions={0} | all-to-all | bytes 524288 | tf_op jit(solution)/shard_map/all_to_all | solution.py:72
  115.8 0.3 reduce_sum.29
  116.1 0.1 broadcast_in_dim.8
  116.3 21.1 %all_to_all.33 = f32[256,1,256]{2,1,0:T(1,128)S(1)} all-to-all(f32[256,1,256]{2,1,0:T(1,128)S(1)} %broadcast_in_dim.8), channel_id=1, replica_groups=mesh['row'=32,'col'=8] {'row','col'}, dimensions={0} | all-to-all | bytes 524288 | tf_op jit(solution)/shard_map/all_to_all | solution.py:79
  137.4 0.1 copy.21
  137.6 0.1 copy.22
  137.7 0.7 bitcast_select_fusion.g_ref
  138.4 31.9 %shard_map.76 = (f32[256,256]{1,0:T(8,128)}, f32[32,256]{1,0:T(8,128)}) custom-call(f32[256,256]{1,0:T(8,128)} %bitcast_select_fusion.g_ref, f32[32,256]{1,0:T(8,128)} %copy-done.1), custom_call_target="tpu_custom_call" | custom-call | tf_op jit(solution)/shard_map/pallas_call | solution.py:54
  170.3 0.7 copy.32
  (10 shorter events, 0.1 us)
Async XLA Ops:
  0.6 28.3 %copy-start = (f32[1,1,2,256,256]{4,3,2,1,0:T(8,128)S(1)}, f32[1,1,2,256,256]{4,3,2,1,0:T(8,128)}, u32[]{:S(2)}) copy-start(f32[1,1,2,256,256]{4,3,2,1,0:T(8,128)} %param.6) | copy-start | bytes 1572868
  2.6 25.8 %all-to-all-start = ((f32[32,32,256]{2,1,0:T(8,128)}), f32[32,32,256]{2,1,0:T(8,128)S(1)}, u32[]{:S(2)}, u32[]{:S(2)}) async-start(f32[32,32,256]{2,1,0:T(8,128)} %broadcast_in_dim.6), calls=%async_computation | async-start | bytes 2097152 | tf_op jit(solution)/shard_map/all_to_all | solution.py:79
  11.2 0.7 copy-start.2
  29.6 0.7 copy-start.3
  52.0 12.6 %all-to-all-start.2 = ((f32[8,32,256]{2,1,0:T(8,128)}), f32[8,32,256]{2,1,0:T(8,128)S(1)}, u32[]{:S(2)}, u32[]{:S(2)}) async-start(f32[8,32,256]{2,1,0:T(8,128)} %broadcast_in_dim.7), calls=%async_computation.2 | async-start | bytes 524288 | tf_op jit(solution)/shard_map/all_to_all | solution.py:79
  93.8 0.6 copy-start.1

commit v4 on v3

--- a/solution.py
+++ b/solution.py
@@ -8,7 +8,7 @@
 BR = 1
 
 
-PHASE = 64
+PHASE = 32
 
 def chol_solve_kernel(g_ref, p_ref, u_ref, x_ref, a_ref):
     n = g_ref.shape[0]
@@ -29,17 +29,18 @@
         def step(j, carry, lo=lo, c0=c0, sub=sub, lane=lane, win=win, xwin=xwin, full=full):
             row = a_ref[pl.ds(j, 1), :]
             ajj = jnp.sum(jnp.where(full == j, row, 0.0), axis=1, keepdims=True)
-            piv = jnp.sqrt(ajj)
-            lfull = jnp.where(full >= j, row / piv, 0.0)
+            inv = lax.rsqrt(ajj)
+            lfull = jnp.where(full >= j, row * inv, 0.0)
             lrow = lfull[:, c0:]
             base = pl.multiple_of((j // 128) * 128, 128)
             blk = a_ref[lo:, pl.ds(base, 128)]
             cola = jnp.sum(jnp.where(win == j - base, blk, 0.0), axis=1, keepdims=True)
-            lcol = jnp.where(sub >= j, cola / piv, 0.0)
+            lcol = jnp.where(sub >= j, cola * inv, 0.0)
             a_ref[lo:, c0:] = a_ref[lo:, c0:] - lcol * lrow
             u_ref[pl.ds(j, 1), :] = lfull
             xblk = x_ref[:, pl.ds(base, 128)]
-            xcol = jnp.sum(jnp.where(xwin == j - base, xblk, 0.0), axis=1, keepdims=True) / piv
+            xcol = jnp.sum(jnp.where(xwin == j - base, xblk, 0.0), axis=1, keepdims=True)
+            xcol = xcol * inv
             rest = x_ref[:, c0:]
             x_ref[:, c0:] = jnp.where(lane == j, xcol, rest - xcol * jnp.where(lane > j, lrow, 0.0))
             return carry

time: 171 us -> 170 us (level)
  no operation moved by 1% of the time
where the time goes in v4:
time: 170 us
  blocking collectives  86.8 us (51%)
  Pallas kernels  30.5 us (18%)
  waiting for transfers between devices  25.6 us (15%)
  starting transfers between devices  12 us (7%)
  local copies, waits for them, and re-layouts  6.04 us (4%)
  matrix products  6.01 us (4%)
    all_to_all x3, blocking collectives, exchange_sum(): lax.all_to_all(x.reshape(size, -1, x.shape[-1]), axes, 0, 0, tiled=False)  65.7 us
    pallas_call x1, Pallas kernels, chol_solve(): pl.pallas_call(chol_solve_kernel, out_shape=(jax.ShapeDtypeStruct((n, n),...  30.5 us
    all_to_all x2, waiting for transfers between devices, exchange_gather(): lax.all_to_all(copies, axes, 0, 0, tiled=False).reshape(-1, x.shape[-1])  25.6 us
    all_to_all x1, blocking collectives, exchange_gather(): lax.all_to_all(copies, axes, 0, 0, tiled=False).reshape(-1, x.shape[-1])  21.1 us
    all_to_all x2, starting transfers between devices, exchange_gather(): lax.all_to_all(copies, axes, 0, 0, tiled=False).reshape(-1, x.shape[-1])  12 us
  transfers between devices with their start and end apart: 2, of which 2 were waited for; matrix products, arithmetic and copies ran while one was open for 0% of the time, Pallas kernels for 0%

profile of v4, /device:TPU:1, one launch (start us, length us, event | category | flops | bytes accessed | tf_op | source)
XLA Modules:
  0.0 169.6 jit_solution(2119257997146786939)
XLA Ops:
  0.6 0.0 copy-start
  0.6 1.9 %broadcast_in_dim.6 = f32[32,32,256]{2,1,0:T(8,128)} broadcast(f32[32,256]{1,0:T(8,128)} %param.5), dimensions={1,2} | broadcast | bytes 1081344 | tf_op jit(solution)/shard_map/broadcast_in_dim | solution.py:79
  2.6 8.6 %all-to-all-start = ((f32[32,32,256]{2,1,0:T(8,128)}), f32[32,32,256]{2,1,0:T(8,128)S(1)}, u32[]{:S(2)}, u32[]{:S(2)}) async-start(f32[32,32,256]{2,1,0:T(8,128)} %broadcast_in_dim.6), calls=%async_computation | async-start | bytes 2097152 | tf_op jit(solution)/shard_map/all_to_all | solution.py:80
  11.9 16.5 %all-to-all-done = f32[32,32,256]{2,1,0:T(8,128)S(1)} async-done(((f32[32,32,256]{2,1,0:T(8,128)}), f32[32,32,256]{2,1,0:T(8,128)S(1)}, u32[]{:S(2)}, u32[]{:S(2)}) %all-to-all-start) | async-done | bytes 1048608 | tf_op jit(solution)/shard_map/all_to_all | solution.py:80
  28.3 0.6 gather_fusion
  28.9 0.7 fusion.1
  29.6 0.0 copy-start.3
  29.6 0.6 copy-done.3
  30.3 2.0 %fusion.3 = f32[1,8,32,256]{3,0,2,1:T(1,128)S(1)} fusion(f32[8,32,256,2]{2,1,0,3:T(8,128)S(1)} %bitcast.50, s32[1,1,2]{2,1,0:T(1,128)S(1)} %copy-done.3, s32[]{:T(128)} %bitcast.43), kind=kOutput, calls=%fused_computation.6 | convolution fusion | flops 1572872 | bytes 786444 | tf_op jit(solution)/shard_map/tb,tik->bik/dot_general | solution.py:106
  32.3 18.9 %all_to_all.30 = f32[8,32,256]{2,1,0:T(8,128)S(1)} all-to-all(f32[8,32,256]{2,1,0:T(8,128)S(1)} %bitcast.49), channel_id=1, replica_groups=mesh['row'=32,'col'=8] {'col'}, dimensions={0} | all-to-all | bytes 524288 | tf_op jit(solution)/shard_map/all_to_all | solution.py:73
  51.3 0.7 broadcast_in_dim.7
  52.0 3.4 %all-to-all-start.2 = ((f32[8,32,256]{2,1,0:T(8,128)}), f32[8,32,256]{2,1,0:T(8,128)S(1)}, u32[]{:S(2)}, u32[]{:S(2)}) async-start(f32[8,32,256]{2,1,0:T(8,128)} %broadcast_in_dim.7), calls=%async_computation.2 | async-start | bytes 524288 | tf_op jit(solution)/shard_map/all_to_all | solution.py:80
  55.4 9.1 %all-to-all-done.2 = f32[8,32,256]{2,1,0:T(8,128)S(1)} async-done(((f32[8,32,256]{2,1,0:T(8,128)}), f32[8,32,256]{2,1,0:T(8,128)S(1)}, u32[]{:S(2)}, u32[]{:S(2)}) %all-to-all-start.2) | async-done | bytes 262176 | tf_op jit(solution)/shard_map/all_to_all | solution.py:80
  64.6 0.1 copy.17
  64.7 0.6 convolution_bitcast_fusion
  65.3 0.2 copy.18
  65.6 2.3 %fusion.7 = f32[4,256,256]{2,0,1:T(4,128)S(1)} fusion(f32[2,256,256]{2,0,1:T(2,128)S(1)} %copy.18, f32[2]{0:T(128)S(1)} %compare_convert_fusion, s32[2]{0:T(128)S(1)} %bitcast.51), kind=kOutput, calls=%fused_computation.20 | convolution fusion | flops 6291472 | bytes 1572880 | tf_op jit(solution)/shard_map/tc,tik->cik/dot_general | solution.py:126
  67.9 0.2 copy.19
  68.1 25.6 %all_to_all.31 = f32[32,32,256]{2,1,0:T(8,128)S(1)} all-to-all(f32[32,32,256]{2,1,0:T(8,128)S(1)} %bitcast.45), channel_id=1, replica_groups=mesh['row'=32,'col'=8] {'row'}, dimensions={0} | all-to-all | bytes 2097152 | tf_op jit(solution)/shard_map/all_to_all | solution.py:73
  93.7 0.1 reduce_sum.28.p_ref
  93.8 0.4 convolution_bitcast_fusion.1
  94.2 0.2 copy-done.1
  94.4 0.3 copy.20
  94.7 21.1 %all_to_all.32 = f32[256,1,256]{2,1,0:T(1,128)S(1)} all-to-all(f32[256,1,256]{2,1,0:T(1,128)S(1)} %copy.20), channel_id=1, replica_groups=mesh['row'=32,'col'=8] {'row','col'}, dimensions={0} | all-to-all | bytes 524288 | tf_op jit(solution)/shard_map/all_to_all | solution.py:73
  115.8 0.3 reduce_sum.29
  116.1 0.1 broadcast_in_dim.8
  116.3 21.1 %all_to_all.33 = f32[256,1,256]{2,1,0:T(1,128)S(1)} all-to-all(f32[256,1,256]{2,1,0:T(1,128)S(1)} %broadcast_in_dim.8), channel_id=1, replica_groups=mesh['row'=32,'col'=8] {'row','col'}, dimensions={0} | all-to-all | bytes 524288 | tf_op jit(solution)/shard_map/all_to_all | solution.py:80
  137.4 0.1 copy.21
  137.6 0.1 copy.22
  137.7 0.7 bitcast_select_fusion.g_ref
  138.4 30.5 %shard_map.76 = (f32[256,256]{1,0:T(8,128)}, f32[32,256]{1,0:T(8,128)}) custom-call(f32[256,256]{1,0:T(8,128)} %bitcast_select_fusion.g_ref, f32[32,256]{1,0:T(8,128)} %copy-done.1), custom_call_target="tpu_custom_call" | custom-call | tf_op jit(solution)/shard_map/pallas_call | solution.py:55
  168.9 0.7 copy.32
  (10 shorter events, 0.1 us)
Async XLA Ops:
  0.6 28.3 %copy-start = (f32[1,1,2,256,256]{4,3,2,1,0:T(8,128)S(1)}, f32[1,1,2,256,256]{4,3,2,1,0:T(8,128)}, u32[]{:S(2)}) copy-start(f32[1,1,2,256,256]{4,3,2,1,0:T(8,128)} %param.6) | copy-start | bytes 1572868
  2.6 25.8 %all-to-all-start = ((f32[32,32,256]{2,1,0:T(8,128)}), f32[32,32,256]{2,1,0:T(8,128)S(1)}, u32[]{:S(2)}, u32[]{:S(2)}) async-start(f32[32,32,256]{2,1,0:T(8,128)} %broadcast_in_dim.6), calls=%async_computation | async-start | bytes 2097152 | tf_op jit(solution)/shard_map/all_to_all | solution.py:80
  11.2 0.7 copy-start.2
  29.6 0.7 copy-start.3
  52.0 12.6 %all-to-all-start.2 = ((f32[8,32,256]{2,1,0:T(8,128)}), f32[8,32,256]{2,1,0:T(8,128)S(1)}, u32[]{:S(2)}, u32[]{:S(2)}) async-start(f32[8,32,256]{2,1,0:T(8,128)} %broadcast_in_dim.7), calls=%async_computation.2 | async-start | bytes 524288 | tf_op jit(solution)/shard_map/all_to_all | solution.py:80
  93.8 0.6 copy-start.1

commit v5 on v4

--- a/solution.py
+++ b/solution.py
@@ -10,42 +10,52 @@
 
 PHASE = 32
 
+def pick(vec, lanes, at):
+    return jnp.sum(jnp.where(lanes == at, vec, 0.0), axis=1, keepdims=True)
+
+
 def chol_solve_kernel(g_ref, p_ref, u_ref, x_ref, a_ref):
     n = g_ref.shape[0]
     m = p_ref.shape[0]
     a_ref[...] = g_ref[...]
     u_ref[...] = jnp.zeros_like(u_ref)
     x_ref[...] = p_ref[...]
+    full = lax.broadcasted_iota(jnp.int32, (1, n), 1)
+    xwin = lax.broadcasted_iota(jnp.int32, (m, 128), 1)
     for lo in range(0, n, PHASE):
         c0 = (lo // 128) * 128
         nr = n - lo
-        nc = n - c0
         sub = lax.broadcasted_iota(jnp.int32, (nr, 1), 0) + lo
-        lane = lax.broadcasted_iota(jnp.int32, (1, nc), 1) + c0
+        lane = lax.broadcasted_iota(jnp.int32, (1, n - c0), 1) + c0
         win = lax.broadcasted_iota(jnp.int32, (nr, 128), 1)
-        xwin = lax.broadcasted_iota(jnp.int32, (m, 128), 1)
-        full = lax.broadcasted_iota(jnp.int32, (1, n), 1)
 
-        def step(j, carry, lo=lo, c0=c0, sub=sub, lane=lane, win=win, xwin=xwin, full=full):
-            row = a_ref[pl.ds(j, 1), :]
-            ajj = jnp.sum(jnp.where(full == j, row, 0.0), axis=1, keepdims=True)
-            inv = lax.rsqrt(ajj)
-            lfull = jnp.where(full >= j, row * inv, 0.0)
-            lrow = lfull[:, c0:]
+        def step(t, carry, lo=lo, c0=c0, sub=sub, lane=lane, win=win):
+            j = 2 * t
+            k = j + 1
+            first = a_ref[pl.ds(j, 1), :]
+            second = a_ref[pl.ds(k, 1), :]
+            inv1 = lax.rsqrt(pick(first, full, j))
+            l21 = pick(first, full, k) * inv1
+            inv2 = lax.rsqrt(pick(second, full, k) - l21 * l21)
+            row1 = jnp.where(full >= j, first * inv1, 0.0)
+            row2 = jnp.where(full >= k, (second - l21 * row1) * inv2, 0.0)
             base = pl.multiple_of((j // 128) * 128, 128)
             blk = a_ref[lo:, pl.ds(base, 128)]
-            cola = jnp.sum(jnp.where(win == j - base, blk, 0.0), axis=1, keepdims=True)
-            lcol = jnp.where(sub >= j, cola * inv, 0.0)
-            a_ref[lo:, c0:] = a_ref[lo:, c0:] - lcol * lrow
-            u_ref[pl.ds(j, 1), :] = lfull
+            col1 = jnp.where(sub >= j, pick(blk, win, j - base) * inv1, 0.0)
+            col2 = jnp.where(sub >= k, (pick(blk, win, k - base) - col1 * l21) * inv2, 0.0)
+            a_ref[lo:, c0:] = a_ref[lo:, c0:] - (col1 * row1[:, c0:] + col2 * row2[:, c0:])
+            u_ref[pl.ds(j, 1), :] = row1
+            u_ref[pl.ds(k, 1), :] = row2
             xblk = x_ref[:, pl.ds(base, 128)]
-            xcol = jnp.sum(jnp.where(xwin == j - base, xblk, 0.0), axis=1, keepdims=True)
-            xcol = xcol * inv
-            rest = x_ref[:, c0:]
-            x_ref[:, c0:] = jnp.where(lane == j, xcol, rest - xcol * jnp.where(lane > j, lrow, 0.0))
+            x1 = pick(xblk, xwin, j - base) * inv1
+            x2 = (pick(xblk, xwin, k - base) - x1 * l21) * inv2
+            later = lane > k
+            rest = x_ref[:, c0:] - (x1 * jnp.where(later, row1[:, c0:], 0.0) + x2 * jnp.where(later, row2[:, c0:], 0.0))
+            x_ref[:, c0:] = jnp.where(lane == j, x1, jnp.where(lane == k, x2, rest))
             return carry
 
-        lax.fori_loop(lo, lo + PHASE, step, 0)
+        lax.fori_loop(lo // 2, (lo + PHASE) // 2, step, 0)
+
 
 def chol_solve(g, p):
     n = g.shape[0]

time: 170 us -> 160 us (0.941)
  Pallas kernels: 30.5 us -> 20.3 us
    pallas_call x1, Pallas kernels: 30.5 us -> 20.3 us  [chol_solve(): pl.pallas_call(chol_solve_kernel, out_shape=(jax.ShapeDtypeStruct((n, n),...]
where the time goes in v5:
time: 160 us; the launch traced here: 159 us
  blocking collectives  86.8 us (54%)
  waiting for transfers between devices  25.6 us (16%)
  Pallas kernels  20.3 us (13%)
  starting transfers between devices  12 us (8%)
  local copies, waits for them, and re-layouts  6.04 us (4%)
  matrix products  6.01 us (4%)
    all_to_all x3, blocking collectives, exchange_sum(): lax.all_to_all(x.reshape(size, -1, x.shape[-1]), axes, 0, 0, tiled=False)  65.7 us
    all_to_all x2, waiting for transfers between devices, exchange_gather(): lax.all_to_all(copies, axes, 0, 0, tiled=False).reshape(-1, x.shape[-1])  25.6 us
    all_to_all x1, blocking collectives, exchange_gather(): lax.all_to_all(copies, axes, 0, 0, tiled=False).reshape(-1, x.shape[-1])  21.1 us
    pallas_call x1, Pallas kernels, chol_solve(): pl.pallas_call(chol_solve_kernel, out_shape=(jax.ShapeDtypeStruct((n, n),...  20.3 us
    all_to_all x2, starting transfers between devices, exchange_gather(): lax.all_to_all(copies, axes, 0, 0, tiled=False).reshape(-1, x.shape[-1])  12 us
  transfers between devices with their start and end apart: 2, of which 2 were waited for; matrix products, arithmetic and copies ran while one was open for 0% of the time, Pallas kernels for 0%

profile of v5, /device:TPU:1, one launch (start us, length us, event | category | flops | bytes accessed | tf_op | source)
XLA Modules:
  0.0 159.5 jit_solution(2826956761869513838)
XLA Ops:
  0.6 0.0 copy-start
  0.6 1.9 %broadcast_in_dim.6 = f32[32,32,256]{2,1,0:T(8,128)} broadcast(f32[32,256]{1,0:T(8,128)} %param.5), dimensions={1,2} | broadcast | bytes 1081344 | tf_op jit(solution)/shard_map/broadcast_in_dim | solution.py:89
  2.6 8.6 %all-to-all-start = ((f32[32,32,256]{2,1,0:T(8,128)}), f32[32,32,256]{2,1,0:T(8,128)S(1)}, u32[]{:S(2)}, u32[]{:S(2)}) async-start(f32[32,32,256]{2,1,0:T(8,128)} %broadcast_in_dim.6), calls=%async_computation | async-start | bytes 2097152 | tf_op jit(solution)/shard_map/all_to_all | solution.py:90
  11.9 16.5 %all-to-all-done = f32[32,32,256]{2,1,0:T(8,128)S(1)} async-done(((f32[32,32,256]{2,1,0:T(8,128)}), f32[32,32,256]{2,1,0:T(8,128)S(1)}, u32[]{:S(2)}, u32[]{:S(2)}) %all-to-all-start) | async-done | bytes 1048608 | tf_op jit(solution)/shard_map/all_to_all | solution.py:90
  28.3 0.6 gather_fusion
  28.9 0.7 fusion.1
  29.6 0.0 copy-start.3
  29.6 0.6 copy-done.3
  30.3 2.0 %fusion.3 = f32[1,8,32,256]{3,0,2,1:T(1,128)S(1)} fusion(f32[8,32,256,2]{2,1,0,3:T(8,128)S(1)} %bitcast.50, s32[1,1,2]{2,1,0:T(1,128)S(1)} %copy-done.3, s32[]{:T(128)} %bitcast.43), kind=kOutput, calls=%fused_computation.6 | convolution fusion | flops 1572872 | bytes 786444 | tf_op jit(solution)/shard_map/tb,tik->bik/dot_general | solution.py:116
  32.3 18.9 %all_to_all.30 = f32[8,32,256]{2,1,0:T(8,128)S(1)} all-to-all(f32[8,32,256]{2,1,0:T(8,128)S(1)} %bitcast.49), channel_id=1, replica_groups=mesh['row'=32,'col'=8] {'col'}, dimensions={0} | all-to-all | bytes 524288 | tf_op jit(solution)/shard_map/all_to_all | solution.py:83
  51.3 0.7 broadcast_in_dim.7
  52.0 3.4 %all-to-all-start.2 = ((f32[8,32,256]{2,1,0:T(8,128)}), f32[8,32,256]{2,1,0:T(8,128)S(1)}, u32[]{:S(2)}, u32[]{:S(2)}) async-start(f32[8,32,256]{2,1,0:T(8,128)} %broadcast_in_dim.7), calls=%async_computation.2 | async-start | bytes 524288 | tf_op jit(solution)/shard_map/all_to_all | solution.py:90
  55.4 9.1 %all-to-all-done.2 = f32[8,32,256]{2,1,0:T(8,128)S(1)} async-done(((f32[8,32,256]{2,1,0:T(8,128)}), f32[8,32,256]{2,1,0:T(8,128)S(1)}, u32[]{:S(2)}, u32[]{:S(2)}) %all-to-all-start.2) | async-done | bytes 262176 | tf_op jit(solution)/shard_map/all_to_all | solution.py:90
  64.6 0.1 copy.17
  64.7 0.6 convolution_bitcast_fusion
  65.3 0.2 copy.18
  65.6 2.3 %fusion.7 = f32[4,256,256]{2,0,1:T(4,128)S(1)} fusion(f32[2,256,256]{2,0,1:T(2,128)S(1)} %copy.18, f32[2]{0:T(128)S(1)} %compare_convert_fusion, s32[2]{0:T(128)S(1)} %bitcast.51), kind=kOutput, calls=%fused_computation.20 | convolution fusion | flops 6291472 | bytes 1572880 | tf_op jit(solution)/shard_map/tc,tik->cik/dot_general | solution.py:136
  67.9 0.2 copy.19
  68.1 25.6 %all_to_all.31 = f32[32,32,256]{2,1,0:T(8,128)S(1)} all-to-all(f32[32,32,256]{2,1,0:T(8,128)S(1)} %bitcast.45), channel_id=1, replica_groups=mesh['row'=32,'col'=8] {'row'}, dimensions={0} | all-to-all | bytes 2097152 | tf_op jit(solution)/shard_map/all_to_all | solution.py:83
  93.7 0.1 reduce_sum.28.p_ref
  93.8 0.4 convolution_bitcast_fusion.1
  94.2 0.2 copy-done.1
  94.4 0.3 copy.20
  94.7 21.1 %all_to_all.32 = f32[256,1,256]{2,1,0:T(1,128)S(1)} all-to-all(f32[256,1,256]{2,1,0:T(1,128)S(1)} %copy.20), channel_id=1, replica_groups=mesh['row'=32,'col'=8] {'row','col'}, dimensions={0} | all-to-all | bytes 524288 | tf_op jit(solution)/shard_map/all_to_all | solution.py:83
  115.8 0.3 reduce_sum.29
  116.1 0.1 broadcast_in_dim.8
  116.3 21.1 %all_to_all.33 = f32[256,1,256]{2,1,0:T(1,128)S(1)} all-to-all(f32[256,1,256]{2,1,0:T(1,128)S(1)} %broadcast_in_dim.8), channel_id=1, replica_groups=mesh['row'=32,'col'=8] {'row','col'}, dimensions={0} | all-to-all | bytes 524288 | tf_op jit(solution)/shard_map/all_to_all | solution.py:90
  137.4 0.1 copy.21
  137.6 0.1 copy.22
  137.7 0.7 bitcast_select_fusion.g_ref
  138.4 20.3 %shard_map.76 = (f32[256,256]{1,0:T(8,128)}, f32[32,256]{1,0:T(8,128)}) custom-call(f32[256,256]{1,0:T(8,128)} %bitcast_select_fusion.g_ref, f32[32,256]{1,0:T(8,128)} %copy-done.1), custom_call_target="tpu_custom_call" | custom-call | tf_op jit(solution)/shard_map/pallas_call | solution.py:65
  158.8 0.7 copy.32
  (10 shorter events, 0.1 us)
Async XLA Ops:
  0.6 28.3 %copy-start = (f32[1,1,2,256,256]{4,3,2,1,0:T(8,128)S(1)}, f32[1,1,2,256,256]{4,3,2,1,0:T(8,128)}, u32[]{:S(2)}) copy-start(f32[1,1,2,256,256]{4,3,2,1,0:T(8,128)} %param.6) | copy-start | bytes 1572868
  2.6 25.8 %all-to-all-start = ((f32[32,32,256]{2,1,0:T(8,128)}), f32[32,32,256]{2,1,0:T(8,128)S(1)}, u32[]{:S(2)}, u32[]{:S(2)}) async-start(f32[32,32,256]{2,1,0:T(8,128)} %broadcast_in_dim.6), calls=%async_computation | async-start | bytes 2097152 | tf_op jit(solution)/shard_map/all_to_all | solution.py:90
  11.2 0.7 copy-start.2
  29.6 0.7 copy-start.3
  52.0 12.6 %all-to-all-start.2 = ((f32[8,32,256]{2,1,0:T(8,128)}), f32[8,32,256]{2,1,0:T(8,128)S(1)}, u32[]{:S(2)}, u32[]{:S(2)}) async-start(f32[8,32,256]{2,1,0:T(8,128)} %broadcast_in_dim.7), calls=%async_computation.2 | async-start | bytes 524288 | tf_op jit(solution)/shard_map/all_to_all | solution.py:90
  93.8 0.6 copy-start.1

commit v6 on v5

--- a/solution.py
+++ b/solution.py
@@ -9,6 +9,8 @@
 
 
 PHASE = 32
+BLOCK = 4
+
 
 def pick(vec, lanes, at):
     return jnp.sum(jnp.where(lanes == at, vec, 0.0), axis=1, keepdims=True)
@@ -17,6 +19,7 @@
 def chol_solve_kernel(g_ref, p_ref, u_ref, x_ref, a_ref):
     n = g_ref.shape[0]
     m = p_ref.shape[0]
+    width = BLOCK
     a_ref[...] = g_ref[...]
     u_ref[...] = jnp.zeros_like(u_ref)
     x_ref[...] = p_ref[...]
@@ -30,31 +33,52 @@
         win = lax.broadcasted_iota(jnp.int32, (nr, 128), 1)
 
         def step(t, carry, lo=lo, c0=c0, sub=sub, lane=lane, win=win):
-            j = 2 * t
-            k = j + 1
-            first = a_ref[pl.ds(j, 1), :]
-            second = a_ref[pl.ds(k, 1), :]
-            inv1 = lax.rsqrt(pick(first, full, j))
-            l21 = pick(first, full, k) * inv1
-            inv2 = lax.rsqrt(pick(second, full, k) - l21 * l21)
-            row1 = jnp.where(full >= j, first * inv1, 0.0)
-            row2 = jnp.where(full >= k, (second - l21 * row1) * inv2, 0.0)
-            base = pl.multiple_of((j // 128) * 128, 128)
+            j0 = width * t
+            base = pl.multiple_of((j0 // 128) * 128, 128)
             blk = a_ref[lo:, pl.ds(base, 128)]
-            col1 = jnp.where(sub >= j, pick(blk, win, j - base) * inv1, 0.0)
-            col2 = jnp.where(sub >= k, (pick(blk, win, k - base) - col1 * l21) * inv2, 0.0)
-            a_ref[lo:, c0:] = a_ref[lo:, c0:] - (col1 * row1[:, c0:] + col2 * row2[:, c0:])
-            u_ref[pl.ds(j, 1), :] = row1
-            u_ref[pl.ds(k, 1), :] = row2
             xblk = x_ref[:, pl.ds(base, 128)]
-            x1 = pick(xblk, xwin, j - base) * inv1
-            x2 = (pick(xblk, xwin, k - base) - x1 * l21) * inv2
-            later = lane > k
-            rest = x_ref[:, c0:] - (x1 * jnp.where(later, row1[:, c0:], 0.0) + x2 * jnp.where(later, row2[:, c0:], 0.0))
-            x_ref[:, c0:] = jnp.where(lane == j, x1, jnp.where(lane == k, x2, rest))
+            raw = [a_ref[pl.ds(j0 + i, 1), :] for i in range(width)]
+            entry = {(i, k): pick(raw[i], full, j0 + k) for i in range(width) for k in range(i, width)}
+            low, inv = {}, []
+            for i in range(width):
+                d = entry[(i, i)]
+                for q in range(i):
+                    d = d - low[(i, q)] * low[(i, q)]
+                inv.append(lax.rsqrt(d))
+                for k in range(i + 1, width):
+                    v = entry[(i, k)]
+                    for q in range(i):
+                        v = v - low[(k, q)] * low[(i, q)]
+                    low[(k, i)] = v * inv[i]
+            rows, cols, xs = [], [], []
+            for i in range(width):
+                j = j0 + i
+                row = raw[i]
+                col = pick(blk, win, j - base)
+                xv = pick(xblk, xwin, j - base)
+                for q in range(i):
+                    row = row - low[(i, q)] * rows[q]
+                    col = col - cols[q] * low[(i, q)]
+                    xv = xv - xs[q] * low[(i, q)]
+                rows.append(jnp.where(full >= j, row * inv[i], 0.0))
+                cols.append(jnp.where(sub >= j, col * inv[i], 0.0))
+                xs.append(xv * inv[i])
+            update = cols[0] * rows[0][:, c0:]
+            for i in range(1, width):
+                update = update + cols[i] * rows[i][:, c0:]
+            a_ref[lo:, c0:] = a_ref[lo:, c0:] - update
+            for i in range(width):
+                u_ref[pl.ds(j0 + i, 1), :] = rows[i]
+            later = lane >= j0 + width
+            rest = x_ref[:, c0:]
+            for i in range(width):
+                rest = rest - xs[i] * jnp.where(later, rows[i][:, c0:], 0.0)
+            for i in range(width):
+                rest = jnp.where(lane == j0 + i, xs[i], rest)
+            x_ref[:, c0:] = rest
             return carry
 
-        lax.fori_loop(lo // 2, (lo + PHASE) // 2, step, 0)
+        lax.fori_loop(lo // width, (lo + PHASE) // width, step, 0)
 
 
 def chol_solve(g, p):

time: 160 us -> 156 us (0.975)
  Pallas kernels: 20.3 us -> 16.4 us
    pallas_call x1, Pallas kernels: 20.3 us -> 16.4 us  [chol_solve(): pl.pallas_call(chol_solve_kernel, out_shape=(jax.ShapeDtypeStruct((n, n),...]
where the time goes in v6:
time: 156 us
  blocking collectives  86.8 us (56%)
  waiting for transfers between devices  25.6 us (16%)
  Pallas kernels  16.4 us (11%)
  starting transfers between devices  12 us (8%)
  local copies, waits for them, and re-layouts  6.04 us (4%)
  matrix products  6.01 us (4%)
    all_to_all x3, blocking collectives, exchange_sum(): lax.all_to_all(x.reshape(size, -1, x.shape[-1]), axes, 0, 0, tiled=False)  65.7 us
    all_to_all x2, waiting for transfers between devices, exchange_gather(): lax.all_to_all(copies, axes, 0, 0, tiled=False).reshape(-1, x.shape[-1])  25.6 us
    all_to_all x1, blocking collectives, exchange_gather(): lax.all_to_all(copies, axes, 0, 0, tiled=False).reshape(-1, x.shape[-1])  21.1 us
    pallas_call x1, Pallas kernels, chol_solve(): pl.pallas_call(chol_solve_kernel, out_shape=(jax.ShapeDtypeStruct((n, n),...  16.4 us
    all_to_all x2, starting transfers between devices, exchange_gather(): lax.all_to_all(copies, axes, 0, 0, tiled=False).reshape(-1, x.shape[-1])  12 us
  transfers between devices with their start and end apart: 2, of which 2 were waited for; matrix products, arithmetic and copies ran while one was open for 0% of the time, Pallas kernels for 0%

profile of v6, /device:TPU:1, one launch (start us, length us, event | category | flops | bytes accessed | tf_op | source)
XLA Modules:
  0.0 155.5 jit_solution(5531475290940969522)
XLA Ops:
  0.6 0.0 copy-start
  0.6 1.9 %broadcast_in_dim.6 = f32[32,32,256]{2,1,0:T(8,128)} broadcast(f32[32,256]{1,0:T(8,128)} %param.5), dimensions={1,2} | broadcast | bytes 1081344 | tf_op jit(solution)/shard_map/broadcast_in_dim | solution.py:113
  2.6 8.6 %all-to-all-start = ((f32[32,32,256]{2,1,0:T(8,128)}), f32[32,32,256]{2,1,0:T(8,128)S(1)}, u32[]{:S(2)}, u32[]{:S(2)}) async-start(f32[32,32,256]{2,1,0:T(8,128)} %broadcast_in_dim.6), calls=%async_computation | async-start | bytes 2097152 | tf_op jit(solution)/shard_map/all_to_all | solution.py:114
  11.9 16.5 %all-to-all-done = f32[32,32,256]{2,1,0:T(8,128)S(1)} async-done(((f32[32,32,256]{2,1,0:T(8,128)}), f32[32,32,256]{2,1,0:T(8,128)S(1)}, u32[]{:S(2)}, u32[]{:S(2)}) %all-to-all-start) | async-done | bytes 1048608 | tf_op jit(solution)/shard_map/all_to_all | solution.py:114
  28.3 0.6 gather_fusion
  28.9 0.7 fusion.1
  29.6 0.0 copy-start.3
  29.6 0.6 copy-done.3
  30.3 2.0 %fusion.3 = f32[1,8,32,256]{3,0,2,1:T(1,128)S(1)} fusion(f32[8,32,256,2]{2,1,0,3:T(8,128)S(1)} %bitcast.50, s32[1,1,2]{2,1,0:T(1,128)S(1)} %copy-done.3, s32[]{:T(128)} %bitcast.43), kind=kOutput, calls=%fused_computation.6 | convolution fusion | flops 1572872 | bytes 786444 | tf_op jit(solution)/shard_map/tb,tik->bik/dot_general | solution.py:140
  32.3 18.9 %all_to_all.30 = f32[8,32,256]{2,1,0:T(8,128)S(1)} all-to-all(f32[8,32,256]{2,1,0:T(8,128)S(1)} %bitcast.49), channel_id=1, replica_groups=mesh['row'=32,'col'=8] {'col'}, dimensions={0} | all-to-all | bytes 524288 | tf_op jit(solution)/shard_map/all_to_all | solution.py:107
  51.3 0.7 broadcast_in_dim.7
  52.0 3.4 %all-to-all-start.2 = ((f32[8,32,256]{2,1,0:T(8,128)}), f32[8,32,256]{2,1,0:T(8,128)S(1)}, u32[]{:S(2)}, u32[]{:S(2)}) async-start(f32[8,32,256]{2,1,0:T(8,128)} %broadcast_in_dim.7), calls=%async_computation.2 | async-start | bytes 524288 | tf_op jit(solution)/shard_map/all_to_all | solution.py:114
  55.4 9.1 %all-to-all-done.2 = f32[8,32,256]{2,1,0:T(8,128)S(1)} async-done(((f32[8,32,256]{2,1,0:T(8,128)}), f32[8,32,256]{2,1,0:T(8,128)S(1)}, u32[]{:S(2)}, u32[]{:S(2)}) %all-to-all-start.2) | async-done | bytes 262176 | tf_op jit(solution)/shard_map/all_to_all | solution.py:114
  64.6 0.1 copy.17
  64.7 0.6 convolution_bitcast_fusion
  65.3 0.2 copy.18
  65.6 2.3 %fusion.7 = f32[4,256,256]{2,0,1:T(4,128)S(1)} fusion(f32[2,256,256]{2,0,1:T(2,128)S(1)} %copy.18, f32[2]{0:T(128)S(1)} %compare_convert_fusion, s32[2]{0:T(128)S(1)} %bitcast.51), kind=kOutput, calls=%fused_computation.20 | convolution fusion | flops 6291472 | bytes 1572880 | tf_op jit(solution)/shard_map/tc,tik->cik/dot_general | solution.py:160
  67.9 0.2 copy.19
  68.1 25.6 %all_to_all.31 = f32[32,32,256]{2,1,0:T(8,128)S(1)} all-to-all(f32[32,32,256]{2,1,0:T(8,128)S(1)} %bitcast.45), channel_id=1, replica_groups=mesh['row'=32,'col'=8] {'row'}, dimensions={0} | all-to-all | bytes 2097152 | tf_op jit(solution)/shard_map/all_to_all | solution.py:107
  93.7 0.1 reduce_sum.28.p_ref
  93.8 0.4 convolution_bitcast_fusion.1
  94.2 0.2 copy-done.1
  94.4 0.3 copy.20
  94.7 21.1 %all_to_all.32 = f32[256,1,256]{2,1,0:T(1,128)S(1)} all-to-all(f32[256,1,256]{2,1,0:T(1,128)S(1)} %copy.20), channel_id=1, replica_groups=mesh['row'=32,'col'=8] {'row','col'}, dimensions={0} | all-to-all | bytes 524288 | tf_op jit(solution)/shard_map/all_to_all | solution.py:107
  115.8 0.3 reduce_sum.29
  116.1 0.1 broadcast_in_dim.8
  116.3 21.1 %all_to_all.33 = f32[256,1,256]{2,1,0:T(1,128)S(1)} all-to-all(f32[256,1,256]{2,1,0:T(1,128)S(1)} %broadcast_in_dim.8), channel_id=1, replica_groups=mesh['row'=32,'col'=8] {'row','col'}, dimensions={0} | all-to-all | bytes 524288 | tf_op jit(solution)/shard_map/all_to_all | solution.py:114
  137.4 0.1 copy.21
  137.6 0.1 copy.22
  137.7 0.7 bitcast_select_fusion.g_ref
  138.4 16.4 %shard_map.76 = (f32[256,256]{1,0:T(8,128)}, f32[32,256]{1,0:T(8,128)}) custom-call(f32[256,256]{1,0:T(8,128)} %bitcast_select_fusion.g_ref, f32[32,256]{1,0:T(8,128)} %copy-done.1), custom_call_target="tpu_custom_call" | custom-call | tf_op jit(solution)/shard_map/pallas_call | solution.py:89
  154.8 0.7 copy.32
  (10 shorter events, 0.1 us)
Async XLA Ops:
  0.6 28.3 %copy-start = (f32[1,1,2,256,256]{4,3,2,1,0:T(8,128)S(1)}, f32[1,1,2,256,256]{4,3,2,1,0:T(8,128)}, u32[]{:S(2)}) copy-start(f32[1,1,2,256,256]{4,3,2,1,0:T(8,128)} %param.6) | copy-start | bytes 1572868
  2.6 25.8 %all-to-all-start = ((f32[32,32,256]{2,1,0:T(8,128)}), f32[32,32,256]{2,1,0:T(8,128)S(1)}, u32[]{:S(2)}, u32[]{:S(2)}) async-start(f32[32,32,256]{2,1,0:T(8,128)} %broadcast_in_dim.6), calls=%async_computation | async-start | bytes 2097152 | tf_op jit(solution)/shard_map/all_to_all | solution.py:114
  11.2 0.7 copy-start.2
  29.6 0.7 copy-start.3
  52.0 12.6 %all-to-all-start.2 = ((f32[8,32,256]{2,1,0:T(8,128)}), f32[8,32,256]{2,1,0:T(8,128)S(1)}, u32[]{:S(2)}, u32[]{:S(2)}) async-start(f32[8,32,256]{2,1,0:T(8,128)} %broadcast_in_dim.7), calls=%async_computation.2 | async-start | bytes 524288 | tf_op jit(solution)/shard_map/all_to_all | solution.py:114
  93.8 0.6 copy-start.1

commit v7 on v6

--- a/solution.py
+++ b/solution.py
@@ -114,11 +114,26 @@
     return lax.all_to_all(copies, axes, 0, 0, tiled=False).reshape(-1, x.shape[-1])
 
 
+def pair_gather(x):
+    other = lax.ppermute(x, "core", [(0, 1), (1, 0)])
+    first = lax.axis_index("core") == 0
+    return jnp.concatenate([jnp.where(first, x, other), jnp.where(first, other, x)], axis=0)
+
+
+def pair_scatter_sum(x):
+    chips = lax.axis_size("chip")
+    pairs = x.reshape(chips, 2, -1, x.shape[-1])
+    first = lax.axis_index("core") == 0
+    keep = jnp.where(first, pairs[:, 0], pairs[:, 1])
+    send = jnp.where(first, pairs[:, 1], pairs[:, 0])
+    return (keep + lax.ppermute(send, "core", [(0, 1), (1, 0)])).reshape(-1, x.shape[-1])
+
+
 def body(start_block, tile_values, tile_rows, tile_cols, tile_count):
     tile_size = tile_values.shape[-1]
     basis_width = start_block.shape[1]
     slot_total = tile_values.shape[2]
-    slab = exchange_gather(start_block, ("row",))
+    slab = exchange_gather(pair_gather(start_block), ("chip",))
     start_blocks = slab.reshape(-1, tile_size, basis_width)
     block_cols = start_blocks.shape[0]
     values = tile_values.reshape(slot_total, tile_size, tile_size)
@@ -165,30 +180,35 @@
         preferred_element_type=jnp.float32,
     )
     partial_flat = partial_projected.reshape(-1, basis_width)
-    projected = exchange_sum(partial_flat, ("row",))
+    projected = exchange_sum(pair_scatter_sum(partial_flat), ("chip",))
     share_rows = projected.shape[0]
-    matrix_order = share_rows * lax.axis_size("row") * lax.axis_size("col")
+    matrix_order = share_rows * group_size(("chip", "core", "col"))
     local_gram = jnp.dot(
         projected.T, projected, precision=lax.Precision.HIGHEST, preferred_element_type=jnp.float32
     )
-    both = ("row", "col")
+    both = ("chip", "core", "col")
     gram_matrix = exchange_gather(exchange_sum(local_gram, both), both) / matrix_order
     factor, new_basis = chol_solve(gram_matrix, projected)
     return (image_block, new_basis, factor)
 
 
 def solution(mesh):
+    devices = mesh.devices
+    split = jax.sharding.Mesh(
+        devices.reshape(devices.shape[0] // 2, 2, devices.shape[1]), ("chip", "core", "col")
+    )
+    rows = ("chip", "core")
     placed = (
-        P(("col", "row"), None),
-        P("row", "col", None, None, None),
-        P("row", "col", None),
-        P("row", "col", None),
-        P("row", "col"),
+        P(("col",) + rows, None),
+        P(rows, "col", None, None, None),
+        P(rows, "col", None),
+        P(rows, "col", None),
+        P(rows, "col"),
     )
     return jax.shard_map(
         body,
-        mesh=mesh,
+        mesh=split,
         in_specs=placed,
-        out_specs=(P("row", None), P(("col", "row"), None), P()),
+        out_specs=(P(rows, None), P(("col",) + rows, None), P()),
         check_vma=False,
     )

time: 156 us -> 152 us (0.974)
  blocking collectives: 86.8 us -> 76.5 us
  starting transfers between devices: 12 us -> 16.3 us
  waiting for transfers between devices: 25.6 us -> 27.6 us
    all_to_all x3, blocking collectives: 65.7 us -> 55.2 us  [exchange_sum(): lax.all_to_all(x.reshape(size, -1, x.shape[-1]), axes, 0, 0, tiled=False)]
    ppermute x0 -> x2, starting transfers between devices: none -> 7.86 us  [the longest x1 4.53 us: pair_scatter_sum(): lax.ppermute(send, 'core', [(0, 1), (1, 0)])]
    all_to_all x2, starting transfers between devices: 12 us -> 8.43 us  [exchange_gather(): lax.all_to_all(copies, axes, 0, 0, tiled=False).reshape(-1, x.shape[-1])]
    ppermute x0 -> x2, waiting for transfers between devices: none -> 2.61 us  [the longest x1 1.54 us: pair_scatter_sum(): lax.ppermute(send, 'core', [(0, 1), (1, 0)])]
  transfers between devices with their start and end apart: 2 -> 4, of which waited for: 2 -> 4; matrix products, arithmetic and copies ran while one was open for 0% -> 0% of each run, Pallas kernels for 0% -> 0%
where the time goes in v7:
time: 152 us
  blocking collectives  76.5 us (50%)
  waiting for transfers between devices  27.6 us (18%)
  Pallas kernels  16.4 us (11%)
  starting transfers between devices  16.3 us (11%)
  matrix products  6 us (4%)
  local copies, waits for them, and re-layouts  5.17 us (3%)
  other arithmetic  2.06 us (1%)
    all_to_all x3, blocking collectives, exchange_sum(): lax.all_to_all(x.reshape(size, -1, x.shape[-1]), axes, 0, 0, tiled=False)  55.2 us
    all_to_all x2, waiting for transfers between devices, exchange_gather(): lax.all_to_all(copies, axes, 0, 0, tiled=False).reshape(-1, x.shape[-1])  25 us
    all_to_all x1, blocking collectives, exchange_gather(): lax.all_to_all(copies, axes, 0, 0, tiled=False).reshape(-1, x.shape[-1])  21.3 us
    pallas_call x1, Pallas kernels, chol_solve(): pl.pallas_call(chol_solve_kernel, out_shape=(jax.ShapeDtypeStruct((n, n),...  16.4 us
    all_to_all x2, starting transfers between devices, exchange_gather(): lax.all_to_all(copies, axes, 0, 0, tiled=False).reshape(-1, x.shape[-1])  8.43 us
    ppermute x1, starting transfers between devices, pair_scatter_sum(): lax.ppermute(send, 'core', [(0, 1), (1, 0)])  4.53 us
    ppermute x1, starting transfers between devices, pair_gather(): other = lax.ppermute(x, 'core', [(0, 1), (1, 0)])  3.33 us
  transfers between devices with their start and end apart: 4, of which 4 were waited for; matrix products, arithmetic and copies ran while one was open for 0% of the time, Pallas kernels for 0%

profile of v7, /device:TPU:1, one launch (start us, length us, event | category | flops | bytes accessed | tf_op | source)
XLA Modules:
  0.0 151.5 jit_solution(9168203006357618587)
XLA Ops:
  0.6 3.3 %collective-permute-start = (f32[32,256]{1,0:T(8,128)}, f32[32,256]{1,0:T(8,128)S(1)}, u32[]{:S(2)}, u32[]{:S(2)}) collective-permute-start(f32[32,256]{1,0:T(8,128)} %param.5), channel_id=1, source_target_pairs={{0,8},{8,0},{1,9},{9,1},{2,10},{10,2},{3,11},{11,3},{4,12},{12,4},... | collective-permute-start | bytes 98312 | tf_op jit(solution)/shard_map/ppermute | solution.py:118
  4.0 1.1 collective-permute-done
  5.0 0.8 broadcast_select_fusion.1
  5.8 1.1 broadcast_in_dim.6
  6.9 5.0 %all-to-all-start = ((f32[16,64,256]{2,1,0:T(8,128)}), f32[16,64,256]{2,1,0:T(8,128)S(1)}, u32[]{:S(2)}, u32[]{:S(2)}) async-start(f32[16,64,256]{2,1,0:T(8,128)} %broadcast_in_dim.6), calls=%async_computation | async-start | bytes 2097152 | tf_op jit(solution)/shard_map/all_to_all | solution.py:114
  12.6 15.7 %all-to-all-done = f32[16,64,256]{2,1,0:T(8,128)S(1)} async-done(((f32[16,64,256]{2,1,0:T(8,128)}), f32[16,64,256]{2,1,0:T(8,128)S(1)}, u32[]{:S(2)}, u32[]{:S(2)}) %all-to-all-start) | async-done | bytes 1048608 | tf_op jit(solution)/shard_map/all_to_all | solution.py:114
  28.3 0.6 gather_fusion
  28.9 0.7 fusion.3
  29.5 0.6 copy-done.3
  30.2 2.0 %fusion.5 = f32[1,8,32,256]{3,0,2,1:T(1,128)S(1)} fusion(f32[8,32,256,2]{2,1,0,3:T(8,128)S(1)} %bitcast.69, s32[1,1,2]{2,1,0:T(1,128)S(1)} %copy-done.3, s32[]{:T(128)} %bitcast.61), kind=kOutput, calls=%fused_computation.10 | convolution fusion | flops 1572872 | bytes 786444 | tf_op jit(solution)/shard_map/tb,tik->bik/dot_general | solution.py:155
  32.2 17.4 %all_to_all.30 = f32[8,32,256]{2,1,0:T(8,128)S(1)} all-to-all(f32[8,32,256]{2,1,0:T(8,128)S(1)} %bitcast.68), channel_id=1, replica_groups=mesh['chip'=16,'core'=2,'col'=8] {'col'}, dimensions={0} | all-to-all | bytes 524288 | tf_op jit(solution)/shard_map/all_to_all | solution.py:107
  49.7 0.7 broadcast_in_dim.7
  50.4 3.4 %all-to-all-start.2 = ((f32[8,32,256]{2,1,0:T(8,128)}), f32[8,32,256]{2,1,0:T(8,128)S(1)}, u32[]{:S(2)}, u32[]{:S(2)}) async-start(f32[8,32,256]{2,1,0:T(8,128)} %broadcast_in_dim.7), calls=%async_computation.2 | async-start | bytes 524288 | tf_op jit(solution)/shard_map/all_to_all | solution.py:114
  53.8 9.3 %all-to-all-done.2 = f32[8,32,256]{2,1,0:T(8,128)S(1)} async-done(((f32[8,32,256]{2,1,0:T(8,128)}), f32[8,32,256]{2,1,0:T(8,128)S(1)}, u32[]{:S(2)}, u32[]{:S(2)}) %all-to-all-start.2) | async-done | bytes 262176 | tf_op jit(solution)/shard_map/all_to_all | solution.py:114
  63.3 0.6 convolution_bitcast_fusion
  63.9 0.2 copy.29
  64.2 2.3 %fusion.9 = f32[4,256,256]{2,0,1:T(4,128)S(1)} fusion(f32[2,256,256]{2,0,1:T(2,128)S(1)} %copy.29, f32[2]{0:T(128)S(1)} %compare_convert_fusion, s32[2]{0:T(128)S(1)} %bitcast.70), kind=kOutput, calls=%fused_computation.27 | convolution fusion | flops 6291472 | bytes 1572880 | tf_op jit(solution)/shard_map/tc,tik->cik/dot_general | solution.py:175
  66.5 0.2 copy.30
  66.8 4.5 %collective-permute-start.1 = (f32[16,32,256]{2,1,0:T(8,128)S(1)}, f32[16,32,256]{2,1,0:T(8,128)S(1)}, u32[]{:S(2)}, u32[]{:S(2)}) collective-permute-start(f32[16,32,256]{2,1,0:T(8,128)S(1)} %select_bitcast_fusion), channel_id=1, source_target_pairs={{0,8},{8,0},{1,9},{9,1},{2,10},{10,2},{3,11},{11,3},{4,12},{12,4},... | collective-permute-start | bytes 1572872 | tf_op jit(solution)/shard_map/ppermute | solution.py:129
  71.3 1.5 %collective-permute-done.1 = f32[16,32,256]{2,1,0:T(8,128)S(1)} collective-permute-done((f32[16,32,256]{2,1,0:T(8,128)S(1)}, f32[16,32,256]{2,1,0:T(8,128)S(1)}, u32[]{:S(2)}, u32[]{:S(2)}) %collective-permute-start.1) | collective-permute-done | bytes 524320 | tf_op jit(solution)/shard_map/ppermute | solution.py:129
  73.0 15.2 %all_to_all.31 = f32[16,32,256]{2,1,0:T(8,128)S(1)} all-to-all(f32[16,32,256]{2,1,0:T(8,128)S(1)} %fusion.1), channel_id=1, replica_groups=mesh['chip'=16,'core'=2,'col'=8] {'chip'}, dimensions={0} | all-to-all | bytes 1048576 | tf_op jit(solution)/shard_map/all_to_all | solution.py:107
  88.3 0.4 convolution_bitcast_fusion.1
  88.7 0.2 copy-done.1
  88.8 0.3 copy.35
  89.1 22.5 %all_to_all.32 = f32[256,1,256]{2,1,0:T(1,128)S(1)} all-to-all(f32[256,1,256]{2,1,0:T(1,128)S(1)} %copy.35), channel_id=1, replica_groups=mesh['chip'=16,'core'=2,'col'=8] {'chip','core','col'}, dimensions={0} | all-to-all | bytes 524288 | tf_op jit(solution)/shard_map/all_to_all | solution.py:107
  111.6 0.3 reduce_sum.29
  111.9 0.1 broadcast_in_dim.8
  112.1 21.3 %all_to_all.33 = f32[256,1,256]{2,1,0:T(1,128)S(1)} all-to-all(f32[256,1,256]{2,1,0:T(1,128)S(1)} %broadcast_in_dim.8), channel_id=1, replica_groups=mesh['chip'=16,'core'=2,'col'=8] {'chip','core','col'}, dimensions={0} | all-to-all | bytes 524288 | tf_op jit(solution)/shard_map/all_to_all | solution.py:114
  133.4 0.1 copy.36
  133.7 0.7 bitcast_select_fusion.1.g_ref
  134.4 16.4 %shard_map.76 = (f32[256,256]{1,0:T(8,128)}, f32[32,256]{1,0:T(8,128)}) custom-call(f32[256,256]{1,0:T(8,128)} %bitcast_select_fusion.1.g_ref, f32[32,256]{1,0:T(8,128)} %copy-done.1), custom_call_target="tpu_custom_call" | custom-call | tf_op jit(solution)/shard_map/pallas_call | solution.py:89
  150.8 0.7 copy.48
  (18 shorter events, 0.6 us)
Async XLA Ops:
  0.6 28.2 %copy-start = (f32[1,1,2,256,256]{4,3,2,1,0:T(8,128)S(1)}, f32[1,1,2,256,256]{4,3,2,1,0:T(8,128)}, u32[]{:S(2)}) copy-start(f32[1,1,2,256,256]{4,3,2,1,0:T(8,128)} %param.6) | copy-start | bytes 1572868
  0.6 4.4 %collective-permute-start = (f32[32,256]{1,0:T(8,128)}, f32[32,256]{1,0:T(8,128)S(1)}, u32[]{:S(2)}, u32[]{:S(2)}) collective-permute-start(f32[32,256]{1,0:T(8,128)} %param.5), channel_id=1, source_target_pairs={{0,8},{8,0},{1,9},{9,1},{2,10},{10,2},{3,11},{11,3},{4,12},{12,4},... | collective-permute-start | bytes 98312 | tf_op jit(solution)/shard_map/ppermute | solution.py:118
  6.9 21.4 %all-to-all-start = ((f32[16,64,256]{2,1,0:T(8,128)}), f32[16,64,256]{2,1,0:T(8,128)S(1)}, u32[]{:S(2)}, u32[]{:S(2)}) async-start(f32[16,64,256]{2,1,0:T(8,128)} %broadcast_in_dim.6), calls=%async_computation | async-start | bytes 2097152 | tf_op jit(solution)/shard_map/all_to_all | solution.py:114
  11.9 0.7 copy-start.2
  29.5 0.7 copy-start.3
  50.4 12.8 %all-to-all-start.2 = ((f32[8,32,256]{2,1,0:T(8,128)}), f32[8,32,256]{2,1,0:T(8,128)S(1)}, u32[]{:S(2)}, u32[]{:S(2)}) async-start(f32[8,32,256]{2,1,0:T(8,128)} %broadcast_in_dim.7), calls=%async_computation.2 | async-start | bytes 524288 | tf_op jit(solution)/shard_map/all_to_all | solution.py:114
  66.8 6.1 %collective-permute-start.1 = (f32[16,32,256]{2,1,0:T(8,128)S(1)}, f32[16,32,256]{2,1,0:T(8,128)S(1)}, u32[]{:S(2)}, u32[]{:S(2)}) collective-permute-start(f32[16,32,256]{2,1,0:T(8,128)S(1)} %select_bitcast_fusion), channel_id=1, source_target_pairs={{0,8},{8,0},{1,9},{9,1},{2,10},{10,2},{3,11},{11,3},{4,12},{12,4},... | collective-permute-start | bytes 1572872 | tf_op jit(solution)/shard_map/ppermute | solution.py:129
  88.2 0.6 copy-start.1

commit v8 on v7

--- a/solution.py
+++ b/solution.py
@@ -117,7 +117,9 @@
 def pair_gather(x):
     other = lax.ppermute(x, "core", [(0, 1), (1, 0)])
     first = lax.axis_index("core") == 0
-    return jnp.concatenate([jnp.where(first, x, other), jnp.where(first, other, x)], axis=0)
+    low = jnp.where(first, x, other).reshape(lax.axis_size("chip"), -1, x.shape[-1])
+    high = jnp.where(first, other, x).reshape(lax.axis_size("chip"), -1, x.shape[-1])
+    return jnp.stack([low, high], axis=1).reshape(-1, x.shape[-1])
 
 
 def pair_scatter_sum(x):
@@ -133,7 +135,7 @@
     tile_size = tile_values.shape[-1]
     basis_width = start_block.shape[1]
     slot_total = tile_values.shape[2]
-    slab = exchange_gather(pair_gather(start_block), ("chip",))
+    slab = pair_gather(exchange_gather(start_block, ("chip",)))
     start_blocks = slab.reshape(-1, tile_size, basis_width)
     block_cols = start_blocks.shape[0]
     values = tile_values.reshape(slot_total, tile_size, tile_size)
@@ -186,8 +188,9 @@
     local_gram = jnp.dot(
         projected.T, projected, precision=lax.Precision.HIGHEST, preferred_element_type=jnp.float32
     )
-    both = ("chip", "core", "col")
-    gram_matrix = exchange_gather(exchange_sum(local_gram, both), both) / matrix_order
+    spread = ("chip", "col")
+    gram_rows = exchange_gather(exchange_sum(pair_scatter_sum(local_gram), spread), spread)
+    gram_matrix = pair_gather(gram_rows) / matrix_order
     factor, new_basis = chol_solve(gram_matrix, projected)
     return (image_block, new_basis, factor)
 

time: 152 us -> 142 us (0.934)
  waiting for transfers between devices: 27.6 us -> 13.3 us
  blocking collectives: 76.5 us -> 85.1 us
  starting transfers between devices: 16.3 us -> 12.6 us
    all_to_all x2 -> x1, waiting for transfers between devices: 25 us -> 9.56 us  [exchange_gather(): lax.all_to_all(copies, axes, 0, 0, tiled=False).reshape(-1, x.shape[-1])]
    all_to_all x1 -> x2, blocking collectives: 21.3 us -> 35.3 us  [exchange_gather(): lax.all_to_all(copies, axes, 0, 0, tiled=False).reshape(-1, x.shape[-1])]
    all_to_all x3, blocking collectives: 55.2 us -> 49.8 us  [exchange_sum(): lax.all_to_all(x.reshape(size, -1, x.shape[-1]), axes, 0, 0, tiled=False)]
    all_to_all x2 -> x1, starting transfers between devices: 8.43 us -> 3.41 us  [exchange_gather(): lax.all_to_all(copies, axes, 0, 0, tiled=False).reshape(-1, x.shape[-1])]
    ppermute x1 -> x2, starting transfers between devices: 3.33 us -> 4.09 us  [pair_gather(): other = lax.ppermute(x, 'core', [(0, 1), (1, 0)])]
    ppermute x1 -> x2, starting transfers between devices: 4.53 us -> 5.13 us  [pair_scatter_sum(): lax.ppermute(send, 'core', [(0, 1), (1, 0)])]
  transfers between devices with their start and end apart: 4 -> 5, of which waited for: 4 -> 5; matrix products, arithmetic and copies ran while one was open for 0% -> 0% of each run, Pallas kernels for 0% -> 0%
where the time goes in v8:
time: 142 us
  blocking collectives  85.1 us (60%)
  Pallas kernels  16.4 us (12%)
  waiting for transfers between devices  13.3 us (9%)
  starting transfers between devices  12.6 us (9%)
  matrix products  5.93 us (4%)
  local copies, waits for them, and re-layouts  5.72 us (4%)
  between operations  1.52 us (1%)
    all_to_all x3, blocking collectives, exchange_sum(): lax.all_to_all(x.reshape(size, -1, x.shape[-1]), axes, 0, 0, tiled=False)  49.8 us
    all_to_all x2, blocking collectives, exchange_gather(): lax.all_to_all(copies, axes, 0, 0, tiled=False).reshape(-1, x.shape[-1])  35.3 us
    pallas_call x1, Pallas kernels, chol_solve(): pl.pallas_call(chol_solve_kernel, out_shape=(jax.ShapeDtypeStruct((n, n),...  16.4 us
    all_to_all x1, waiting for transfers between devices, exchange_gather(): lax.all_to_all(copies, axes, 0, 0, tiled=False).reshape(-1, x.shape[-1])  9.56 us
    ppermute x2, starting transfers between devices, pair_scatter_sum(): lax.ppermute(send, 'core', [(0, 1), (1, 0)])  5.13 us
    ppermute x2, starting transfers between devices, pair_gather(): other = lax.ppermute(x, 'core', [(0, 1), (1, 0)])  4.09 us
    all_to_all x1, starting transfers between devices, exchange_gather(): lax.all_to_all(copies, axes, 0, 0, tiled=False).reshape(-1, x.shape[-1])  3.41 us
  transfers between devices with their start and end apart: 5, of which 5 were waited for; matrix products, arithmetic and copies ran while one was open for 0% of the time, Pallas kernels for 0%

profile of v8, /device:TPU:1, one launch (start us, length us, event | category | flops | bytes accessed | tf_op | source)
XLA Modules:
  0.0 142.0 jit_solution(9932395616936349892)
XLA Ops:
  0.6 0.9 broadcast_in_dim.6
  1.5 17.9 %all_to_all.30 = f32[16,32,256]{2,1,0:T(8,128)S(1)} all-to-all(f32[16,32,256]{2,1,0:T(8,128)S(1)} %broadcast_in_dim.6), channel_id=1, replica_groups=mesh['chip'=16,'core'=2,'col'=8] {'chip'}, dimensions={0} | all-to-all | bytes 1048576 | tf_op jit(solution)/shard_map/all_to_all | solution.py:114
  19.4 2.0 %collective-permute-start = (f32[512,256]{1,0:T(8,128)S(1)}, f32[512,256]{1,0:T(8,128)S(1)}, u32[]{:S(2)}, u32[]{:S(2)}) collective-permute-start(f32[512,256]{1,0:T(8,128)S(1)} %bitcast.112), channel_id=1, source_target_pairs={{0,8},{8,0},{1,9},{9,1},{2,10},{10,2},{3,11},{11,3},{4,12},{12,4},... | collective-permute-start | bytes 1572872 | tf_op jit(solution)/shard_map/ppermute | solution.py:118
  22.1 0.6 copy-done.2
  22.7 0.2 collective-permute-done
  23.1 0.6 gather_fusion
  23.7 0.7 fusion.3
  24.4 0.6 copy-done.3
  25.0 2.0 %fusion.5 = f32[1,8,32,256]{3,0,2,1:T(1,128)S(1)} fusion(f32[8,32,256,2]{2,1,0,3:T(8,128)S(1)} %bitcast.116, s32[1,1,2]{2,1,0:T(1,128)S(1)} %copy-done.3, s32[]{:T(128)} %bitcast.104), kind=kOutput, calls=%fused_computation.10 | convolution fusion | flops 1572872 | bytes 786444 | tf_op jit(solution)/shard_map/tb,tik->bik/dot_general | solution.py:157
  27.1 19.1 %all_to_all.31 = f32[8,32,256]{2,1,0:T(8,128)S(1)} all-to-all(f32[8,32,256]{2,1,0:T(8,128)S(1)} %bitcast.115), channel_id=1, replica_groups=mesh['chip'=16,'core'=2,'col'=8] {'col'}, dimensions={0} | all-to-all | bytes 524288 | tf_op jit(solution)/shard_map/all_to_all | solution.py:107
  46.1 0.7 broadcast_in_dim.7
  46.9 3.4 %all-to-all-start.2 = ((f32[8,32,256]{2,1,0:T(8,128)}), f32[8,32,256]{2,1,0:T(8,128)S(1)}, u32[]{:S(2)}, u32[]{:S(2)}) async-start(f32[8,32,256]{2,1,0:T(8,128)} %broadcast_in_dim.7), calls=%async_computation.2 | async-start | bytes 524288 | tf_op jit(solution)/shard_map/all_to_all | solution.py:114
  50.3 9.6 %all-to-all-done.2 = f32[8,32,256]{2,1,0:T(8,128)S(1)} async-done(((f32[8,32,256]{2,1,0:T(8,128)}), f32[8,32,256]{2,1,0:T(8,128)S(1)}, u32[]{:S(2)}, u32[]{:S(2)}) %all-to-all-start.2) | async-done | bytes 262176 | tf_op jit(solution)/shard_map/all_to_all | solution.py:114
  60.0 0.6 convolution_bitcast_fusion
  60.6 0.2 copy.45
  60.9 2.3 %fusion.14 = f32[4,256,256]{2,0,1:T(4,128)S(1)} fusion(f32[2,256,256]{2,0,1:T(2,128)S(1)} %copy.45, f32[2]{0:T(128)S(1)} %compare_convert_fusion, s32[2]{0:T(128)S(1)} %bitcast.120), kind=kOutput, calls=%fused_computation.36 | convolution fusion | flops 6291472 | bytes 1572880 | tf_op jit(solution)/shard_map/tc,tik->cik/dot_general | solution.py:177
  63.2 0.2 copy.46
  63.5 3.3 %collective-permute-start.1 = (f32[16,32,256]{2,1,0:T(8,128)S(1)}, f32[16,32,256]{2,1,0:T(8,128)S(1)}, u32[]{:S(2)}, u32[]{:S(2)}) collective-permute-start(f32[16,32,256]{2,1,0:T(8,128)S(1)} %select_bitcast_fusion), channel_id=1, source_target_pairs={{0,8},{8,0},{1,9},{9,1},{2,10},{10,2},{3,11},{11,3},{4,12},{12,4},... | collective-permute-start | bytes 1572872 | tf_op jit(solution)/shard_map/ppermute | solution.py:131
  66.7 1.5 %collective-permute-done.1 = f32[16,32,256]{2,1,0:T(8,128)S(1)} collective-permute-done((f32[16,32,256]{2,1,0:T(8,128)S(1)}, f32[16,32,256]{2,1,0:T(8,128)S(1)}, u32[]{:S(2)}, u32[]{:S(2)}) %collective-permute-start.1) | collective-permute-done | bytes 524320 | tf_op jit(solution)/shard_map/ppermute | solution.py:131
  68.4 13.4 %all_to_all.32 = f32[16,32,256]{2,1,0:T(8,128)S(1)} all-to-all(f32[16,32,256]{2,1,0:T(8,128)S(1)} %fusion.1), channel_id=1, replica_groups=mesh['chip'=16,'core'=2,'col'=8] {'chip'}, dimensions={0} | all-to-all | bytes 1048576 | tf_op jit(solution)/shard_map/all_to_all | solution.py:107
  81.9 0.5 copy-done.1
  82.4 0.3 fusion.11
  82.8 1.9 %collective-permute-start.2 = (f32[16,8,256]{2,1,0:T(8,128)S(1)}, f32[16,8,256]{2,1,0:T(8,128)S(1)}, u32[]{:S(2)}, u32[]{:S(2)}) collective-permute-start(f32[16,8,256]{2,1,0:T(8,128)S(1)} %select_bitcast_fusion.3), channel_id=1, source_target_pairs={{0,8},{8,0},{1,9},{9,1},{2,10},{10,2},{3,11},{11,3},{4,12},{12,4},... | collective-permute-start | bytes 393224 | tf_op jit(solution)/shard_map/ppermute | solution.py:131
  84.7 1.0 collective-permute-done.2
  85.8 17.3 %all_to_all.33 = f32[128,1,256]{2,1,0:T(1,128)S(1)} all-to-all(f32[128,1,256]{2,1,0:T(1,128)S(1)} %copy.56), channel_id=1, replica_groups=mesh['chip'=16,'core'=2,'col'=8] {'chip','col'}, dimensions={0} | all-to-all | bytes 262144 | tf_op jit(solution)/shard_map/all_to_all | solution.py:107
  103.2 0.2 reduce_sum.29
  103.4 17.4 %all_to_all.34 = f32[128,1,256]{2,1,0:T(1,128)S(1)} all-to-all(f32[128,1,256]{2,1,0:T(1,128)S(1)} %broadcast_in_dim.8), channel_id=1, replica_groups=mesh['chip'=16,'core'=2,'col'=8] {'chip','col'}, dimensions={0} | all-to-all | bytes 262144 | tf_op jit(solution)/shard_map/all_to_all | solution.py:114
  120.8 2.1 %collective-permute-start.3 = (f32[128,256]{1,0:T(8,128)S(1)}, f32[128,256]{1,0:T(8,128)S(1)}, u32[]{:S(2)}, u32[]{:S(2)}) collective-permute-start(f32[128,256]{1,0:T(8,128)S(1)} %bitcast.119), channel_id=1, source_target_pairs={{0,8},{8,0},{1,9},{9,1},{2,10},{10,2},{3,11},{11,3},{4,12},{12,4},... | collective-permute-start | bytes 393224 | tf_op jit(solution)/shard_map/ppermute | solution.py:118
  122.9 1.0 collective-permute-done.3
  124.1 0.7 bitcast_select_fusion.1.g_ref
  124.9 16.4 %shard_map.76 = (f32[256,256]{1,0:T(8,128)}, f32[32,256]{1,0:T(8,128)}) custom-call(f32[256,256]{1,0:T(8,128)} %bitcast_select_fusion.1.g_ref, f32[32,256]{1,0:T(8,128)} %copy-done.1), custom_call_target="tpu_custom_call" | custom-call | tf_op jit(solution)/shard_map/pallas_call | solution.py:89
  141.3 0.7 copy.78
  (26 shorter events, 1.1 us)
Async XLA Ops:
  0.6 23.1 %copy-start = (f32[1,1,2,256,256]{4,3,2,1,0:T(8,128)S(1)}, f32[1,1,2,256,256]{4,3,2,1,0:T(8,128)}, u32[]{:S(2)}) copy-start(f32[1,1,2,256,256]{4,3,2,1,0:T(8,128)} %param.6) | copy-start | bytes 1572868
  19.4 3.5 %collective-permute-start = (f32[512,256]{1,0:T(8,128)S(1)}, f32[512,256]{1,0:T(8,128)S(1)}, u32[]{:S(2)}, u32[]{:S(2)}) collective-permute-start(f32[512,256]{1,0:T(8,128)S(1)} %bitcast.112), channel_id=1, source_target_pairs={{0,8},{8,0},{1,9},{9,1},{2,10},{10,2},{3,11},{11,3},{4,12},{12,4},... | collective-permute-start | bytes 1572872 | tf_op jit(solution)/shard_map/ppermute | solution.py:118
  22.0 0.7 copy-start.2
  24.4 0.7 copy-start.3
  46.9 13.0 %all-to-all-start.2 = ((f32[8,32,256]{2,1,0:T(8,128)}), f32[8,32,256]{2,1,0:T(8,128)S(1)}, u32[]{:S(2)}, u32[]{:S(2)}) async-start(f32[8,32,256]{2,1,0:T(8,128)} %broadcast_in_dim.7), calls=%async_computation.2 | async-start | bytes 524288 | tf_op jit(solution)/shard_map/all_to_all | solution.py:114
  63.5 4.8 %collective-permute-start.1 = (f32[16,32,256]{2,1,0:T(8,128)S(1)}, f32[16,32,256]{2,1,0:T(8,128)S(1)}, u32[]{:S(2)}, u32[]{:S(2)}) collective-permute-start(f32[16,32,256]{2,1,0:T(8,128)S(1)} %select_bitcast_fusion), channel_id=1, source_target_pairs={{0,8},{8,0},{1,9},{9,1},{2,10},{10,2},{3,11},{11,3},{4,12},{12,4},... | collective-permute-start | bytes 1572872 | tf_op jit(solution)/shard_map/ppermute | solution.py:131
  81.8 0.6 copy-start.1
  82.8 2.8 %collective-permute-start.2 = (f32[16,8,256]{2,1,0:T(8,128)S(1)}, f32[16,8,256]{2,1,0:T(8,128)S(1)}, u32[]{:S(2)}, u32[]{:S(2)}) collective-permute-start(f32[16,8,256]{2,1,0:T(8,128)S(1)} %select_bitcast_fusion.3), channel_id=1, source_target_pairs={{0,8},{8,0},{1,9},{9,1},{2,10},{10,2},{3,11},{11,3},{4,12},{12,4},... | collective-permute-start | bytes 393224 | tf_op jit(solution)/shard_map/ppermute | solution.py:131
  120.8 3.1 %collective-permute-start.3 = (f32[128,256]{1,0:T(8,128)S(1)}, f32[128,256]{1,0:T(8,128)S(1)}, u32[]{:S(2)}, u32[]{:S(2)}) collective-permute-start(f32[128,256]{1,0:T(8,128)S(1)} %bitcast.119), channel_id=1, source_target_pairs={{0,8},{8,0},{1,9},{9,1},{2,10},{10,2},{3,11},{11,3},{4,12},{12,4},... | collective-permute-start | bytes 393224 | tf_op jit(solution)/shard_map/ppermute | solution.py:118

commit v9 on v8

--- a/solution.py
+++ b/solution.py
@@ -143,10 +143,8 @@
     col_ids = tile_cols.reshape(slot_total)
     live_count = tile_count.reshape(())
     block_rows = BR
-    live_mask = (jnp.arange(slot_total, dtype=jnp.int32) < live_count).astype(jnp.float32)
-    row_onehot = (row_ids[:, None] == jnp.arange(block_rows, dtype=jnp.int32)[None, :]).astype(
-        jnp.float32
-    ) * live_mask[:, None]
+    live = jnp.arange(slot_total, dtype=jnp.int32) < live_count
+    row_hit = (row_ids[:, None] == jnp.arange(block_rows, dtype=jnp.int32)[None, :]) & live[:, None]
     products = jnp.einsum(
         "tij,tjk->tik",
         values,
@@ -154,19 +152,13 @@
         precision=lax.Precision.HIGHEST,
         preferred_element_type=jnp.float32,
     )
-    partial_image = jnp.einsum(
-        "tb,tik->bik",
-        row_onehot,
-        products,
-        precision=lax.Precision.HIGHEST,
-        preferred_element_type=jnp.float32,
+    partial_image = jnp.sum(
+        jnp.where(row_hit[:, :, None, None], products[:, None], 0.0), axis=0
     )
     partial_rows = partial_image.reshape(-1, basis_width)
     image_block = exchange_gather(exchange_sum(partial_rows, ("col",)), ("col",))
     image_blocks = image_block.reshape(block_rows, tile_size, basis_width)
-    col_onehot = (col_ids[:, None] == jnp.arange(block_cols, dtype=jnp.int32)[None, :]).astype(
-        jnp.float32
-    ) * live_mask[:, None]
+    col_hit = (col_ids[:, None] == jnp.arange(block_cols, dtype=jnp.int32)[None, :]) & live[:, None]
     back_products = jnp.einsum(
         "tji,tjk->tik",
         values,
@@ -174,12 +166,8 @@
         precision=lax.Precision.HIGHEST,
         preferred_element_type=jnp.float32,
     )
-    partial_projected = jnp.einsum(
-        "tc,tik->cik",
-        col_onehot,
-        back_products,
-        precision=lax.Precision.HIGHEST,
-        preferred_element_type=jnp.float32,
+    partial_projected = jnp.sum(
+        jnp.where(col_hit[:, :, None, None], back_products[:, None], 0.0), axis=0
     )
     partial_flat = partial_projected.reshape(-1, basis_width)
     projected = exchange_sum(pair_scatter_sum(partial_flat), ("chip",))

time: 142 us -> 138 us (0.972)
  blocking collectives: 85.1 us -> 67 us
  waiting for transfers between devices: 13.3 us -> 24.2 us
  starting transfers between devices: 12.6 us -> 20.3 us
  matrix products: 5.93 us -> 1.98 us
    all_to_all x2 -> x1, blocking collectives: 35.3 us -> 17.2 us  [exchange_gather(): lax.all_to_all(copies, axes, 0, 0, tiled=False).reshape(-1, x.shape[-1])]
    all_to_all x1 -> x2, waiting for transfers between devices: 9.56 us -> 19.2 us  [exchange_gather(): lax.all_to_all(copies, axes, 0, 0, tiled=False).reshape(-1, x.shape[-1])]
    all_to_all x1 -> x2, starting transfers between devices: 3.41 us -> 11 us  [exchange_gather(): lax.all_to_all(copies, axes, 0, 0, tiled=False).reshape(-1, x.shape[-1])]
    dot_general x2 -> x0, matrix products: 4.33 us -> none  [the longest x1 2.32 us: body(): jnp.einsum('tc,tik->cik', col_onehot, back_products, precision=lax.Precis...]
    unnamed x10, local copies, waits for them, and re-layouts: 2.52 us -> 0.73 us
  transfers between devices with their start and end apart: 5 -> 6, of which waited for: 5 -> 6; matrix products, arithmetic and copies ran while one was open for 0% -> 0% of each run, Pallas kernels for 0% -> 0%
where the time goes in v9:
time: 138 us
  blocking collectives  67 us (49%)
  waiting for transfers between devices  24.2 us (18%)
  starting transfers between devices  20.3 us (15%)
  Pallas kernels  16.4 us (12%)
  local copies, waits for them, and re-layouts  4.59 us (3%)
  matrix products  1.98 us (1%)
  other arithmetic  1.67 us (1%)
  between operations  1.51 us (1%)
    all_to_all x3, blocking collectives, exchange_sum(): lax.all_to_all(x.reshape(size, -1, x.shape[-1]), axes, 0, 0, tiled=False)  49.7 us
    all_to_all x2, waiting for transfers between devices, exchange_gather(): lax.all_to_all(copies, axes, 0, 0, tiled=False).reshape(-1, x.shape[-1])  19.2 us
    all_to_all x1, blocking collectives, exchange_gather(): lax.all_to_all(copies, axes, 0, 0, tiled=False).reshape(-1, x.shape[-1])  17.2 us
    pallas_call x1, Pallas kernels, chol_solve(): pl.pallas_call(chol_solve_kernel, out_shape=(jax.ShapeDtypeStruct((n, n),...  16.4 us
    all_to_all x2, starting transfers between devices, exchange_gather(): lax.all_to_all(copies, axes, 0, 0, tiled=False).reshape(-1, x.shape[-1])  11 us
    ppermute x2, starting transfers between devices, pair_scatter_sum(): lax.ppermute(send, 'core', [(0, 1), (1, 0)])  5.26 us
    ppermute x2, starting transfers between devices, pair_gather(): other = lax.ppermute(x, 'core', [(0, 1), (1, 0)])  4.09 us
  transfers between devices with their start and end apart: 6, of which 6 were waited for; matrix products, arithmetic and copies ran while one was open for 0% of the time, Pallas kernels for 0%

profile of v9, /device:TPU:1, one launch (start us, length us, event | category | flops | bytes accessed | tf_op | source)
XLA Modules:
  0.0 137.7 jit_solution(8051803240090812402)
XLA Ops:
  0.7 1.6 %broadcast_in_dim.39 = f32[16,32,256]{2,1,0:T(8,128)} broadcast(f32[32,256]{1,0:T(8,128)} %param.5), dimensions={1,2} | broadcast | bytes 557056 | tf_op jit(solution)/shard_map/broadcast_in_dim | solution.py:113
  2.3 7.6 %all-to-all-start = ((f32[16,32,256]{2,1,0:T(8,128)}), f32[16,32,256]{2,1,0:T(8,128)S(1)}, u32[]{:S(2)}, u32[]{:S(2)}) async-start(f32[16,32,256]{2,1,0:T(8,128)} %broadcast_in_dim.39), calls=%async_computation | async-start | bytes 1048576 | tf_op jit(solution)/shard_map/all_to_all | solution.py:114
  10.6 9.9 %all-to-all-done = f32[16,32,256]{2,1,0:T(8,128)S(1)} async-done(((f32[16,32,256]{2,1,0:T(8,128)}), f32[16,32,256]{2,1,0:T(8,128)S(1)}, u32[]{:S(2)}, u32[]{:S(2)}) %all-to-all-start) | async-done | bytes 524320 | tf_op jit(solution)/shard_map/all_to_all | solution.py:114
  20.4 2.0 %collective-permute-start = (f32[512,256]{1,0:T(8,128)S(1)}, f32[512,256]{1,0:T(8,128)S(1)}, u32[]{:S(2)}, u32[]{:S(2)}) collective-permute-start(f32[512,256]{1,0:T(8,128)S(1)} %bitcast.98), channel_id=1, source_target_pairs={{0,8},{8,0},{1,9},{9,1},{2,10},{10,2},{3,11},{11,3},{4,12},{12,4},... | collective-permute-start | bytes 1572872 | tf_op jit(solution)/shard_map/ppermute | solution.py:118
  22.4 1.5 %collective-permute-done = f32[512,256]{1,0:T(8,128)S(1)} collective-permute-done((f32[512,256]{1,0:T(8,128)S(1)}, f32[512,256]{1,0:T(8,128)S(1)}, u32[]{:S(2)}, u32[]{:S(2)}) %collective-permute-start) | collective-permute-done | bytes 524320 | tf_op jit(solution)/shard_map/ppermute | solution.py:118
  24.1 0.6 gather_fusion
  24.7 1.0 fusion
  25.7 0.1 copy.50
  25.9 19.0 %all_to_all.30 = f32[8,32,256]{2,1,0:T(8,128)S(1)} all-to-all(f32[8,32,256]{2,1,0:T(8,128)S(1)} %bitcast.102), channel_id=1, replica_groups=mesh['chip'=16,'core'=2,'col'=8] {'col'}, dimensions={0} | all-to-all | bytes 524288 | tf_op jit(solution)/shard_map/all_to_all | solution.py:107
  44.9 0.7 broadcast_in_dim.41
  45.6 3.4 %all-to-all-start.2 = ((f32[8,32,256]{2,1,0:T(8,128)}), f32[8,32,256]{2,1,0:T(8,128)S(1)}, u32[]{:S(2)}, u32[]{:S(2)}) async-start(f32[8,32,256]{2,1,0:T(8,128)} %broadcast_in_dim.41), calls=%async_computation.2 | async-start | bytes 524288 | tf_op jit(solution)/shard_map/all_to_all | solution.py:114
  49.1 9.4 %all-to-all-done.2 = f32[8,32,256]{2,1,0:T(8,128)S(1)} async-done(((f32[8,32,256]{2,1,0:T(8,128)}), f32[8,32,256]{2,1,0:T(8,128)S(1)}, u32[]{:S(2)}, u32[]{:S(2)}) %all-to-all-start.2) | async-done | bytes 262176 | tf_op jit(solution)/shard_map/all_to_all | solution.py:114
  58.5 0.1 copy.51
  58.6 0.6 convolution_bitcast_fusion
  59.2 0.2 copy.52
  59.4 0.2 select_reduce_fusion
  59.8 3.4 %collective-permute-start.1 = (f32[16,32,256]{2,1,0:T(8,128)S(1)}, f32[16,32,256]{2,1,0:T(8,128)S(1)}, u32[]{:S(2)}, u32[]{:S(2)}) collective-permute-start(f32[16,32,256]{2,1,0:T(8,128)S(1)} %select_bitcast_fusion), channel_id=1, source_target_pairs={{0,8},{8,0},{1,9},{9,1},{2,10},{10,2},{3,11},{11,3},{4,12},{12,4},... | collective-permute-start | bytes 1572872 | tf_op jit(solution)/shard_map/ppermute | solution.py:131
  63.2 1.5 %collective-permute-done.1 = f32[16,32,256]{2,1,0:T(8,128)S(1)} collective-permute-done((f32[16,32,256]{2,1,0:T(8,128)S(1)}, f32[16,32,256]{2,1,0:T(8,128)S(1)}, u32[]{:S(2)}, u32[]{:S(2)}) %collective-permute-start.1) | collective-permute-done | bytes 524320 | tf_op jit(solution)/shard_map/ppermute | solution.py:131
  64.8 13.4 %all_to_all.31 = f32[16,32,256]{2,1,0:T(8,128)S(1)} all-to-all(f32[16,32,256]{2,1,0:T(8,128)S(1)} %fusion.2), channel_id=1, replica_groups=mesh['chip'=16,'core'=2,'col'=8] {'chip'}, dimensions={0} | all-to-all | bytes 1048576 | tf_op jit(solution)/shard_map/all_to_all | solution.py:107
  78.3 0.3 fusion.9
  78.7 1.9 %collective-permute-start.2 = (f32[16,8,256]{2,1,0:T(8,128)S(1)}, f32[16,8,256]{2,1,0:T(8,128)S(1)}, u32[]{:S(2)}, u32[]{:S(2)}) collective-permute-start(f32[16,8,256]{2,1,0:T(8,128)S(1)} %select_bitcast_fusion.3), channel_id=1, source_target_pairs={{0,8},{8,0},{1,9},{9,1},{2,10},{10,2},{3,11},{11,3},{4,12},{12,4},... | collective-permute-start | bytes 393224 | tf_op jit(solution)/shard_map/ppermute | solution.py:131
  80.6 1.0 collective-permute-done.2
  81.6 0.1 copy.62
  81.7 17.3 %all_to_all.32 = f32[128,1,256]{2,1,0:T(1,128)S(1)} all-to-all(f32[128,1,256]{2,1,0:T(1,128)S(1)} %copy.62), channel_id=1, replica_groups=mesh['chip'=16,'core'=2,'col'=8] {'chip','col'}, dimensions={0} | all-to-all | bytes 262144 | tf_op jit(solution)/shard_map/all_to_all | solution.py:107
  99.1 0.2 reduce_sum.52
  99.3 17.2 %all_to_all.33 = f32[128,1,256]{2,1,0:T(1,128)S(1)} all-to-all(f32[128,1,256]{2,1,0:T(1,128)S(1)} %broadcast_in_dim.66), channel_id=1, replica_groups=mesh['chip'=16,'core'=2,'col'=8] {'chip','col'}, dimensions={0} | all-to-all | bytes 262144 | tf_op jit(solution)/shard_map/all_to_all | solution.py:114
  116.6 2.1 %collective-permute-start.3 = (f32[128,256]{1,0:T(8,128)S(1)}, f32[128,256]{1,0:T(8,128)S(1)}, u32[]{:S(2)}, u32[]{:S(2)}) collective-permute-start(f32[128,256]{1,0:T(8,128)S(1)} %bitcast.105), channel_id=1, source_target_pairs={{0,8},{8,0},{1,9},{9,1},{2,10},{10,2},{3,11},{11,3},{4,12},{12,4},... | collective-permute-start | bytes 393224 | tf_op jit(solution)/shard_map/ppermute | solution.py:118
  118.7 1.0 collective-permute-done.3
  119.7 0.1 copy.64
  119.9 0.7 bitcast_select_fusion.1.g_ref
  120.6 16.4 %shard_map.76 = (f32[256,256]{1,0:T(8,128)}, f32[32,256]{1,0:T(8,128)}) custom-call(f32[256,256]{1,0:T(8,128)} %bitcast_select_fusion.1.g_ref, f32[32,256]{1,0:T(8,128)} %copy-done.1), custom_call_target="tpu_custom_call" | custom-call | tf_op jit(solution)/shard_map/pallas_call | solution.py:89
  137.0 0.7 copy.78
  (26 shorter events, 0.8 us)
Async XLA Ops:
  0.6 24.0 %copy-start = (f32[1,1,2,256,256]{4,3,2,1,0:T(8,128)S(1)}, f32[1,1,2,256,256]{4,3,2,1,0:T(8,128)}, u32[]{:S(2)}) copy-start(f32[1,1,2,256,256]{4,3,2,1,0:T(8,128)} %param.6) | copy-start | bytes 1572868
  0.6 21.7 %copy-start.3 = (s32[1,1,2]{2,1,0:T(1,128)S(1)}, s32[1,1,2]{2,1,0:T(1,128)}, u32[]{:S(2)}) copy-start(s32[1,1,2]{2,1,0:T(1,128)} %param.8) | copy-start | bytes 28
  0.7 21.8 %copy-start.2 = (s32[1,1,2]{2,1,0:T(1,128)S(1)}, s32[1,1,2]{2,1,0:T(1,128)}, u32[]{:S(2)}) copy-start(s32[1,1,2]{2,1,0:T(1,128)} %param.7) | copy-start | bytes 28
  2.3 18.1 %all-to-all-start = ((f32[16,32,256]{2,1,0:T(8,128)}), f32[16,32,256]{2,1,0:T(8,128)S(1)}, u32[]{:S(2)}, u32[]{:S(2)}) async-start(f32[16,32,256]{2,1,0:T(8,128)} %broadcast_in_dim.39), calls=%async_computation | async-start | bytes 1048576 | tf_op jit(solution)/shard_map/all_to_all | solution.py:114
  20.4 3.5 %collective-permute-start = (f32[512,256]{1,0:T(8,128)S(1)}, f32[512,256]{1,0:T(8,128)S(1)}, u32[]{:S(2)}, u32[]{:S(2)}) collective-permute-start(f32[512,256]{1,0:T(8,128)S(1)} %bitcast.98), channel_id=1, source_target_pairs={{0,8},{8,0},{1,9},{9,1},{2,10},{10,2},{3,11},{11,3},{4,12},{12,4},... | collective-permute-start | bytes 1572872 | tf_op jit(solution)/shard_map/ppermute | solution.py:118
  45.6 12.9 %all-to-all-start.2 = ((f32[8,32,256]{2,1,0:T(8,128)}), f32[8,32,256]{2,1,0:T(8,128)S(1)}, u32[]{:S(2)}, u32[]{:S(2)}) async-start(f32[8,32,256]{2,1,0:T(8,128)} %broadcast_in_dim.41), calls=%async_computation.2 | async-start | bytes 524288 | tf_op jit(solution)/shard_map/all_to_all | solution.py:114
  59.8 4.9 %collective-permute-start.1 = (f32[16,32,256]{2,1,0:T(8,128)S(1)}, f32[16,32,256]{2,1,0:T(8,128)S(1)}, u32[]{:S(2)}, u32[]{:S(2)}) collective-permute-start(f32[16,32,256]{2,1,0:T(8,128)S(1)} %select_bitcast_fusion), channel_id=1, source_target_pairs={{0,8},{8,0},{1,9},{9,1},{2,10},{10,2},{3,11},{11,3},{4,12},{12,4},... | collective-permute-start | bytes 1572872 | tf_op jit(solution)/shard_map/ppermute | solution.py:131
  78.2 21.0 %copy-start.1 = (f32[32,256]{1,0:T(8,128)}, f32[32,256]{1,0:T(8,128)S(1)}, u32[]{:S(2)}) copy-start(f32[32,256]{1,0:T(8,128)S(1)} %reduce_sum.51.p_ref) | copy-start | bytes 98308
  78.7 2.8 %collective-permute-start.2 = (f32[16,8,256]{2,1,0:T(8,128)S(1)}, f32[16,8,256]{2,1,0:T(8,128)S(1)}, u32[]{:S(2)}, u32[]{:S(2)}) collective-permute-start(f32[16,8,256]{2,1,0:T(8,128)S(1)} %select_bitcast_fusion.3), channel_id=1, source_target_pairs={{0,8},{8,0},{1,9},{9,1},{2,10},{10,2},{3,11},{11,3},{4,12},{12,4},... | collective-permute-start | bytes 393224 | tf_op jit(solution)/shard_map/ppermute | solution.py:131
  116.6 3.1 %collective-permute-start.3 = (f32[128,256]{1,0:T(8,128)S(1)}, f32[128,256]{1,0:T(8,128)S(1)}, u32[]{:S(2)}, u32[]{:S(2)}) collective-permute-start(f32[128,256]{1,0:T(8,128)S(1)} %bitcast.105), channel_id=1, source_target_pairs={{0,8},{8,0},{1,9},{9,1},{2,10},{10,2},{3,11},{11,3},{4,12},{12,4},... | collective-permute-start | bytes 393224 | tf_op jit(solution)/shard_map/ppermute | solution.py:118

commit v10 on v9

--- a/solution.py
+++ b/solution.py
@@ -8,7 +8,7 @@
 BR = 1
 
 
-PHASE = 32
+PHASE = 16
 BLOCK = 4
 
 

time: 138 us -> 138 us (level)
  no operation moved by 1% of the time
where the time goes in v10:
time: 138 us
  blocking collectives  67 us (49%)
  waiting for transfers between devices  24.4 us (18%)
  starting transfers between devices  20.4 us (15%)
  Pallas kernels  16.1 us (12%)
  local copies, waits for them, and re-layouts  4.59 us (3%)
  matrix products  1.98 us (1%)
  other arithmetic  1.67 us (1%)
  between operations  1.51 us (1%)
    all_to_all x3, blocking collectives, exchange_sum(): lax.all_to_all(x.reshape(size, -1, x.shape[-1]), axes, 0, 0, tiled=False)  49.8 us
    all_to_all x2, waiting for transfers between devices, exchange_gather(): lax.all_to_all(copies, axes, 0, 0, tiled=False).reshape(-1, x.shape[-1])  19.4 us
    all_to_all x1, blocking collectives, exchange_gather(): lax.all_to_all(copies, axes, 0, 0, tiled=False).reshape(-1, x.shape[-1])  17.2 us
    pallas_call x1, Pallas kernels, chol_solve(): pl.pallas_call(chol_solve_kernel, out_shape=(jax.ShapeDtypeStruct((n, n),...  16.1 us
    all_to_all x2, starting transfers between devices, exchange_gather(): lax.all_to_all(copies, axes, 0, 0, tiled=False).reshape(-1, x.shape[-1])  11 us
    ppermute x2, starting transfers between devices, pair_scatter_sum(): lax.ppermute(send, 'core', [(0, 1), (1, 0)])  5.11 us
    ppermute x2, starting transfers between devices, pair_gather(): other = lax.ppermute(x, 'core', [(0, 1), (1, 0)])  4.28 us
  transfers between devices with their start and end apart: 6, of which 6 were waited for; matrix products, arithmetic and copies ran while one was open for 0% of the time, Pallas kernels for 0%

profile of v10, /device:TPU:1, one launch (start us, length us, event | category | flops | bytes accessed | tf_op | source)
XLA Modules:
  0.0 137.6 jit_solution(7686399765454534803)
XLA Ops:
  0.7 1.6 %broadcast_in_dim.39 = f32[16,32,256]{2,1,0:T(8,128)} broadcast(f32[32,256]{1,0:T(8,128)} %param.5), dimensions={1,2} | broadcast | bytes 557056 | tf_op jit(solution)/shard_map/broadcast_in_dim | solution.py:113
  2.3 7.6 %all-to-all-start = ((f32[16,32,256]{2,1,0:T(8,128)}), f32[16,32,256]{2,1,0:T(8,128)S(1)}, u32[]{:S(2)}, u32[]{:S(2)}) async-start(f32[16,32,256]{2,1,0:T(8,128)} %broadcast_in_dim.39), calls=%async_computation | async-start | bytes 1048576 | tf_op jit(solution)/shard_map/all_to_all | solution.py:114
  10.6 9.9 %all-to-all-done = f32[16,32,256]{2,1,0:T(8,128)S(1)} async-done(((f32[16,32,256]{2,1,0:T(8,128)}), f32[16,32,256]{2,1,0:T(8,128)S(1)}, u32[]{:S(2)}, u32[]{:S(2)}) %all-to-all-start) | async-done | bytes 524320 | tf_op jit(solution)/shard_map/all_to_all | solution.py:114
  20.4 2.0 %collective-permute-start = (f32[512,256]{1,0:T(8,128)S(1)}, f32[512,256]{1,0:T(8,128)S(1)}, u32[]{:S(2)}, u32[]{:S(2)}) collective-permute-start(f32[512,256]{1,0:T(8,128)S(1)} %bitcast.98), channel_id=1, source_target_pairs={{0,8},{8,0},{1,9},{9,1},{2,10},{10,2},{3,11},{11,3},{4,12},{12,4},... | collective-permute-start | bytes 1572872 | tf_op jit(solution)/shard_map/ppermute | solution.py:118
  22.4 1.5 %collective-permute-done = f32[512,256]{1,0:T(8,128)S(1)} collective-permute-done((f32[512,256]{1,0:T(8,128)S(1)}, f32[512,256]{1,0:T(8,128)S(1)}, u32[]{:S(2)}, u32[]{:S(2)}) %collective-permute-start) | collective-permute-done | bytes 524320 | tf_op jit(solution)/shard_map/ppermute | solution.py:118
  24.1 0.6 gather_fusion
  24.7 1.0 fusion
  25.7 0.1 copy.50
  25.9 19.1 %all_to_all.30 = f32[8,32,256]{2,1,0:T(8,128)S(1)} all-to-all(f32[8,32,256]{2,1,0:T(8,128)S(1)} %bitcast.102), channel_id=1, replica_groups=mesh['chip'=16,'core'=2,'col'=8] {'col'}, dimensions={0} | all-to-all | bytes 524288 | tf_op jit(solution)/shard_map/all_to_all | solution.py:107
  45.0 0.7 broadcast_in_dim.41
  45.7 3.4 %all-to-all-start.2 = ((f32[8,32,256]{2,1,0:T(8,128)}), f32[8,32,256]{2,1,0:T(8,128)S(1)}, u32[]{:S(2)}, u32[]{:S(2)}) async-start(f32[8,32,256]{2,1,0:T(8,128)} %broadcast_in_dim.41), calls=%async_computation.2 | async-start | bytes 524288 | tf_op jit(solution)/shard_map/all_to_all | solution.py:114
  49.2 9.5 %all-to-all-done.2 = f32[8,32,256]{2,1,0:T(8,128)S(1)} async-done(((f32[8,32,256]{2,1,0:T(8,128)}), f32[8,32,256]{2,1,0:T(8,128)S(1)}, u32[]{:S(2)}, u32[]{:S(2)}) %all-to-all-start.2) | async-done | bytes 262176 | tf_op jit(solution)/shard_map/all_to_all | solution.py:114
  58.7 0.1 copy.51
  58.8 0.6 convolution_bitcast_fusion
  59.4 0.2 copy.52
  59.6 0.2 select_reduce_fusion
  60.0 3.3 %collective-permute-start.1 = (f32[16,32,256]{2,1,0:T(8,128)S(1)}, f32[16,32,256]{2,1,0:T(8,128)S(1)}, u32[]{:S(2)}, u32[]{:S(2)}) collective-permute-start(f32[16,32,256]{2,1,0:T(8,128)S(1)} %select_bitcast_fusion), channel_id=1, source_target_pairs={{0,8},{8,0},{1,9},{9,1},{2,10},{10,2},{3,11},{11,3},{4,12},{12,4},... | collective-permute-start | bytes 1572872 | tf_op jit(solution)/shard_map/ppermute | solution.py:131
  63.2 1.5 %collective-permute-done.1 = f32[16,32,256]{2,1,0:T(8,128)S(1)} collective-permute-done((f32[16,32,256]{2,1,0:T(8,128)S(1)}, f32[16,32,256]{2,1,0:T(8,128)S(1)}, u32[]{:S(2)}, u32[]{:S(2)}) %collective-permute-start.1) | collective-permute-done | bytes 524320 | tf_op jit(solution)/shard_map/ppermute | solution.py:131
  64.9 13.3 %all_to_all.31 = f32[16,32,256]{2,1,0:T(8,128)S(1)} all-to-all(f32[16,32,256]{2,1,0:T(8,128)S(1)} %fusion.2), channel_id=1, replica_groups=mesh['chip'=16,'core'=2,'col'=8] {'chip'}, dimensions={0} | all-to-all | bytes 1048576 | tf_op jit(solution)/shard_map/all_to_all | solution.py:107
  78.3 0.3 fusion.9
  78.7 1.9 %collective-permute-start.2 = (f32[16,8,256]{2,1,0:T(8,128)S(1)}, f32[16,8,256]{2,1,0:T(8,128)S(1)}, u32[]{:S(2)}, u32[]{:S(2)}) collective-permute-start(f32[16,8,256]{2,1,0:T(8,128)S(1)} %select_bitcast_fusion.3), channel_id=1, source_target_pairs={{0,8},{8,0},{1,9},{9,1},{2,10},{10,2},{3,11},{11,3},{4,12},{12,4},... | collective-permute-start | bytes 393224 | tf_op jit(solution)/shard_map/ppermute | solution.py:131
  80.6 1.0 collective-permute-done.2
  81.6 0.1 copy.62
  81.7 17.3 %all_to_all.32 = f32[128,1,256]{2,1,0:T(1,128)S(1)} all-to-all(f32[128,1,256]{2,1,0:T(1,128)S(1)} %copy.62), channel_id=1, replica_groups=mesh['chip'=16,'core'=2,'col'=8] {'chip','col'}, dimensions={0} | all-to-all | bytes 262144 | tf_op jit(solution)/shard_map/all_to_all | solution.py:107
  99.1 0.2 reduce_sum.52
  99.3 17.2 %all_to_all.33 = f32[128,1,256]{2,1,0:T(1,128)S(1)} all-to-all(f32[128,1,256]{2,1,0:T(1,128)S(1)} %broadcast_in_dim.66), channel_id=1, replica_groups=mesh['chip'=16,'core'=2,'col'=8] {'chip','col'}, dimensions={0} | all-to-all | bytes 262144 | tf_op jit(solution)/shard_map/all_to_all | solution.py:114
  116.6 2.3 %collective-permute-start.3 = (f32[128,256]{1,0:T(8,128)S(1)}, f32[128,256]{1,0:T(8,128)S(1)}, u32[]{:S(2)}, u32[]{:S(2)}) collective-permute-start(f32[128,256]{1,0:T(8,128)S(1)} %bitcast.105), channel_id=1, source_target_pairs={{0,8},{8,0},{1,9},{9,1},{2,10},{10,2},{3,11},{11,3},{4,12},{12,4},... | collective-permute-start | bytes 393224 | tf_op jit(solution)/shard_map/ppermute | solution.py:118
  118.9 1.0 collective-permute-done.3
  119.9 0.1 copy.64
  120.1 0.7 bitcast_select_fusion.1.g_ref
  120.8 16.1 %shard_map.76 = (f32[256,256]{1,0:T(8,128)}, f32[32,256]{1,0:T(8,128)}) custom-call(f32[256,256]{1,0:T(8,128)} %bitcast_select_fusion.1.g_ref, f32[32,256]{1,0:T(8,128)} %copy-done.1), custom_call_target="tpu_custom_call" | custom-call | tf_op jit(solution)/shard_map/pallas_call | solution.py:89
  136.9 0.7 copy.78
  (26 shorter events, 0.8 us)
Async XLA Ops:
  0.6 24.0 %copy-start = (f32[1,1,2,256,256]{4,3,2,1,0:T(8,128)S(1)}, f32[1,1,2,256,256]{4,3,2,1,0:T(8,128)}, u32[]{:S(2)}) copy-start(f32[1,1,2,256,256]{4,3,2,1,0:T(8,128)} %param.6) | copy-start | bytes 1572868
  0.6 21.7 %copy-start.3 = (s32[1,1,2]{2,1,0:T(1,128)S(1)}, s32[1,1,2]{2,1,0:T(1,128)}, u32[]{:S(2)}) copy-start(s32[1,1,2]{2,1,0:T(1,128)} %param.8) | copy-start | bytes 28
  0.7 21.8 %copy-start.2 = (s32[1,1,2]{2,1,0:T(1,128)S(1)}, s32[1,1,2]{2,1,0:T(1,128)}, u32[]{:S(2)}) copy-start(s32[1,1,2]{2,1,0:T(1,128)} %param.7) | copy-start | bytes 28
  2.3 18.1 %all-to-all-start = ((f32[16,32,256]{2,1,0:T(8,128)}), f32[16,32,256]{2,1,0:T(8,128)S(1)}, u32[]{:S(2)}, u32[]{:S(2)}) async-start(f32[16,32,256]{2,1,0:T(8,128)} %broadcast_in_dim.39), calls=%async_computation | async-start | bytes 1048576 | tf_op jit(solution)/shard_map/all_to_all | solution.py:114
  20.4 3.5 %collective-permute-start = (f32[512,256]{1,0:T(8,128)S(1)}, f32[512,256]{1,0:T(8,128)S(1)}, u32[]{:S(2)}, u32[]{:S(2)}) collective-permute-start(f32[512,256]{1,0:T(8,128)S(1)} %bitcast.98), channel_id=1, source_target_pairs={{0,8},{8,0},{1,9},{9,1},{2,10},{10,2},{3,11},{11,3},{4,12},{12,4},... | collective-permute-start | bytes 1572872 | tf_op jit(solution)/shard_map/ppermute | solution.py:118
  45.7 13.0 %all-to-all-start.2 = ((f32[8,32,256]{2,1,0:T(8,128)}), f32[8,32,256]{2,1,0:T(8,128)S(1)}, u32[]{:S(2)}, u32[]{:S(2)}) async-start(f32[8,32,256]{2,1,0:T(8,128)} %broadcast_in_dim.41), calls=%async_computation.2 | async-start | bytes 524288 | tf_op jit(solution)/shard_map/all_to_all | solution.py:114
  60.0 4.8 %collective-permute-start.1 = (f32[16,32,256]{2,1,0:T(8,128)S(1)}, f32[16,32,256]{2,1,0:T(8,128)S(1)}, u32[]{:S(2)}, u32[]{:S(2)}) collective-permute-start(f32[16,32,256]{2,1,0:T(8,128)S(1)} %select_bitcast_fusion), channel_id=1, source_target_pairs={{0,8},{8,0},{1,9},{9,1},{2,10},{10,2},{3,11},{11,3},{4,12},{12,4},... | collective-permute-start | bytes 1572872 | tf_op jit(solution)/shard_map/ppermute | solution.py:131
  78.2 21.0 %copy-start.1 = (f32[32,256]{1,0:T(8,128)}, f32[32,256]{1,0:T(8,128)S(1)}, u32[]{:S(2)}) copy-start(f32[32,256]{1,0:T(8,128)S(1)} %reduce_sum.51.p_ref) | copy-start | bytes 98308
  78.7 2.8 %collective-permute-start.2 = (f32[16,8,256]{2,1,0:T(8,128)S(1)}, f32[16,8,256]{2,1,0:T(8,128)S(1)}, u32[]{:S(2)}, u32[]{:S(2)}) collective-permute-start(f32[16,8,256]{2,1,0:T(8,128)S(1)} %select_bitcast_fusion.3), channel_id=1, source_target_pairs={{0,8},{8,0},{1,9},{9,1},{2,10},{10,2},{3,11},{11,3},{4,12},{12,4},... | collective-permute-start | bytes 393224 | tf_op jit(solution)/shard_map/ppermute | solution.py:131
  116.6 3.3 %collective-permute-start.3 = (f32[128,256]{1,0:T(8,128)S(1)}, f32[128,256]{1,0:T(8,128)S(1)}, u32[]{:S(2)}, u32[]{:S(2)}) collective-permute-start(f32[128,256]{1,0:T(8,128)S(1)} %bitcast.105), channel_id=1, source_target_pairs={{0,8},{8,0},{1,9},{9,1},{2,10},{10,2},{3,11},{11,3},{4,12},{12,4},... | collective-permute-start | bytes 393224 | tf_op jit(solution)/shard_map/ppermute | solution.py:118

commit v11 on v10

--- a/solution.py
+++ b/solution.py
@@ -145,12 +145,16 @@
     block_rows = BR
     live = jnp.arange(slot_total, dtype=jnp.int32) < live_count
     row_hit = (row_ids[:, None] == jnp.arange(block_rows, dtype=jnp.int32)[None, :]) & live[:, None]
-    products = jnp.einsum(
-        "tij,tjk->tik",
-        values,
-        start_blocks[col_ids],
-        precision=lax.Precision.HIGHEST,
-        preferred_element_type=jnp.float32,
+    products = jnp.stack(
+        [
+            jnp.dot(
+                values[slot],
+                lax.dynamic_index_in_dim(start_blocks, col_ids[slot], 0, keepdims=False),
+                precision=lax.Precision.HIGHEST,
+                preferred_element_type=jnp.float32,
+            )
+            for slot in range(slot_total)
+        ]
     )
     partial_image = jnp.sum(
         jnp.where(row_hit[:, :, None, None], products[:, None], 0.0), axis=0

time: 138 us -> 143 us (1.036)
  blocking collectives: 67 us -> 86.2 us
  starting transfers between devices: 20.4 us -> 10.2 us
  waiting for transfers between devices: 24.4 us -> 15.6 us
  between operations: 1.51 us -> 5.4 us
    all_to_all x1 -> x2, blocking collectives: 17.2 us -> 35.1 us  [exchange_gather(): lax.all_to_all(copies, axes, 0, 0, tiled=False).reshape(-1, x.shape[-1])]
    all_to_all x2 -> x1, starting transfers between devices: 11 us -> 3.41 us  [exchange_gather(): lax.all_to_all(copies, axes, 0, 0, tiled=False).reshape(-1, x.shape[-1])]
    all_to_all x2 -> x1, waiting for transfers between devices: 19.4 us -> 12.1 us  [exchange_gather(): lax.all_to_all(copies, axes, 0, 0, tiled=False).reshape(-1, x.shape[-1])]
    ppermute x2, starting transfers between devices: 5.11 us -> 2.53 us  [pair_scatter_sum(): lax.ppermute(send, 'core', [(0, 1), (1, 0)])]
    ppermute x2, waiting for transfers between devices: 2.48 us -> 0.99 us  [pair_gather(): other = lax.ppermute(x, 'core', [(0, 1), (1, 0)])]
  transfers between devices with their start and end apart: 6 -> 5, of which waited for: 6 -> 4; matrix products, arithmetic and copies ran while one was open for 0% -> 0% of each run, Pallas kernels for 0% -> 0%
where the time goes in v11:
time: 143 us; the launch traced here: 142 us
  blocking collectives  86.2 us (60%)
  Pallas kernels  16.1 us (11%)
  waiting for transfers between devices  15.6 us (11%)
  starting transfers between devices  10.2 us (7%)
  between operations  5.4 us (4%)
  local copies, waits for them, and re-layouts  4.67 us (3%)
  matrix products  2.15 us (2%)
  other arithmetic  1.8 us (1%)
    all_to_all x3, blocking collectives, exchange_sum(): lax.all_to_all(x.reshape(size, -1, x.shape[-1]), axes, 0, 0, tiled=False)  51.1 us
    all_to_all x2, blocking collectives, exchange_gather(): lax.all_to_all(copies, axes, 0, 0, tiled=False).reshape(-1, x.shape[-1])  35.1 us
    pallas_call x1, Pallas kernels, chol_solve(): pl.pallas_call(chol_solve_kernel, out_shape=(jax.ShapeDtypeStruct((n, n),...  16.1 us
    all_to_all x1, waiting for transfers between devices, exchange_gather(): lax.all_to_all(copies, axes, 0, 0, tiled=False).reshape(-1, x.shape[-1])  12.1 us
    ppermute x2, starting transfers between devices, pair_gather(): other = lax.ppermute(x, 'core', [(0, 1), (1, 0)])  4.28 us
    all_to_all x1, starting transfers between devices, exchange_gather(): lax.all_to_all(copies, axes, 0, 0, tiled=False).reshape(-1, x.shape[-1])  3.41 us
  transfers between devices with their start and end apart: 5, of which 4 were waited for; matrix products, arithmetic and copies ran while one was open for 0% of the time, Pallas kernels for 0%

profile of v11, /device:TPU:1, one launch (start us, length us, event | category | flops | bytes accessed | tf_op | source)
XLA Modules:
  0.0 142.1 jit_solution(8439178526943303427)
XLA Ops:
  0.7 0.8 broadcast_in_dim.39
  1.5 17.9 %all_to_all.30 = f32[16,32,256]{2,1,0:T(8,128)S(1)} all-to-all(f32[16,32,256]{2,1,0:T(8,128)S(1)} %broadcast_in_dim.39), channel_id=1, replica_groups=mesh['chip'=16,'core'=2,'col'=8] {'chip'}, dimensions={0} | all-to-all | bytes 1048576 | tf_op jit(solution)/shard_map/all_to_all | solution.py:114
  19.4 2.0 %collective-permute-start = (f32[512,256]{1,0:T(8,128)S(1)}, f32[512,256]{1,0:T(8,128)S(1)}, u32[]{:S(2)}, u32[]{:S(2)}) collective-permute-start(f32[512,256]{1,0:T(8,128)S(1)} %bitcast.113), channel_id=1, source_target_pairs={{0,8},{8,0},{1,9},{9,1},{2,10},{10,2},{3,11},{11,3},{4,12},{12,4},... | collective-permute-start | bytes 1572872 | tf_op jit(solution)/shard_map/ppermute | solution.py:118
  21.3 0.6 fusion.20
  26.7 0.9 copy-done
  27.6 0.6 convolution_bitcast_fusion.1
  28.2 0.6 convolution_bitcast_fusion.2
  29.0 0.1 copy.61
  29.1 20.3 %all_to_all.31 = f32[8,32,256]{2,1,0:T(8,128)S(1)} all-to-all(f32[8,32,256]{2,1,0:T(8,128)S(1)} %bitcast.116), channel_id=1, replica_groups=mesh['chip'=16,'core'=2,'col'=8] {'col'}, dimensions={0} | all-to-all | bytes 524288 | tf_op jit(solution)/shard_map/all_to_all | solution.py:107
  49.5 0.7 broadcast_in_dim.41
  50.2 3.4 %all-to-all-start.2 = ((f32[8,32,256]{2,1,0:T(8,128)}), f32[8,32,256]{2,1,0:T(8,128)S(1)}, u32[]{:S(2)}, u32[]{:S(2)}) async-start(f32[8,32,256]{2,1,0:T(8,128)} %broadcast_in_dim.41), calls=%async_computation.2 | async-start | bytes 524288 | tf_op jit(solution)/shard_map/all_to_all | solution.py:114
  53.7 12.1 %all-to-all-done.2 = f32[8,32,256]{2,1,0:T(8,128)S(1)} async-done(((f32[8,32,256]{2,1,0:T(8,128)}), f32[8,32,256]{2,1,0:T(8,128)S(1)}, u32[]{:S(2)}, u32[]{:S(2)}) %all-to-all-start.2) | async-done | bytes 262176 | tf_op jit(solution)/shard_map/all_to_all | solution.py:114
  65.8 0.1 copy.62
  65.9 0.6 convolution_bitcast_fusion
  66.5 0.2 copy.63
  66.7 0.2 select_reduce_fusion
  67.1 0.7 collective-permute-start.1
  67.7 1.5 %collective-permute-done.1 = f32[16,32,256]{2,1,0:T(8,128)S(1)} collective-permute-done((f32[16,32,256]{2,1,0:T(8,128)S(1)}, f32[16,32,256]{2,1,0:T(8,128)S(1)}, u32[]{:S(2)}, u32[]{:S(2)}) %collective-permute-start.1) | collective-permute-done | bytes 524320 | tf_op jit(solution)/shard_map/ppermute | solution.py:131
  69.4 13.4 %all_to_all.32 = f32[16,32,256]{2,1,0:T(8,128)S(1)} all-to-all(f32[16,32,256]{2,1,0:T(8,128)S(1)} %fusion.2), channel_id=1, replica_groups=mesh['chip'=16,'core'=2,'col'=8] {'chip'}, dimensions={0} | all-to-all | bytes 1048576 | tf_op jit(solution)/shard_map/all_to_all | solution.py:107
  82.9 0.3 fusion.16
  83.3 1.9 %collective-permute-start.2 = (f32[16,8,256]{2,1,0:T(8,128)S(1)}, f32[16,8,256]{2,1,0:T(8,128)S(1)}, u32[]{:S(2)}, u32[]{:S(2)}) collective-permute-start(f32[16,8,256]{2,1,0:T(8,128)S(1)} %select_bitcast_fusion.3), channel_id=1, source_target_pairs={{0,8},{8,0},{1,9},{9,1},{2,10},{10,2},{3,11},{11,3},{4,12},{12,4},... | collective-permute-start | bytes 393224 | tf_op jit(solution)/shard_map/ppermute | solution.py:131
  85.1 1.0 collective-permute-done.2
  86.2 0.1 copy.73
  86.3 17.3 %all_to_all.33 = f32[128,1,256]{2,1,0:T(1,128)S(1)} all-to-all(f32[128,1,256]{2,1,0:T(1,128)S(1)} %copy.73), channel_id=1, replica_groups=mesh['chip'=16,'core'=2,'col'=8] {'chip','col'}, dimensions={0} | all-to-all | bytes 262144 | tf_op jit(solution)/shard_map/all_to_all | solution.py:107
  103.6 0.2 reduce_sum.49
  103.9 17.2 %all_to_all.34 = f32[128,1,256]{2,1,0:T(1,128)S(1)} all-to-all(f32[128,1,256]{2,1,0:T(1,128)S(1)} %broadcast_in_dim.65), channel_id=1, replica_groups=mesh['chip'=16,'core'=2,'col'=8] {'chip','col'}, dimensions={0} | all-to-all | bytes 262144 | tf_op jit(solution)/shard_map/all_to_all | solution.py:114
  121.1 2.3 %collective-permute-start.3 = (f32[128,256]{1,0:T(8,128)S(1)}, f32[128,256]{1,0:T(8,128)S(1)}, u32[]{:S(2)}, u32[]{:S(2)}) collective-permute-start(f32[128,256]{1,0:T(8,128)S(1)} %bitcast.119), channel_id=1, source_target_pairs={{0,8},{8,0},{1,9},{9,1},{2,10},{10,2},{3,11},{11,3},{4,12},{12,4},... | collective-permute-start | bytes 393224 | tf_op jit(solution)/shard_map/ppermute | solution.py:118
  123.4 1.0 collective-permute-done.3
  124.5 0.1 copy.75
  124.6 0.7 bitcast_select_fusion.1.g_ref
  125.3 16.1 %shard_map.76 = (f32[256,256]{1,0:T(8,128)}, f32[32,256]{1,0:T(8,128)}) custom-call(f32[256,256]{1,0:T(8,128)} %bitcast_select_fusion.1.g_ref, f32[32,256]{1,0:T(8,128)} %copy-done.1), custom_call_target="tpu_custom_call" | custom-call | tf_op jit(solution)/shard_map/pallas_call | solution.py:89
  141.4 0.7 copy.88
  (25 shorter events, 0.9 us)
Async XLA Ops:
  0.6 20.7 %copy-start.2 = (s32[1,1,2]{2,1,0:T(1,128)S(1)}, s32[1,1,2]{2,1,0:T(1,128)}, u32[]{:S(2)}) copy-start(s32[1,1,2]{2,1,0:T(1,128)} %param.8) | copy-start | bytes 28
  0.6 25.8 %copy-start.3 = (s32[1,1,2]{2,1,0:T(1,128)S(1)}, s32[1,1,2]{2,1,0:T(1,128)}, u32[]{:S(2)}) copy-start(s32[1,1,2]{2,1,0:T(1,128)} %param.7) | copy-start | bytes 28
  19.4 7.1 %collective-permute-start = (f32[512,256]{1,0:T(8,128)S(1)}, f32[512,256]{1,0:T(8,128)S(1)}, u32[]{:S(2)}, u32[]{:S(2)}) collective-permute-start(f32[512,256]{1,0:T(8,128)S(1)} %bitcast.113), channel_id=1, source_target_pairs={{0,8},{8,0},{1,9},{9,1},{2,10},{10,2},{3,11},{11,3},{4,12},{12,4},... | collective-permute-start | bytes 1572872 | tf_op jit(solution)/shard_map/ppermute | solution.py:118
  26.6 1.0 copy-start
  50.2 15.6 %all-to-all-start.2 = ((f32[8,32,256]{2,1,0:T(8,128)}), f32[8,32,256]{2,1,0:T(8,128)S(1)}, u32[]{:S(2)}, u32[]{:S(2)}) async-start(f32[8,32,256]{2,1,0:T(8,128)} %broadcast_in_dim.41), calls=%async_computation.2 | async-start | bytes 524288 | tf_op jit(solution)/shard_map/all_to_all | solution.py:114
  67.1 2.2 %collective-permute-start.1 = (f32[16,32,256]{2,1,0:T(8,128)S(1)}, f32[16,32,256]{2,1,0:T(8,128)S(1)}, u32[]{:S(2)}, u32[]{:S(2)}) collective-permute-start(f32[16,32,256]{2,1,0:T(8,128)S(1)} %select_bitcast_fusion), channel_id=1, source_target_pairs={{0,8},{8,0},{1,9},{9,1},{2,10},{10,2},{3,11},{11,3},{4,12},{12,4},... | collective-permute-start | bytes 1572872 | tf_op jit(solution)/shard_map/ppermute | solution.py:131
  82.8 21.0 %copy-start.1 = (f32[32,256]{1,0:T(8,128)}, f32[32,256]{1,0:T(8,128)S(1)}, u32[]{:S(2)}) copy-start(f32[32,256]{1,0:T(8,128)S(1)} %reduce_sum.48.p_ref) | copy-start | bytes 98308
  83.3 2.9 %collective-permute-start.2 = (f32[16,8,256]{2,1,0:T(8,128)S(1)}, f32[16,8,256]{2,1,0:T(8,128)S(1)}, u32[]{:S(2)}, u32[]{:S(2)}) collective-permute-start(f32[16,8,256]{2,1,0:T(8,128)S(1)} %select_bitcast_fusion.3), channel_id=1, source_target_pairs={{0,8},{8,0},{1,9},{9,1},{2,10},{10,2},{3,11},{11,3},{4,12},{12,4},... | collective-permute-start | bytes 393224 | tf_op jit(solution)/shard_map/ppermute | solution.py:131
  121.1 3.3 %collective-permute-start.3 = (f32[128,256]{1,0:T(8,128)S(1)}, f32[128,256]{1,0:T(8,128)S(1)}, u32[]{:S(2)}, u32[]{:S(2)}) collective-permute-start(f32[128,256]{1,0:T(8,128)S(1)} %bitcast.119), channel_id=1, source_target_pairs={{0,8},{8,0},{1,9},{9,1},{2,10},{10,2},{3,11},{11,3},{4,12},{12,4},... | collective-permute-start | bytes 393224 | tf_op jit(solution)/shard_map/ppermute | solution.py:118

commit v12 on v10

--- a/solution.py
+++ b/solution.py
@@ -125,9 +125,9 @@
 def pair_scatter_sum(x):
     chips = lax.axis_size("chip")
     pairs = x.reshape(chips, 2, -1, x.shape[-1])
-    first = lax.axis_index("core") == 0
-    keep = jnp.where(first, pairs[:, 0], pairs[:, 1])
-    send = jnp.where(first, pairs[:, 1], pairs[:, 0])
+    core = lax.axis_index("core")
+    keep = lax.dynamic_index_in_dim(pairs, core, 1, keepdims=False)
+    send = lax.dynamic_index_in_dim(pairs, 1 - core, 1, keepdims=False)
     return (keep + lax.ppermute(send, "core", [(0, 1), (1, 0)])).reshape(-1, x.shape[-1])
 
 

time: 138 us -> 138 us (level)
  no operation moved by 1% of the time
where the time goes in v12:
time: 138 us; the launch traced here: 137 us
  blocking collectives  67 us (49%)
  waiting for transfers between devices  24.4 us (18%)
  starting transfers between devices  20.4 us (15%)
  Pallas kernels  16.1 us (12%)
  local copies, waits for them, and re-layouts  4.65 us (3%)
  matrix products  1.98 us (1%)
  other arithmetic  1.54 us (1%)
  between operations  1.51 us (1%)
    all_to_all x3, blocking collectives, exchange_sum(): lax.all_to_all(x.reshape(size, -1, x.shape[-1]), axes, 0, 0, tiled=False)  49.8 us
    all_to_all x2, waiting for transfers between devices, exchange_gather(): lax.all_to_all(copies, axes, 0, 0, tiled=False).reshape(-1, x.shape[-1])  19.4 us
    all_to_all x1, blocking collectives, exchange_gather(): lax.all_to_all(copies, axes, 0, 0, tiled=False).reshape(-1, x.shape[-1])  17.2 us
    pallas_call x1, Pallas kernels, chol_solve(): pl.pallas_call(chol_solve_kernel, out_shape=(jax.ShapeDtypeStruct((n, n),...  16.1 us
    all_to_all x2, starting transfers between devices, exchange_gather(): lax.all_to_all(copies, axes, 0, 0, tiled=False).reshape(-1, x.shape[-1])  11 us
    ppermute x2, starting transfers between devices, pair_scatter_sum(): lax.ppermute(send, 'core', [(0, 1), (1, 0)])  5.11 us
    ppermute x2, starting transfers between devices, pair_gather(): other = lax.ppermute(x, 'core', [(0, 1), (1, 0)])  4.28 us
  transfers between devices with their start and end apart: 6, of which 6 were waited for; matrix products, arithmetic and copies ran while one was open for 0% of the time, Pallas kernels for 0%

profile of v12, /device:TPU:1, one launch (start us, length us, event | category | flops | bytes accessed | tf_op | source)
XLA Modules:
  0.0 137.5 jit_solution(2303365779135113589)
XLA Ops:
  0.7 1.6 %broadcast_in_dim.39 = f32[16,32,256]{2,1,0:T(8,128)} broadcast(f32[32,256]{1,0:T(8,128)} %param.5), dimensions={1,2} | broadcast | bytes 557056 | tf_op jit(solution)/shard_map/broadcast_in_dim | solution.py:113
  2.3 7.6 %all-to-all-start = ((f32[16,32,256]{2,1,0:T(8,128)}), f32[16,32,256]{2,1,0:T(8,128)S(1)}, u32[]{:S(2)}, u32[]{:S(2)}) async-start(f32[16,32,256]{2,1,0:T(8,128)} %broadcast_in_dim.39), calls=%async_computation | async-start | bytes 1048576 | tf_op jit(solution)/shard_map/all_to_all | solution.py:114
  10.6 9.9 %all-to-all-done = f32[16,32,256]{2,1,0:T(8,128)S(1)} async-done(((f32[16,32,256]{2,1,0:T(8,128)}), f32[16,32,256]{2,1,0:T(8,128)S(1)}, u32[]{:S(2)}, u32[]{:S(2)}) %all-to-all-start) | async-done | bytes 524320 | tf_op jit(solution)/shard_map/all_to_all | solution.py:114
  20.4 2.0 %collective-permute-start = (f32[512,256]{1,0:T(8,128)S(1)}, f32[512,256]{1,0:T(8,128)S(1)}, u32[]{:S(2)}, u32[]{:S(2)}) collective-permute-start(f32[512,256]{1,0:T(8,128)S(1)} %bitcast.64), channel_id=1, source_target_pairs={{0,8},{8,0},{1,9},{9,1},{2,10},{10,2},{3,11},{11,3},{4,12},{12,4},... | collective-permute-start | bytes 1572872 | tf_op jit(solution)/shard_map/ppermute | solution.py:118
  22.4 1.5 %collective-permute-done = f32[512,256]{1,0:T(8,128)S(1)} collective-permute-done((f32[512,256]{1,0:T(8,128)S(1)}, f32[512,256]{1,0:T(8,128)S(1)}, u32[]{:S(2)}, u32[]{:S(2)}) %collective-permute-start) | collective-permute-done | bytes 524320 | tf_op jit(solution)/shard_map/ppermute | solution.py:118
  24.1 0.6 gather_fusion
  24.7 1.0 fusion
  25.7 0.1 copy.26
  25.9 19.1 %all_to_all.30 = f32[8,32,256]{2,1,0:T(8,128)S(1)} all-to-all(f32[8,32,256]{2,1,0:T(8,128)S(1)} %bitcast.68), channel_id=1, replica_groups=mesh['chip'=16,'core'=2,'col'=8] {'col'}, dimensions={0} | all-to-all | bytes 524288 | tf_op jit(solution)/shard_map/all_to_all | solution.py:107
  45.0 0.7 broadcast_in_dim.41
  45.7 3.4 %all-to-all-start.2 = ((f32[8,32,256]{2,1,0:T(8,128)}), f32[8,32,256]{2,1,0:T(8,128)S(1)}, u32[]{:S(2)}, u32[]{:S(2)}) async-start(f32[8,32,256]{2,1,0:T(8,128)} %broadcast_in_dim.41), calls=%async_computation.2 | async-start | bytes 524288 | tf_op jit(solution)/shard_map/all_to_all | solution.py:114
  49.2 9.5 %all-to-all-done.2 = f32[8,32,256]{2,1,0:T(8,128)S(1)} async-done(((f32[8,32,256]{2,1,0:T(8,128)}), f32[8,32,256]{2,1,0:T(8,128)S(1)}, u32[]{:S(2)}, u32[]{:S(2)}) %all-to-all-start.2) | async-done | bytes 262176 | tf_op jit(solution)/shard_map/all_to_all | solution.py:114
  58.7 0.1 copy.27
  58.8 0.6 convolution_bitcast_fusion
  59.4 0.2 copy.28
  59.6 0.2 select_reduce_fusion
  59.9 3.3 %collective-permute-start.1 = (f32[16,32,256]{2,1,0:T(8,128)S(1)}, f32[16,32,256]{2,1,0:T(8,128)S(1)}, u32[]{:S(2)}, u32[]{:S(2)}) collective-permute-start(f32[16,32,256]{2,1,0:T(8,128)S(1)} %dynamic-slice_bitcast_fusion), channel_id=1, source_target_pairs={{0,8},{8,0},{1,9},{9,1},{2,10},{10,2},{3,11},{11,3},{4,12},{12,4},... | collective-permute-start | bytes 1572872 | tf_op jit(solution)/shard_map/ppermute | solution.py:131
  63.2 1.5 %collective-permute-done.1 = f32[16,32,256]{2,1,0:T(8,128)S(1)} collective-permute-done((f32[16,32,256]{2,1,0:T(8,128)S(1)}, f32[16,32,256]{2,1,0:T(8,128)S(1)}, u32[]{:S(2)}, u32[]{:S(2)}) %collective-permute-start.1) | collective-permute-done | bytes 524320 | tf_op jit(solution)/shard_map/ppermute | solution.py:131
  64.8 13.3 %all_to_all.31 = f32[16,32,256]{2,1,0:T(8,128)S(1)} all-to-all(f32[16,32,256]{2,1,0:T(8,128)S(1)} %bitcast_add_fusion), channel_id=1, replica_groups=mesh['chip'=16,'core'=2,'col'=8] {'chip'}, dimensions={0} | all-to-all | bytes 1048576 | tf_op jit(solution)/shard_map/all_to_all | solution.py:107
  78.3 0.3 fusion.4
  78.7 1.9 %collective-permute-start.2 = (f32[16,8,256]{2,1,0:T(8,128)S(1)}, f32[16,8,256]{2,1,0:T(8,128)S(1)}, u32[]{:S(2)}, u32[]{:S(2)}) collective-permute-start(f32[16,8,256]{2,1,0:T(8,128)S(1)} %dynamic-slice_bitcast_fusion.1), channel_id=1, source_target_pairs={{0,8},{8,0},{1,9},{9,1},{2,10},{10,2},{3,11},{11,3},{4,12},{12,4},... | collective-permute-start | bytes 393224 | tf_op jit(solution)/shard_map/ppermute | solution.py:131
  80.5 1.0 collective-permute-done.2
  81.5 0.1 reshape_reshape.19
  81.7 17.3 %all_to_all.32 = f32[128,1,256]{2,1,0:T(1,128)S(1)} all-to-all(f32[128,1,256]{2,1,0:T(1,128)S(1)} %reshape_reshape.19), channel_id=1, replica_groups=mesh['chip'=16,'core'=2,'col'=8] {'chip','col'}, dimensions={0} | all-to-all | bytes 262144 | tf_op jit(solution)/shard_map/all_to_all | solution.py:107
  99.0 0.2 reduce_sum.52
  99.2 17.2 %all_to_all.33 = f32[128,1,256]{2,1,0:T(1,128)S(1)} all-to-all(f32[128,1,256]{2,1,0:T(1,128)S(1)} %broadcast_in_dim.66), channel_id=1, replica_groups=mesh['chip'=16,'core'=2,'col'=8] {'chip','col'}, dimensions={0} | all-to-all | bytes 262144 | tf_op jit(solution)/shard_map/all_to_all | solution.py:114
  116.5 2.3 %collective-permute-start.3 = (f32[128,256]{1,0:T(8,128)S(1)}, f32[128,256]{1,0:T(8,128)S(1)}, u32[]{:S(2)}, u32[]{:S(2)}) collective-permute-start(f32[128,256]{1,0:T(8,128)S(1)} %bitcast.71), channel_id=1, source_target_pairs={{0,8},{8,0},{1,9},{9,1},{2,10},{10,2},{3,11},{11,3},{4,12},{12,4},... | collective-permute-start | bytes 393224 | tf_op jit(solution)/shard_map/ppermute | solution.py:118
  118.8 1.0 collective-permute-done.3
  119.9 0.1 copy.31
  120.0 0.7 bitcast_select_fusion.g_ref
  120.7 16.1 %shard_map.76 = (f32[256,256]{1,0:T(8,128)}, f32[32,256]{1,0:T(8,128)}) custom-call(f32[256,256]{1,0:T(8,128)} %bitcast_select_fusion.g_ref, f32[32,256]{1,0:T(8,128)} %copy-done.1), custom_call_target="tpu_custom_call" | custom-call | tf_op jit(solution)/shard_map/pallas_call | solution.py:89
  136.8 0.7 copy.43
  (26 shorter events, 0.7 us)
Async XLA Ops:
  0.6 24.0 %copy-start = (f32[1,1,2,256,256]{4,3,2,1,0:T(8,128)S(1)}, f32[1,1,2,256,256]{4,3,2,1,0:T(8,128)}, u32[]{:S(2)}) copy-start(f32[1,1,2,256,256]{4,3,2,1,0:T(8,128)} %param.6) | copy-start | bytes 1572868
  0.6 21.7 %copy-start.3 = (s32[1,1,2]{2,1,0:T(1,128)S(1)}, s32[1,1,2]{2,1,0:T(1,128)}, u32[]{:S(2)}) copy-start(s32[1,1,2]{2,1,0:T(1,128)} %param.8) | copy-start | bytes 28
  0.7 21.8 %copy-start.2 = (s32[1,1,2]{2,1,0:T(1,128)S(1)}, s32[1,1,2]{2,1,0:T(1,128)}, u32[]{:S(2)}) copy-start(s32[1,1,2]{2,1,0:T(1,128)} %param.7) | copy-start | bytes 28
  2.3 18.1 %all-to-all-start = ((f32[16,32,256]{2,1,0:T(8,128)}), f32[16,32,256]{2,1,0:T(8,128)S(1)}, u32[]{:S(2)}, u32[]{:S(2)}) async-start(f32[16,32,256]{2,1,0:T(8,128)} %broadcast_in_dim.39), calls=%async_computation | async-start | bytes 1048576 | tf_op jit(solution)/shard_map/all_to_all | solution.py:114
  20.4 3.5 %collective-permute-start = (f32[512,256]{1,0:T(8,128)S(1)}, f32[512,256]{1,0:T(8,128)S(1)}, u32[]{:S(2)}, u32[]{:S(2)}) collective-permute-start(f32[512,256]{1,0:T(8,128)S(1)} %bitcast.64), channel_id=1, source_target_pairs={{0,8},{8,0},{1,9},{9,1},{2,10},{10,2},{3,11},{11,3},{4,12},{12,4},... | collective-permute-start | bytes 1572872 | tf_op jit(solution)/shard_map/ppermute | solution.py:118
  45.7 13.0 %all-to-all-start.2 = ((f32[8,32,256]{2,1,0:T(8,128)}), f32[8,32,256]{2,1,0:T(8,128)S(1)}, u32[]{:S(2)}, u32[]{:S(2)}) async-start(f32[8,32,256]{2,1,0:T(8,128)} %broadcast_in_dim.41), calls=%async_computation.2 | async-start | bytes 524288 | tf_op jit(solution)/shard_map/all_to_all | solution.py:114
  59.9 4.8 %collective-permute-start.1 = (f32[16,32,256]{2,1,0:T(8,128)S(1)}, f32[16,32,256]{2,1,0:T(8,128)S(1)}, u32[]{:S(2)}, u32[]{:S(2)}) collective-permute-start(f32[16,32,256]{2,1,0:T(8,128)S(1)} %dynamic-slice_bitcast_fusion), channel_id=1, source_target_pairs={{0,8},{8,0},{1,9},{9,1},{2,10},{10,2},{3,11},{11,3},{4,12},{12,4},... | collective-permute-start | bytes 1572872 | tf_op jit(solution)/shard_map/ppermute | solution.py:131
  78.2 38.3 %copy-start.1 = (f32[32,256]{1,0:T(8,128)}, f32[32,256]{1,0:T(8,128)S(1)}, u32[]{:S(2)}) copy-start(f32[32,256]{1,0:T(8,128)S(1)} %reduce_sum.51.p_ref) | copy-start | bytes 98308
  78.7 2.8 %collective-permute-start.2 = (f32[16,8,256]{2,1,0:T(8,128)S(1)}, f32[16,8,256]{2,1,0:T(8,128)S(1)}, u32[]{:S(2)}, u32[]{:S(2)}) collective-permute-start(f32[16,8,256]{2,1,0:T(8,128)S(1)} %dynamic-slice_bitcast_fusion.1), channel_id=1, source_target_pairs={{0,8},{8,0},{1,9},{9,1},{2,10},{10,2},{3,11},{11,3},{4,12},{12,4},... | collective-permute-start | bytes 393224 | tf_op jit(solution)/shard_map/ppermute | solution.py:131
  116.5 3.3 %collective-permute-start.3 = (f32[128,256]{1,0:T(8,128)S(1)}, f32[128,256]{1,0:T(8,128)S(1)}, u32[]{:S(2)}, u32[]{:S(2)}) collective-permute-start(f32[128,256]{1,0:T(8,128)S(1)} %bitcast.71), channel_id=1, source_target_pairs={{0,8},{8,0},{1,9},{9,1},{2,10},{10,2},{3,11},{11,3},{4,12},{12,4},... | collective-permute-start | bytes 393224 | tf_op jit(solution)/shard_map/ppermute | solution.py:118

commit v13 on v12

--- a/solution.py
+++ b/solution.py
@@ -116,9 +116,10 @@
 
 def pair_gather(x):
     other = lax.ppermute(x, "core", [(0, 1), (1, 0)])
-    first = lax.axis_index("core") == 0
-    low = jnp.where(first, x, other).reshape(lax.axis_size("chip"), -1, x.shape[-1])
-    high = jnp.where(first, other, x).reshape(lax.axis_size("chip"), -1, x.shape[-1])
+    core = lax.axis_index("core")
+    both = jnp.stack([x, other]).reshape(2, lax.axis_size("chip"), -1, x.shape[-1])
+    low = lax.dynamic_index_in_dim(both, core, 0, keepdims=False)
+    high = lax.dynamic_index_in_dim(both, 1 - core, 0, keepdims=False)
     return jnp.stack([low, high], axis=1).reshape(-1, x.shape[-1])
 
 

time: 138 us -> 138 us (level)
  no operation moved by 1% of the time
where the time goes in v13:
time: 138 us
  blocking collectives  67 us (49%)
  waiting for transfers between devices  24.2 us (18%)
  starting transfers between devices  20.5 us (15%)
  Pallas kernels  16.1 us (12%)
  local copies, waits for them, and re-layouts  4.63 us (3%)
  matrix products  1.98 us (1%)
  other arithmetic  1.77 us (1%)
  between operations  1.5 us (1%)
    all_to_all x3, blocking collectives, exchange_sum(): lax.all_to_all(x.reshape(size, -1, x.shape[-1]), axes, 0, 0, tiled=False)  49.7 us
    all_to_all x2, waiting for transfers between devices, exchange_gather(): lax.all_to_all(copies, axes, 0, 0, tiled=False).reshape(-1, x.shape[-1])  19.2 us
    all_to_all x1, blocking collectives, exchange_gather(): lax.all_to_all(copies, axes, 0, 0, tiled=False).reshape(-1, x.shape[-1])  17.2 us
    pallas_call x1, Pallas kernels, chol_solve(): pl.pallas_call(chol_solve_kernel, out_shape=(jax.ShapeDtypeStruct((n, n),...  16.1 us
    all_to_all x2, starting transfers between devices, exchange_gather(): lax.all_to_all(copies, axes, 0, 0, tiled=False).reshape(-1, x.shape[-1])  11 us
    ppermute x2, starting transfers between devices, pair_scatter_sum(): lax.ppermute(send, 'core', [(0, 1), (1, 0)])  5.26 us
    ppermute x2, starting transfers between devices, pair_gather(): other = lax.ppermute(x, 'core', [(0, 1), (1, 0)])  4.28 us
  transfers between devices with their start and end apart: 6, of which 6 were waited for; matrix products, arithmetic and copies ran while one was open for 0% of the time, Pallas kernels for 0%

profile of v13, /device:TPU:1, one launch (start us, length us, event | category | flops | bytes accessed | tf_op | source)
XLA Modules:
  0.0 137.7 jit_solution(18143054204531944291)
XLA Ops:
  0.7 1.6 %broadcast_in_dim.39 = f32[16,32,256]{2,1,0:T(8,128)} broadcast(f32[32,256]{1,0:T(8,128)} %param.5), dimensions={1,2} | broadcast | bytes 557056 | tf_op jit(solution)/shard_map/broadcast_in_dim | solution.py:113
  2.3 7.6 %all-to-all-start = ((f32[16,32,256]{2,1,0:T(8,128)}), f32[16,32,256]{2,1,0:T(8,128)S(1)}, u32[]{:S(2)}, u32[]{:S(2)}) async-start(f32[16,32,256]{2,1,0:T(8,128)} %broadcast_in_dim.39), calls=%async_computation | async-start | bytes 1048576 | tf_op jit(solution)/shard_map/all_to_all | solution.py:114
  10.6 9.9 %all-to-all-done = f32[16,32,256]{2,1,0:T(8,128)S(1)} async-done(((f32[16,32,256]{2,1,0:T(8,128)}), f32[16,32,256]{2,1,0:T(8,128)S(1)}, u32[]{:S(2)}, u32[]{:S(2)}) %all-to-all-start) | async-done | bytes 524320 | tf_op jit(solution)/shard_map/all_to_all | solution.py:114
  20.4 2.0 %collective-permute-start = (f32[512,256]{1,0:T(8,128)S(1)}, f32[512,256]{1,0:T(8,128)S(1)}, u32[]{:S(2)}, u32[]{:S(2)}) collective-permute-start(f32[512,256]{1,0:T(8,128)S(1)} %bitcast.65), channel_id=1, source_target_pairs={{0,8},{8,0},{1,9},{9,1},{2,10},{10,2},{3,11},{11,3},{4,12},{12,4},... | collective-permute-start | bytes 1572872 | tf_op jit(solution)/shard_map/ppermute | solution.py:118
  22.4 1.5 %collective-permute-done = f32[512,256]{1,0:T(8,128)S(1)} collective-permute-done((f32[512,256]{1,0:T(8,128)S(1)}, f32[512,256]{1,0:T(8,128)S(1)}, u32[]{:S(2)}, u32[]{:S(2)}) %collective-permute-start) | collective-permute-done | bytes 524320 | tf_op jit(solution)/shard_map/ppermute | solution.py:118
  23.9 0.2 fusion.4
  24.3 0.6 gather_fusion
  24.9 1.0 fusion
  25.9 0.1 copy.24
  26.0 19.0 %all_to_all.30 = f32[8,32,256]{2,1,0:T(8,128)S(1)} all-to-all(f32[8,32,256]{2,1,0:T(8,128)S(1)} %bitcast.68), channel_id=1, replica_groups=mesh['chip'=16,'core'=2,'col'=8] {'col'}, dimensions={0} | all-to-all | bytes 524288 | tf_op jit(solution)/shard_map/all_to_all | solution.py:107
  45.1 0.7 broadcast_in_dim.41
  45.8 3.4 %all-to-all-start.2 = ((f32[8,32,256]{2,1,0:T(8,128)}), f32[8,32,256]{2,1,0:T(8,128)S(1)}, u32[]{:S(2)}, u32[]{:S(2)}) async-start(f32[8,32,256]{2,1,0:T(8,128)} %broadcast_in_dim.41), calls=%async_computation.2 | async-start | bytes 524288 | tf_op jit(solution)/shard_map/all_to_all | solution.py:114
  49.3 9.4 %all-to-all-done.2 = f32[8,32,256]{2,1,0:T(8,128)S(1)} async-done(((f32[8,32,256]{2,1,0:T(8,128)}), f32[8,32,256]{2,1,0:T(8,128)S(1)}, u32[]{:S(2)}, u32[]{:S(2)}) %all-to-all-start.2) | async-done | bytes 262176 | tf_op jit(solution)/shard_map/all_to_all | solution.py:114
  58.8 0.6 convolution_bitcast_fusion
  59.4 0.2 copy.26
  59.6 0.2 select_reduce_fusion
  59.9 3.4 %collective-permute-start.1 = (f32[16,32,256]{2,1,0:T(8,128)S(1)}, f32[16,32,256]{2,1,0:T(8,128)S(1)}, u32[]{:S(2)}, u32[]{:S(2)}) collective-permute-start(f32[16,32,256]{2,1,0:T(8,128)S(1)} %dynamic-slice_bitcast_fusion), channel_id=1, source_target_pairs={{0,8},{8,0},{1,9},{9,1},{2,10},{10,2},{3,11},{11,3},{4,12},{12,4},... | collective-permute-start | bytes 1572872 | tf_op jit(solution)/shard_map/ppermute | solution.py:132
  63.3 1.5 %collective-permute-done.1 = f32[16,32,256]{2,1,0:T(8,128)S(1)} collective-permute-done((f32[16,32,256]{2,1,0:T(8,128)S(1)}, f32[16,32,256]{2,1,0:T(8,128)S(1)}, u32[]{:S(2)}, u32[]{:S(2)}) %collective-permute-start.1) | collective-permute-done | bytes 524320 | tf_op jit(solution)/shard_map/ppermute | solution.py:132
  64.9 13.4 %all_to_all.31 = f32[16,32,256]{2,1,0:T(8,128)S(1)} all-to-all(f32[16,32,256]{2,1,0:T(8,128)S(1)} %bitcast_add_fusion), channel_id=1, replica_groups=mesh['chip'=16,'core'=2,'col'=8] {'chip'}, dimensions={0} | all-to-all | bytes 1048576 | tf_op jit(solution)/shard_map/all_to_all | solution.py:107
  78.5 0.3 fusion.12
  78.8 1.9 %collective-permute-start.2 = (f32[16,8,256]{2,1,0:T(8,128)S(1)}, f32[16,8,256]{2,1,0:T(8,128)S(1)}, u32[]{:S(2)}, u32[]{:S(2)}) collective-permute-start(f32[16,8,256]{2,1,0:T(8,128)S(1)} %dynamic-slice_bitcast_fusion.1), channel_id=1, source_target_pairs={{0,8},{8,0},{1,9},{9,1},{2,10},{10,2},{3,11},{11,3},{4,12},{12,4},... | collective-permute-start | bytes 393224 | tf_op jit(solution)/shard_map/ppermute | solution.py:132
  80.7 1.0 collective-permute-done.2
  81.7 0.1 reshape_reshape.19
  81.9 17.3 %all_to_all.32 = f32[128,1,256]{2,1,0:T(1,128)S(1)} all-to-all(f32[128,1,256]{2,1,0:T(1,128)S(1)} %reshape_reshape.19), channel_id=1, replica_groups=mesh['chip'=16,'core'=2,'col'=8] {'chip','col'}, dimensions={0} | all-to-all | bytes 262144 | tf_op jit(solution)/shard_map/all_to_all | solution.py:107
  99.2 0.2 reduce_sum.52
  99.4 17.2 %all_to_all.33 = f32[128,1,256]{2,1,0:T(1,128)S(1)} all-to-all(f32[128,1,256]{2,1,0:T(1,128)S(1)} %broadcast_in_dim.66), channel_id=1, replica_groups=mesh['chip'=16,'core'=2,'col'=8] {'chip','col'}, dimensions={0} | all-to-all | bytes 262144 | tf_op jit(solution)/shard_map/all_to_all | solution.py:114
  116.7 2.3 %collective-permute-start.3 = (f32[128,256]{1,0:T(8,128)S(1)}, f32[128,256]{1,0:T(8,128)S(1)}, u32[]{:S(2)}, u32[]{:S(2)}) collective-permute-start(f32[128,256]{1,0:T(8,128)S(1)} %bitcast.71), channel_id=1, source_target_pairs={{0,8},{8,0},{1,9},{9,1},{2,10},{10,2},{3,11},{11,3},{4,12},{12,4},... | collective-permute-start | bytes 393224 | tf_op jit(solution)/shard_map/ppermute | solution.py:118
  119.0 1.0 collective-permute-done.3
  120.0 0.1 copy.28
  120.2 0.7 bitcast_select_fusion.g_ref
  120.9 16.1 %shard_map.76 = (f32[256,256]{1,0:T(8,128)}, f32[32,256]{1,0:T(8,128)}) custom-call(f32[256,256]{1,0:T(8,128)} %bitcast_select_fusion.g_ref, f32[32,256]{1,0:T(8,128)} %copy-done.1), custom_call_target="tpu_custom_call" | custom-call | tf_op jit(solution)/shard_map/pallas_call | solution.py:89
  137.0 0.7 copy.38
  (25 shorter events, 0.8 us)
Async XLA Ops:
  0.6 24.2 %copy-start = (f32[1,1,2,256,256]{4,3,2,1,0:T(8,128)S(1)}, f32[1,1,2,256,256]{4,3,2,1,0:T(8,128)}, u32[]{:S(2)}) copy-start(f32[1,1,2,256,256]{4,3,2,1,0:T(8,128)} %param.6) | copy-start | bytes 1572868
  0.6 21.7 %copy-start.3 = (s32[1,1,2]{2,1,0:T(1,128)S(1)}, s32[1,1,2]{2,1,0:T(1,128)}, u32[]{:S(2)}) copy-start(s32[1,1,2]{2,1,0:T(1,128)} %param.8) | copy-start | bytes 28
  0.7 21.8 %copy-start.2 = (s32[1,1,2]{2,1,0:T(1,128)S(1)}, s32[1,1,2]{2,1,0:T(1,128)}, u32[]{:S(2)}) copy-start(s32[1,1,2]{2,1,0:T(1,128)} %param.7) | copy-start | bytes 28
  2.3 18.1 %all-to-all-start = ((f32[16,32,256]{2,1,0:T(8,128)}), f32[16,32,256]{2,1,0:T(8,128)S(1)}, u32[]{:S(2)}, u32[]{:S(2)}) async-start(f32[16,32,256]{2,1,0:T(8,128)} %broadcast_in_dim.39), calls=%async_computation | async-start | bytes 1048576 | tf_op jit(solution)/shard_map/all_to_all | solution.py:114
  20.4 3.5 %collective-permute-start = (f32[512,256]{1,0:T(8,128)S(1)}, f32[512,256]{1,0:T(8,128)S(1)}, u32[]{:S(2)}, u32[]{:S(2)}) collective-permute-start(f32[512,256]{1,0:T(8,128)S(1)} %bitcast.65), channel_id=1, source_target_pairs={{0,8},{8,0},{1,9},{9,1},{2,10},{10,2},{3,11},{11,3},{4,12},{12,4},... | collective-permute-start | bytes 1572872 | tf_op jit(solution)/shard_map/ppermute | solution.py:118
  45.8 12.9 %all-to-all-start.2 = ((f32[8,32,256]{2,1,0:T(8,128)}), f32[8,32,256]{2,1,0:T(8,128)S(1)}, u32[]{:S(2)}, u32[]{:S(2)}) async-start(f32[8,32,256]{2,1,0:T(8,128)} %broadcast_in_dim.41), calls=%async_computation.2 | async-start | bytes 524288 | tf_op jit(solution)/shard_map/all_to_all | solution.py:114
  59.9 4.9 %collective-permute-start.1 = (f32[16,32,256]{2,1,0:T(8,128)S(1)}, f32[16,32,256]{2,1,0:T(8,128)S(1)}, u32[]{:S(2)}, u32[]{:S(2)}) collective-permute-start(f32[16,32,256]{2,1,0:T(8,128)S(1)} %dynamic-slice_bitcast_fusion), channel_id=1, source_target_pairs={{0,8},{8,0},{1,9},{9,1},{2,10},{10,2},{3,11},{11,3},{4,12},{12,4},... | collective-permute-start | bytes 1572872 | tf_op jit(solution)/shard_map/ppermute | solution.py:132
  78.4 38.3 %copy-start.1 = (f32[32,256]{1,0:T(8,128)}, f32[32,256]{1,0:T(8,128)S(1)}, u32[]{:S(2)}) copy-start(f32[32,256]{1,0:T(8,128)S(1)} %reduce_sum.51.p_ref) | copy-start | bytes 98308
  78.8 2.8 %collective-permute-start.2 = (f32[16,8,256]{2,1,0:T(8,128)S(1)}, f32[16,8,256]{2,1,0:T(8,128)S(1)}, u32[]{:S(2)}, u32[]{:S(2)}) collective-permute-start(f32[16,8,256]{2,1,0:T(8,128)S(1)} %dynamic-slice_bitcast_fusion.1), channel_id=1, source_target_pairs={{0,8},{8,0},{1,9},{9,1},{2,10},{10,2},{3,11},{11,3},{4,12},{12,4},... | collective-permute-start | bytes 393224 | tf_op jit(solution)/shard_map/ppermute | solution.py:132
  116.7 3.3 %collective-permute-start.3 = (f32[128,256]{1,0:T(8,128)S(1)}, f32[128,256]{1,0:T(8,128)S(1)}, u32[]{:S(2)}, u32[]{:S(2)}) collective-permute-start(f32[128,256]{1,0:T(8,128)S(1)} %bitcast.71), channel_id=1, source_target_pairs={{0,8},{8,0},{1,9},{9,1},{2,10},{10,2},{3,11},{11,3},{4,12},{12,4},... | collective-permute-start | bytes 393224 | tf_op jit(solution)/shard_map/ppermute | solution.py:118

commit v14 on v13

--- a/solution.py
+++ b/solution.py
@@ -21,7 +21,6 @@
     m = p_ref.shape[0]
     width = BLOCK
     a_ref[...] = g_ref[...]
-    u_ref[...] = jnp.zeros_like(u_ref)
     x_ref[...] = p_ref[...]
     full = lax.broadcasted_iota(jnp.int32, (1, n), 1)
     xwin = lax.broadcasted_iota(jnp.int32, (m, 128), 1)

time: 138 us -> 138 us (level)
  no operation moved by 1% of the time
where the time goes in v14:
time: 138 us
  blocking collectives  67 us (49%)
  waiting for transfers between devices  24.2 us (18%)
  starting transfers between devices  20.5 us (15%)
  Pallas kernels  16 us (12%)
  local copies, waits for them, and re-layouts  4.63 us (3%)
  matrix products  1.98 us (1%)
  other arithmetic  1.77 us (1%)
  between operations  1.5 us (1%)
    all_to_all x3, blocking collectives, exchange_sum(): lax.all_to_all(x.reshape(size, -1, x.shape[-1]), axes, 0, 0, tiled=False)  49.7 us
    all_to_all x2, waiting for transfers between devices, exchange_gather(): lax.all_to_all(copies, axes, 0, 0, tiled=False).reshape(-1, x.shape[-1])  19.2 us
    all_to_all x1, blocking collectives, exchange_gather(): lax.all_to_all(copies, axes, 0, 0, tiled=False).reshape(-1, x.shape[-1])  17.2 us
    pallas_call x1, Pallas kernels, chol_solve(): pl.pallas_call(chol_solve_kernel, out_shape=(jax.ShapeDtypeStruct((n, n),...  16 us
    all_to_all x2, starting transfers between devices, exchange_gather(): lax.all_to_all(copies, axes, 0, 0, tiled=False).reshape(-1, x.shape[-1])  11 us
    ppermute x2, starting transfers between devices, pair_scatter_sum(): lax.ppermute(send, 'core', [(0, 1), (1, 0)])  5.26 us
    ppermute x2, starting transfers between devices, pair_gather(): other = lax.ppermute(x, 'core', [(0, 1), (1, 0)])  4.28 us
  transfers between devices with their start and end apart: 6, of which 6 were waited for; matrix products, arithmetic and copies ran while one was open for 0% of the time, Pallas kernels for 0%

profile of v14, /device:TPU:1, one launch (start us, length us, event | category | flops | bytes accessed | tf_op | source)
XLA Modules:
  0.0 137.7 jit_solution(13549845308512476352)
XLA Ops:
  0.7 1.6 %broadcast_in_dim.39 = f32[16,32,256]{2,1,0:T(8,128)} broadcast(f32[32,256]{1,0:T(8,128)} %param.5), dimensions={1,2} | broadcast | bytes 557056 | tf_op jit(solution)/shard_map/broadcast_in_dim | solution.py:112
  2.3 7.6 %all-to-all-start = ((f32[16,32,256]{2,1,0:T(8,128)}), f32[16,32,256]{2,1,0:T(8,128)S(1)}, u32[]{:S(2)}, u32[]{:S(2)}) async-start(f32[16,32,256]{2,1,0:T(8,128)} %broadcast_in_dim.39), calls=%async_computation | async-start | bytes 1048576 | tf_op jit(solution)/shard_map/all_to_all | solution.py:113
  10.6 9.9 %all-to-all-done = f32[16,32,256]{2,1,0:T(8,128)S(1)} async-done(((f32[16,32,256]{2,1,0:T(8,128)}), f32[16,32,256]{2,1,0:T(8,128)S(1)}, u32[]{:S(2)}, u32[]{:S(2)}) %all-to-all-start) | async-done | bytes 524320 | tf_op jit(solution)/shard_map/all_to_all | solution.py:113
  20.4 2.0 %collective-permute-start = (f32[512,256]{1,0:T(8,128)S(1)}, f32[512,256]{1,0:T(8,128)S(1)}, u32[]{:S(2)}, u32[]{:S(2)}) collective-permute-start(f32[512,256]{1,0:T(8,128)S(1)} %bitcast.65), channel_id=1, source_target_pairs={{0,8},{8,0},{1,9},{9,1},{2,10},{10,2},{3,11},{11,3},{4,12},{12,4},... | collective-permute-start | bytes 1572872 | tf_op jit(solution)/shard_map/ppermute | solution.py:117
  22.4 1.5 %collective-permute-done = f32[512,256]{1,0:T(8,128)S(1)} collective-permute-done((f32[512,256]{1,0:T(8,128)S(1)}, f32[512,256]{1,0:T(8,128)S(1)}, u32[]{:S(2)}, u32[]{:S(2)}) %collective-permute-start) | collective-permute-done | bytes 524320 | tf_op jit(solution)/shard_map/ppermute | solution.py:117
  23.9 0.2 fusion.4
  24.3 0.6 gather_fusion
  24.9 1.0 fusion
  25.9 0.1 copy.24
  26.0 19.0 %all_to_all.30 = f32[8,32,256]{2,1,0:T(8,128)S(1)} all-to-all(f32[8,32,256]{2,1,0:T(8,128)S(1)} %bitcast.68), channel_id=1, replica_groups=mesh['chip'=16,'core'=2,'col'=8] {'col'}, dimensions={0} | all-to-all | bytes 524288 | tf_op jit(solution)/shard_map/all_to_all | solution.py:106
  45.1 0.7 broadcast_in_dim.41
  45.8 3.4 %all-to-all-start.2 = ((f32[8,32,256]{2,1,0:T(8,128)}), f32[8,32,256]{2,1,0:T(8,128)S(1)}, u32[]{:S(2)}, u32[]{:S(2)}) async-start(f32[8,32,256]{2,1,0:T(8,128)} %broadcast_in_dim.41), calls=%async_computation.2 | async-start | bytes 524288 | tf_op jit(solution)/shard_map/all_to_all | solution.py:113
  49.3 9.4 %all-to-all-done.2 = f32[8,32,256]{2,1,0:T(8,128)S(1)} async-done(((f32[8,32,256]{2,1,0:T(8,128)}), f32[8,32,256]{2,1,0:T(8,128)S(1)}, u32[]{:S(2)}, u32[]{:S(2)}) %all-to-all-start.2) | async-done | bytes 262176 | tf_op jit(solution)/shard_map/all_to_all | solution.py:113
  58.8 0.6 convolution_bitcast_fusion
  59.4 0.2 copy.26
  59.6 0.2 select_reduce_fusion
  59.9 3.4 %collective-permute-start.1 = (f32[16,32,256]{2,1,0:T(8,128)S(1)}, f32[16,32,256]{2,1,0:T(8,128)S(1)}, u32[]{:S(2)}, u32[]{:S(2)}) collective-permute-start(f32[16,32,256]{2,1,0:T(8,128)S(1)} %dynamic-slice_bitcast_fusion), channel_id=1, source_target_pairs={{0,8},{8,0},{1,9},{9,1},{2,10},{10,2},{3,11},{11,3},{4,12},{12,4},... | collective-permute-start | bytes 1572872 | tf_op jit(solution)/shard_map/ppermute | solution.py:131
  63.3 1.5 %collective-permute-done.1 = f32[16,32,256]{2,1,0:T(8,128)S(1)} collective-permute-done((f32[16,32,256]{2,1,0:T(8,128)S(1)}, f32[16,32,256]{2,1,0:T(8,128)S(1)}, u32[]{:S(2)}, u32[]{:S(2)}) %collective-permute-start.1) | collective-permute-done | bytes 524320 | tf_op jit(solution)/shard_map/ppermute | solution.py:131
  64.9 13.4 %all_to_all.31 = f32[16,32,256]{2,1,0:T(8,128)S(1)} all-to-all(f32[16,32,256]{2,1,0:T(8,128)S(1)} %bitcast_add_fusion), channel_id=1, replica_groups=mesh['chip'=16,'core'=2,'col'=8] {'chip'}, dimensions={0} | all-to-all | bytes 1048576 | tf_op jit(solution)/shard_map/all_to_all | solution.py:106
  78.5 0.3 fusion.12
  78.8 1.9 %collective-permute-start.2 = (f32[16,8,256]{2,1,0:T(8,128)S(1)}, f32[16,8,256]{2,1,0:T(8,128)S(1)}, u32[]{:S(2)}, u32[]{:S(2)}) collective-permute-start(f32[16,8,256]{2,1,0:T(8,128)S(1)} %dynamic-slice_bitcast_fusion.1), channel_id=1, source_target_pairs={{0,8},{8,0},{1,9},{9,1},{2,10},{10,2},{3,11},{11,3},{4,12},{12,4},... | collective-permute-start | bytes 393224 | tf_op jit(solution)/shard_map/ppermute | solution.py:131
  80.7 1.0 collective-permute-done.2
  81.7 0.1 reshape_reshape.19
  81.9 17.3 %all_to_all.32 = f32[128,1,256]{2,1,0:T(1,128)S(1)} all-to-all(f32[128,1,256]{2,1,0:T(1,128)S(1)} %reshape_reshape.19), channel_id=1, replica_groups=mesh['chip'=16,'core'=2,'col'=8] {'chip','col'}, dimensions={0} | all-to-all | bytes 262144 | tf_op jit(solution)/shard_map/all_to_all | solution.py:106
  99.2 0.2 reduce_sum.52
  99.4 17.2 %all_to_all.33 = f32[128,1,256]{2,1,0:T(1,128)S(1)} all-to-all(f32[128,1,256]{2,1,0:T(1,128)S(1)} %broadcast_in_dim.66), channel_id=1, replica_groups=mesh['chip'=16,'core'=2,'col'=8] {'chip','col'}, dimensions={0} | all-to-all | bytes 262144 | tf_op jit(solution)/shard_map/all_to_all | solution.py:113
  116.7 2.3 %collective-permute-start.3 = (f32[128,256]{1,0:T(8,128)S(1)}, f32[128,256]{1,0:T(8,128)S(1)}, u32[]{:S(2)}, u32[]{:S(2)}) collective-permute-start(f32[128,256]{1,0:T(8,128)S(1)} %bitcast.71), channel_id=1, source_target_pairs={{0,8},{8,0},{1,9},{9,1},{2,10},{10,2},{3,11},{11,3},{4,12},{12,4},... | collective-permute-start | bytes 393224 | tf_op jit(solution)/shard_map/ppermute | solution.py:117
  119.0 1.0 collective-permute-done.3
  120.0 0.1 copy.28
  120.2 0.7 bitcast_select_fusion.g_ref
  120.9 16.0 %shard_map.76 = (f32[256,256]{1,0:T(8,128)}, f32[32,256]{1,0:T(8,128)}) custom-call(f32[256,256]{1,0:T(8,128)} %bitcast_select_fusion.g_ref, f32[32,256]{1,0:T(8,128)} %copy-done.1), custom_call_target="tpu_custom_call" | custom-call | tf_op jit(solution)/shard_map/pallas_call | solution.py:88
  137.0 0.7 copy.38
  (25 shorter events, 0.8 us)
Async XLA Ops:
  0.6 24.2 %copy-start = (f32[1,1,2,256,256]{4,3,2,1,0:T(8,128)S(1)}, f32[1,1,2,256,256]{4,3,2,1,0:T(8,128)}, u32[]{:S(2)}) copy-start(f32[1,1,2,256,256]{4,3,2,1,0:T(8,128)} %param.6) | copy-start | bytes 1572868
  0.6 21.7 %copy-start.3 = (s32[1,1,2]{2,1,0:T(1,128)S(1)}, s32[1,1,2]{2,1,0:T(1,128)}, u32[]{:S(2)}) copy-start(s32[1,1,2]{2,1,0:T(1,128)} %param.8) | copy-start | bytes 28
  0.7 21.8 %copy-start.2 = (s32[1,1,2]{2,1,0:T(1,128)S(1)}, s32[1,1,2]{2,1,0:T(1,128)}, u32[]{:S(2)}) copy-start(s32[1,1,2]{2,1,0:T(1,128)} %param.7) | copy-start | bytes 28
  2.3 18.1 %all-to-all-start = ((f32[16,32,256]{2,1,0:T(8,128)}), f32[16,32,256]{2,1,0:T(8,128)S(1)}, u32[]{:S(2)}, u32[]{:S(2)}) async-start(f32[16,32,256]{2,1,0:T(8,128)} %broadcast_in_dim.39), calls=%async_computation | async-start | bytes 1048576 | tf_op jit(solution)/shard_map/all_to_all | solution.py:113
  20.4 3.5 %collective-permute-start = (f32[512,256]{1,0:T(8,128)S(1)}, f32[512,256]{1,0:T(8,128)S(1)}, u32[]{:S(2)}, u32[]{:S(2)}) collective-permute-start(f32[512,256]{1,0:T(8,128)S(1)} %bitcast.65), channel_id=1, source_target_pairs={{0,8},{8,0},{1,9},{9,1},{2,10},{10,2},{3,11},{11,3},{4,12},{12,4},... | collective-permute-start | bytes 1572872 | tf_op jit(solution)/shard_map/ppermute | solution.py:117
  45.8 12.9 %all-to-all-start.2 = ((f32[8,32,256]{2,1,0:T(8,128)}), f32[8,32,256]{2,1,0:T(8,128)S(1)}, u32[]{:S(2)}, u32[]{:S(2)}) async-start(f32[8,32,256]{2,1,0:T(8,128)} %broadcast_in_dim.41), calls=%async_computation.2 | async-start | bytes 524288 | tf_op jit(solution)/shard_map/all_to_all | solution.py:113
  59.9 4.9 %collective-permute-start.1 = (f32[16,32,256]{2,1,0:T(8,128)S(1)}, f32[16,32,256]{2,1,0:T(8,128)S(1)}, u32[]{:S(2)}, u32[]{:S(2)}) collective-permute-start(f32[16,32,256]{2,1,0:T(8,128)S(1)} %dynamic-slice_bitcast_fusion), channel_id=1, source_target_pairs={{0,8},{8,0},{1,9},{9,1},{2,10},{10,2},{3,11},{11,3},{4,12},{12,4},... | collective-permute-start | bytes 1572872 | tf_op jit(solution)/shard_map/ppermute | solution.py:131
  78.4 38.3 %copy-start.1 = (f32[32,256]{1,0:T(8,128)}, f32[32,256]{1,0:T(8,128)S(1)}, u32[]{:S(2)}) copy-start(f32[32,256]{1,0:T(8,128)S(1)} %reduce_sum.51.p_ref) | copy-start | bytes 98308
  78.8 2.8 %collective-permute-start.2 = (f32[16,8,256]{2,1,0:T(8,128)S(1)}, f32[16,8,256]{2,1,0:T(8,128)S(1)}, u32[]{:S(2)}, u32[]{:S(2)}) collective-permute-start(f32[16,8,256]{2,1,0:T(8,128)S(1)} %dynamic-slice_bitcast_fusion.1), channel_id=1, source_target_pairs={{0,8},{8,0},{1,9},{9,1},{2,10},{10,2},{3,11},{11,3},{4,12},{12,4},... | collective-permute-start | bytes 393224 | tf_op jit(solution)/shard_map/ppermute | solution.py:131
  116.7 3.3 %collective-permute-start.3 = (f32[128,256]{1,0:T(8,128)S(1)}, f32[128,256]{1,0:T(8,128)S(1)}, u32[]{:S(2)}, u32[]{:S(2)}) collective-permute-start(f32[128,256]{1,0:T(8,128)S(1)} %bitcast.71), channel_id=1, source_target_pairs={{0,8},{8,0},{1,9},{9,1},{2,10},{10,2},{3,11},{11,3},{4,12},{12,4},... | collective-permute-start | bytes 393224 | tf_op jit(solution)/shard_map/ppermute | solution.py:117
